TPU v7x, 32 devices: a whole 2x2x4 slice. The times are simulated.
32 devices in a mesh: row: 4 (over x, core), col: 8 (over z, y).
Axes of the slice: x: 2, y: 2, z: 4, core: 2. Of those that a mesh axis runs over, the one named last changes fastest.
Arguments:
- amplitudes: float32 [8, 64, 512, 512], P(None, None, None, ('row', 'col')), may hold values from -6 to 6
- cycle_integrals: float32 [64, 512, 4, 512], P('col'), may hold values from -0.125 to 0.125
- occ_irrep: int32 [64], replicated, may hold values from 0 to 7
- virt_irrep: int32 [512], replicated, may hold values from 0 to 7
Outputs:
- cycle: float32 [8, 512, 2048], P(None, 'row', 'col')
All inputs are finite; a program needn't handle non-finite values.
Results may differ from a plain program's by a relative error of at most 0.0003.
Values sent between devices are 32-bit elements; how exact they have to be, the bound alone decides.
No kernel may reach another device: no remote copies, remote signals or barrier semaphores. Data moves between devices by JAX's collectives and lax.ppermute only.
A program may use at most 256 MiB of HBM per device.

v0:
```python
import jax
import jax.numpy as jnp
from jax import lax
from jax.sharding import PartitionSpec as P


def per_device(amplitudes, cycle_integrals, occ_irrep, virt_irrep):
    slab_rows, occ_count, virt_count, c_local = amplitudes.shape
    col_count = lax.axis_size("col")
    row_count = lax.axis_size("row")
    k_local = occ_count // col_count
    a_local = virt_count // row_count
    column_slab = cycle_integrals.shape[2]
    col_place = lax.axis_index("col")
    row_place = lax.axis_index("row")
    k_irrep = lax.dynamic_slice_in_dim(occ_irrep, col_place * k_local, k_local)
    c_irrep = lax.dynamic_slice_in_dim(
        virt_irrep, (row_place * col_count + col_place) * c_local, c_local
    )
    slab_irrep = occ_irrep[:slab_rows]
    column_irrep = occ_irrep[:column_slab]
    amp_sym = (
        slab_irrep[:, None, None, None]
        ^ occ_irrep[None, :, None, None]
        ^ (virt_irrep[None, None, :, None] ^ c_irrep[None, None, None, :])
    )
    masked_amps = jnp.where(amp_sym == 0, amplitudes, 0.0)
    int_sym = (
        k_irrep[:, None, None, None]
        ^ virt_irrep[None, :, None, None]
        ^ (column_irrep[None, None, :, None] ^ virt_irrep[None, None, None, :])
    )
    masked_ints = jnp.where(int_sym == 0, cycle_integrals, 0.0)
    grouped = masked_amps.reshape(slab_rows, col_count, k_local, row_count, a_local, c_local)
    grouped = jnp.transpose(grouped, (0, 3, 1, 2, 4, 5)).reshape(
        slab_rows, row_count * col_count, k_local, a_local, c_local
    )
    items = lax.all_to_all(grouped, ("row", "col"), split_axis=1, concat_axis=4, tiled=True)
    count = items.shape[0]
    blocks = items.reshape(count, k_local, a_local, virt_count)
    partial_value = jnp.einsum(
        "ikac,kcjb->iajb",
        blocks,
        masked_ints,
        precision=lax.Precision.HIGHEST,
        preferred_element_type=jnp.float32,
    )
    flat = partial_value.reshape(count, a_local, column_slab * virt_count)
    return lax.psum_scatter(flat, "col", scatter_dimension=2, tiled=True)


def solution(mesh):
    placed = (P(None, None, None, ("row", "col")), P("col", None, None, None), P(), P())
    return jax.shard_map(
        per_device, mesh=mesh, in_specs=placed, out_specs=P(None, "row", "col"), check_vma=False
    )
```

profile of v0, /device:TPU:0, one launch (start us, length us, event | category | flops | bytes accessed | tf_op | source)
XLA Modules:
  0.0 813.8 jit_solution(898013345767864175)
XLA Ops:
  6.5 0.8 fusion.1
  7.3 0.7 broadcast_xor_fusion.3
  8.1 0.8 dynamic_slice.6
  8.8 0.8 broadcast_xor_fusion
  9.6 11.7 %fusion = f32[8,64,512,16]{2,3,1,0:T(8,128)} fusion(f32[8,64,512,16]{2,3,1,0:T(8,128)} %param.4, s32[512,16]{0,1:T(8,128)S(1)} %broadcast_xor_fusion, s32[8,64]{1,0:T(8,128)S(1)} %broadcast_xor_fusion.3), kind=kLoop, calls=%fused_computation.3 | loop fusion | flops 12582912 | bytes 33589248 | tf_op jit(solution)/shard_map/jit(_where)/select_n | solution.py:27
  21.2 19.2 %reshape.140 = f32[8,8,8,4,128,16]{4,3,5,2,1,0:T(4,128)} reshape(f32[8,64,512,16]{2,3,1,0:T(8,128)} %fusion) | data formatting | bytes 33554432 | tf_op jit(solution)/shard_map/reshape | solution.py:34
  40.4 12.7 %copy.10 = f32[8,8,8,4,128,16]{4,5,2,0,1,3:T(8,128)} copy(f32[8,8,8,4,128,16]{4,3,5,2,1,0:T(4,128)} %reshape.140) | data formatting | bytes 33554432 | tf_op jit(solution)/shard_map/reshape | solution.py:34
  53.1 0.0 copy-start
  53.1 0.0 copy-start.1
  53.1 7.4 all-to-all-start
  60.5 0.0 reduce-scatter.2.cloned.1.call-start
  60.6 0.0 copy-done
  60.6 0.0 copy-done.1
  60.6 0.1 broadcast_xor_fusion.2
  60.7 0.1 broadcast_xor_fusion.1
  60.7 23.1 %select_bitcast_fusion = f32[4,512,512,8]{1,0,2,3:T(4,128)} fusion(f32[8,512,4,512]{3,2,1,0:T(4,128)} %param.5, s32[4,512]{1,0:T(4,128)S(1)} %broadcast_xor_fusion.2, s32[8,512]{1,0:T(8,128)S(1)} %broadcast_xor_fusion.1), kind=kLoop, calls=%fused_computation | loop fusion | flops 25165824 | bytes 67133440 | tf_op jit(solution)/shard_map/ikac,kcjb->iajb/dot_general | solution.py:41
  83.8 37.9 %copy.17 = f32[4,512,512,8]{2,1,0,3:T(8,128)} copy(f32[4,512,512,8]{1,0,2,3:T(4,128)} %select_bitcast_fusion) | data formatting | bytes 67108864 | tf_op jit(solution)/shard_map/ikac,kcjb->iajb/dot_general | solution.py:41
  121.7 313.9 %all-to-all-done = f32[8,32,8,128,16]{3,4,2,0,1:T(8,128)} async-done(((f32[8,32,8,128,16]{3,4,2,0,1:T(8,128)}), f32[8,32,8,128,16]{3,4,2,0,1:T(8,128)}, u32[]{:S(2)}, u32[]{:S(2)}) %all-to-all-start) | async-done | bytes 16777248 | tf_op jit(solution)/shard_map/all_to_all | solution.py:38
  435.6 6.7 copy.11
  442.3 218.8 %convolution_bitcast_fusion = f32[8,128,2048]{2,1,0:T(8,128)} fusion(f32[8,8,128,512]{2,3,1,0:T(8,128)S(1)} %bitcast.25, f32[2048,512,8,1]{1,0,2,3:T(8,128)} %bitcast.24), kind=kOutput, calls=%fused_computation.4 | convolution fusion | flops 103079215104 | bytes 58720256 | tf_op jit(solution)/shard_map/ikac,kcjb->iajb/dot_general | solution.py:41
  661.1 0.0 reduce-scatter.2.cloned.1.call-update
  661.2 145.8 %reduce-scatter.2.cloned.1.call-done = f32[8,128,256]{2,1,0:T(8,128)} async-done(((f32[8,128,2048]{2,1,0:T(8,128)}), f32[8,128,256]{2,1,0:T(8,128)}) %reduce-scatter.2.cloned.1.call-update) | async-done | bytes 1048592 | tf_op jit(solution)/shard_map/reduce_scatter | solution.py:49
Async XLA Ops:
  53.1 7.5 copy-start
  53.1 7.5 copy-start.1
  53.1 382.5 %all-to-all-start = ((f32[8,32,8,128,16]{3,4,2,0,1:T(8,128)}), f32[8,32,8,128,16]{3,4,2,0,1:T(8,128)}, u32[]{:S(2)}, u32[]{:S(2)}) async-start(f32[8,32,8,128,16]{3,4,2,0,1:T(8,128)} %bitcast.23), calls=%async_computation | async-start | bytes 33554432 | tf_op jit(solution)/shard_map/all_to_all | solution.py:38
  60.5 746.5 %reduce-scatter.2.cloned.1.call-start = ((), (), s32[]{:S(2)}) async-start(), calls=%async_computation.2 | async-start | bytes 9437184 | tf_op jit(solution)/shard_map/reduce_scatter | solution.py:49
Sparse Core Ops, SparseCore 0:
  661.3 145.6 reduce-scatter.1
where the time goes:
time: 816 us; the launch traced here: 814 us
  waiting for transfers between devices  460 us (56%)
  matrix products  219 us (27%)
  local copies, waits for them, and re-layouts  78 us (10%)
  other arithmetic  36.3 us (4%)
  between operations  13.4 us (2%)
    all_to_all x1, waiting for transfers between devices, per_device(): lax.all_to_all(grouped, ('row', 'col'), split_axis=1, concat_axis=4, tile...  314 us
    dot_general x1, matrix products, per_device(): jnp.einsum('ikac,kcjb->iajb', blocks, masked_ints, precision=lax.Precisio...  219 us
    reduce_scatter x1, waiting for transfers between devices, per_device(): return lax.psum_scatter(flat, 'col', scatter_dimension=2, tiled=True)  146 us
    dot_general x1, local copies, waits for them, and re-layouts, per_device(): jnp.einsum('ikac,kcjb->iajb', blocks, masked_ints, precision=lax.Precisio...  37.9 us
    reshape x2, local copies, waits for them, and re-layouts, per_device(): masked_amps.reshape(slab_rows, col_count, k_local, row_count, a_local, c_...  31.9 us
    dot_general x1, other arithmetic, per_device(): jnp.einsum('ikac,kcjb->iajb', blocks, masked_ints, precision=lax.Precisio...  23.1 us
  transfers between devices with their start and end apart: 2, of which 2 were waited for; matrix products, arithmetic and copies ran while one was open for 8% of the time, Pallas kernels for 0%

commit v1 on v0

v1 whole, which is shorter than its diff:
```python
import jax
import jax.numpy as jnp
from jax import lax
from jax.sharding import PartitionSpec as P


def per_device(amplitudes, cycle_integrals, occ_irrep, virt_irrep):
    slab_rows, occ_count, virt_count, c_local = amplitudes.shape
    col_count = lax.axis_size("col")
    row_count = lax.axis_size("row")
    k_local = occ_count // col_count
    a_local = virt_count // row_count
    column_slab = cycle_integrals.shape[2]
    col_place = lax.axis_index("col")
    row_place = lax.axis_index("row")
    k_irrep = lax.dynamic_slice_in_dim(occ_irrep, col_place * k_local, k_local)
    c_irrep = lax.dynamic_slice_in_dim(
        virt_irrep, (row_place * col_count + col_place) * c_local, c_local
    )
    slab_irrep = occ_irrep[:slab_rows]
    column_irrep = occ_irrep[:column_slab]
    int_sym = (
        k_irrep[:, None, None, None]
        ^ virt_irrep[None, :, None, None]
        ^ (column_irrep[None, None, :, None] ^ virt_irrep[None, None, None, :])
    )
    masked_ints = jnp.where(int_sym == 0, cycle_integrals, 0.0)

    chunks = 4 if slab_rows % 4 == 0 else 1
    rows = slab_rows // chunks
    results = []
    for step in range(chunks):
        amps = amplitudes[step * rows:(step + 1) * rows]
        amp_sym = (
            slab_irrep[step * rows:(step + 1) * rows, None, None, None]
            ^ occ_irrep[None, :, None, None]
            ^ (virt_irrep[None, None, :, None] ^ c_irrep[None, None, None, :])
        )
        masked_amps = jnp.where(amp_sym == 0, amps, 0.0)
        grouped = masked_amps.reshape(rows, col_count, k_local, row_count, a_local, c_local)
        grouped = jnp.transpose(grouped, (0, 3, 1, 2, 4, 5)).reshape(
            rows, row_count * col_count, k_local, a_local, c_local
        )
        items = lax.all_to_all(grouped, ("row", "col"), split_axis=1, concat_axis=4, tiled=True)
        blocks = items.reshape(rows, k_local, a_local, virt_count)
        partial_value = jnp.einsum(
            "ikac,kcjb->iajb",
            blocks,
            masked_ints,
            precision=lax.Precision.HIGH,
            preferred_element_type=jnp.float32,
        )
        flat = partial_value.reshape(rows, a_local, column_slab * virt_count)
        results.append(lax.psum_scatter(flat, "col", scatter_dimension=2, tiled=True))
    return jnp.concatenate(results, axis=0)


def solution(mesh):
    placed = (P(None, None, None, ("row", "col")), P("col", None, None, None), P(), P())
    return jax.shard_map(
        per_device, mesh=mesh, in_specs=placed, out_specs=P(None, "row", "col"), check_vma=False
    )
```

time: 816 us -> 663 us (0.81)
  matrix products: 219 us -> 78.2 us
  waiting for transfers between devices: 460 us -> 410 us
  local copies, waits for them, and re-layouts: 78 us -> 100 us
  starting transfers between devices: 7.47 us -> 21.1 us
    dot_general x1 -> x4, matrix products: 219 us -> 78.2 us  [per_device(): jnp.einsum('ikac,kcjb->iajb', blocks, masked_ints, precision=lax.Precisio...]
    all_to_all x1 -> x4, waiting for transfers between devices: 314 us -> 245 us  [per_device(): lax.all_to_all(grouped, ('row', 'col'), split_axis=1, concat_axis=4, tile...]
    reduce_scatter x1 -> x4, waiting for transfers between devices: 146 us -> 165 us  [per_device(): lax.psum_scatter(flat, 'col', scatter_dimension=2, tiled=True)]
    all_to_all x1 -> x4, starting transfers between devices: 7.43 us -> 20.7 us  [per_device(): lax.all_to_all(grouped, ('row', 'col'), split_axis=1, concat_axis=4, tile...]
    all_to_all x1 -> x4, local copies, waits for them, and re-layouts: 6.75 us -> 18.7 us  [per_device(): lax.all_to_all(grouped, ('row', 'col'), split_axis=1, concat_axis=4, tile...]
    reshape x2 -> x8, local copies, waits for them, and re-layouts: 31.9 us -> 40 us  [per_device(): masked_amps.reshape(rows, col_count, k_local, row_count, a_local, c_local)]
  transfers between devices with their start and end apart: 2 -> 8, of which waited for: 2 -> 6; matrix products, arithmetic and copies ran while one was open for 8% -> 29% of each run, Pallas kernels for 0% -> 0%
where the time goes in v1:
time: 663 us; the launch traced here: 661 us
  waiting for transfers between devices  410 us (62%)
  local copies, waits for them, and re-layouts  100 us (15%)
  matrix products  78.2 us (12%)
  other arithmetic  38.3 us (6%)
  starting transfers between devices  21.1 us (3%)
  between operations  13.2 us (2%)
    all_to_all x4, waiting for transfers between devices, per_device(): lax.all_to_all(grouped, ('row', 'col'), split_axis=1, concat_axis=4, tile...  245 us
    reduce_scatter x4, waiting for transfers between devices, per_device(): lax.psum_scatter(flat, 'col', scatter_dimension=2, tiled=True)  165 us
    dot_general x4, matrix products, per_device(): jnp.einsum('ikac,kcjb->iajb', blocks, masked_ints, precision=lax.Precisio...  78.2 us
    reshape x8, local copies, waits for them, and re-layouts, per_device(): masked_amps.reshape(rows, col_count, k_local, row_count, a_local, c_local)  40 us
    dot_general x1, local copies, waits for them, and re-layouts, per_device(): jnp.einsum('ikac,kcjb->iajb', blocks, masked_ints, precision=lax.Precisio...  39.8 us
    dot_general x1, other arithmetic, per_device(): jnp.einsum('ikac,kcjb->iajb', blocks, masked_ints, precision=lax.Precisio...  23.1 us
    all_to_all x4, starting transfers between devices, per_device(): lax.all_to_all(grouped, ('row', 'col'), split_axis=1, concat_axis=4, tile...  20.7 us
    all_to_all x4, local copies, waits for them, and re-layouts, per_device(): lax.all_to_all(grouped, ('row', 'col'), split_axis=1, concat_axis=4, tile...  18.7 us
  transfers between devices with their start and end apart: 8, of which 6 were waited for; matrix products, arithmetic and copies ran while one was open for 29% of the time, Pallas kernels for 0%

profile of v1, /device:TPU:0, one launch (start us, length us, event | category | flops | bytes accessed | tf_op | source)
XLA Modules:
  0.0 660.6 jit_solution(17040442675466477142)
XLA Ops:
  9.6 11.3 %slice_select_fusion.3 = (f32[2,64,512,16]{2,3,1,0:T(8,128)}, f32[2,64,512,16]{2,3,1,0:T(8,128)}, f32[2,64,512,16]{2,3,1,0:T(8,128)}, f32[2,64,512,16]{2,3,1,0:T(8,128)}) fusion(f32[8,64,512,16]{2,3,1,0:T(8,128)} %param.4, s32[512,16]{0,1:T(8,128)S(1)} %broadcast_xor_fusion, s32[2,64]{1,0:T(2,128)S(1)} %get-tuple-element.9, ...), kind=kLoop, calls=%fused_computation.16 | loop fusion | flops 12582912 | bytes 33589248 | tf_op jit(solution)/shard_map/jit(_where)/select_n | solution.py:39
  21.0 5.3 reshape.260
  26.2 4.7 copy.25
  31.0 7.4 %all-to-all-start = ((f32[2,32,8,128,16]{3,4,2,0,1:T(8,128)}), f32[2,32,8,128,16]{3,4,2,0,1:T(8,128)}, u32[]{:S(2)}, u32[]{:S(2)}) async-start(f32[2,32,8,128,16]{3,4,2,0,1:T(8,128)} %bitcast.96), calls=%async_computation | async-start | bytes 8388608 | tf_op jit(solution)/shard_map/all_to_all | solution.py:44
  38.4 5.3 reshape.269
  48.4 86.0 %all-to-all-done = f32[2,32,8,128,16]{3,4,2,0,1:T(8,128)} async-done(((f32[2,32,8,128,16]{3,4,2,0,1:T(8,128)}), f32[2,32,8,128,16]{3,4,2,0,1:T(8,128)}, u32[]{:S(2)}, u32[]{:S(2)}) %all-to-all-start) | async-done | bytes 4194336 | tf_op jit(solution)/shard_map/all_to_all | solution.py:44
  138.2 5.3 reshape.266
  143.4 4.7 copy.33
  148.2 85.9 %all-to-all-done.3 = f32[2,32,8,128,16]{3,4,2,0,1:T(8,128)} async-done(((f32[2,32,8,128,16]{3,4,2,0,1:T(8,128)}), f32[2,32,8,128,16]{3,4,2,0,1:T(8,128)}, u32[]{:S(2)}, u32[]{:S(2)}) %all-to-all-start.3) | async-done | bytes 4194336 | tf_op jit(solution)/shard_map/all_to_all | solution.py:44
  238.0 23.1 %select_bitcast_fusion = f32[4,512,512,8]{1,0,2,3:T(4,128)} fusion(f32[8,512,4,512]{3,2,1,0:T(4,128)} %param.5, s32[4,512]{1,0:T(4,128)S(1)} %broadcast_xor_fusion.2, s32[8,512]{1,0:T(8,128)S(1)} %broadcast_xor_fusion.1), kind=kLoop, calls=%fused_computation.8 | loop fusion | flops 25165824 | bytes 67133440 | tf_op jit(solution)/shard_map/ikac,kcjb->iajb/dot_general | solution.py:46
  261.1 39.8 %dot_general.17 = f32[2048,512,8]{0,1,2:T(8,128)} reshape(f32[4,512,512,8]{1,0,2,3:T(4,128)} %select_bitcast_fusion) | data formatting | bytes 67108864 | tf_op jit(solution)/shard_map/ikac,kcjb->iajb/dot_general | solution.py:46
  300.8 4.7 copy.26
  305.6 19.4 %fusion.8 = f32[2,128,2048]{2,1,0:T(8,128)} fusion(f32[2,8,128,512]{2,3,1,0:T(8,128)} %bitcast.91, f32[2048,512,8]{0,1,2:T(8,128)} %dot_general.17), kind=kOutput, calls=%fused_computation.18 | convolution fusion | flops 12884901888 | bytes 39845888 | tf_op jit(solution)/shard_map/ikac,kcjb->iajb/dot_general | solution.py:46
  325.0 5.3 reshape.263
  330.3 4.8 copy.29
  339.7 5.9 all-to-all-start.1
  345.8 19.7 %fusion.17 = f32[2,128,2048]{2,1,0:T(8,128)} fusion(f32[2,8,128,512]{2,3,1,0:T(8,128)} %bitcast.89, f32[2048,512,8]{0,1,2:T(8,128)} %dot_general.17), kind=kOutput, calls=%fused_computation.21 | convolution fusion | flops 12884901888 | bytes 39845888 | tf_op jit(solution)/shard_map/ikac,kcjb->iajb/dot_general | solution.py:46
  370.2 19.5 %fusion.14 = f32[2,128,2048]{2,1,0:T(8,128)} fusion(f32[2,8,128,512]{2,3,1,0:T(8,128)} %bitcast.92, f32[2048,512,8]{0,1,2:T(8,128)} %dot_general.17), kind=kOutput, calls=%fused_computation.20 | convolution fusion | flops 12884901888 | bytes 39845888 | tf_op jit(solution)/shard_map/ikac,kcjb->iajb/dot_general | solution.py:46
  389.8 72.7 %all-to-all-done.1 = f32[2,32,8,128,16]{3,4,2,0,1:T(8,128)} async-done(((f32[2,32,8,128,16]{3,4,2,0,1:T(8,128)}), f32[2,32,8,128,16]{3,4,2,0,1:T(8,128)}, u32[]{:S(2)}, u32[]{:S(2)}) %all-to-all-start.1) | async-done | bytes 4194336 | tf_op jit(solution)/shard_map/all_to_all | solution.py:44
  462.4 4.8 copy.30
  467.3 19.6 %fusion.11 = f32[2,128,2048]{2,1,0:T(8,128)} fusion(f32[2,8,128,512]{2,3,1,0:T(8,128)} %bitcast.90, f32[2048,512,8]{0,1,2:T(8,128)} %dot_general.17), kind=kOutput, calls=%fused_computation.19 | convolution fusion | flops 12884901888 | bytes 39845888 | tf_op jit(solution)/shard_map/ikac,kcjb->iajb/dot_general | solution.py:46
  486.9 23.6 %reduce-scatter.11.cloned.1.call-done = f32[2,128,256]{2,1,0:T(8,128)} async-done(((f32[2,128,2048]{2,1,0:T(8,128)}), f32[2,128,256]{2,1,0:T(8,128)}) %reduce-scatter.11.cloned.1.call-update) | async-done | bytes 262160 | tf_op jit(solution)/shard_map/reduce_scatter | solution.py:54
  510.5 70.8 %reduce-scatter.9.cloned.1.call-done = f32[2,128,256]{2,1,0:T(8,128)} async-done(((f32[2,128,2048]{2,1,0:T(8,128)}), f32[2,128,256]{2,1,0:T(8,128)}) %reduce-scatter.9.cloned.1.call-update) | async-done | bytes 262160 | tf_op jit(solution)/shard_map/reduce_scatter | solution.py:54
  581.4 70.5 %reduce-scatter.7.cloned.1.call-done = f32[2,128,256]{2,1,0:T(8,128)} async-done(((f32[2,128,2048]{2,1,0:T(8,128)}), f32[2,128,256]{2,1,0:T(8,128)}) %reduce-scatter.7.cloned.1.call-update) | async-done | bytes 262160 | tf_op jit(solution)/shard_map/reduce_scatter | solution.py:54
  (27 shorter events, 27.3 us)
Async XLA Ops:
  31.0 103.4 %all-to-all-start = ((f32[2,32,8,128,16]{3,4,2,0,1:T(8,128)}), f32[2,32,8,128,16]{3,4,2,0,1:T(8,128)}, u32[]{:S(2)}, u32[]{:S(2)}) async-start(f32[2,32,8,128,16]{3,4,2,0,1:T(8,128)} %bitcast.96), calls=%async_computation | async-start | bytes 8388608 | tf_op jit(solution)/shard_map/all_to_all | solution.py:44
  134.4 3.7 copy-start.1
  134.4 99.7 %all-to-all-start.3 = ((f32[2,32,8,128,16]{3,4,2,0,1:T(8,128)}), f32[2,32,8,128,16]{3,4,2,0,1:T(8,128)}, u32[]{:S(2)}, u32[]{:S(2)}) async-start(f32[2,32,8,128,16]{3,4,2,0,1:T(8,128)} %bitcast.95), calls=%async_computation.6 | async-start | bytes 8388608 | tf_op jit(solution)/shard_map/all_to_all | solution.py:44
  234.1 3.8 copy-start
  234.1 105.6 %all-to-all-start.2 = ((f32[2,32,8,128,16]{3,4,2,0,1:T(8,128)}), f32[2,32,8,128,16]{3,4,2,0,1:T(8,128)}, u32[]{:S(2)}, u32[]{:S(2)}) async-start(f32[2,32,8,128,16]{3,4,2,0,1:T(8,128)} %bitcast.94), calls=%async_computation.4 | async-start | bytes 8388608 | tf_op jit(solution)/shard_map/all_to_all | solution.py:44
  237.8 249.1 %reduce-scatter.5.cloned.1.call-start = ((), (), s32[]{:S(2)}) async-start(), calls=%async_computation.8 | async-start | bytes 2359296 | tf_op jit(solution)/shard_map/reduce_scatter | solution.py:54
  339.7 122.8 %all-to-all-start.1 = ((f32[2,32,8,128,16]{3,4,2,0,1:T(8,128)}), f32[2,32,8,128,16]{3,4,2,0,1:T(8,128)}, u32[]{:S(2)}, u32[]{:S(2)}) async-start(f32[2,32,8,128,16]{3,4,2,0,1:T(8,128)} %bitcast.93), calls=%async_computation.2 | async-start | bytes 8388608 | tf_op jit(solution)/shard_map/all_to_all | solution.py:44
  345.6 164.9 %reduce-scatter.11.cloned.1.call-start = ((), (), s32[]{:S(2)}) async-start(), calls=%async_computation.11 | async-start | bytes 2359296 | tf_op jit(solution)/shard_map/reduce_scatter | solution.py:54
  365.6 215.8 %reduce-scatter.9.cloned.1.call-start = ((), (), s32[]{:S(2)}) async-start(), calls=%async_computation.10 | async-start | bytes 2359296 | tf_op jit(solution)/shard_map/reduce_scatter | solution.py:54
  389.7 262.1 %reduce-scatter.7.cloned.1.call-start = ((), (), s32[]{:S(2)}) async-start(), calls=%async_computation.9 | async-start | bytes 2359296 | tf_op jit(solution)/shard_map/reduce_scatter | solution.py:54
Sparse Core Ops, SparseCore 0:
  325.1 113.2 reduce-scatter.4
  442.0 68.5 reduce-scatter.10
  514.1 67.2 reduce-scatter.8
  584.7 67.0 reduce-scatter.6

commit v2 on v1

v2 whole, which is shorter than its diff:
```python
import jax
import jax.numpy as jnp
from jax import lax
from jax.sharding import PartitionSpec as P


def chunk_plan(slab_rows):
    if slab_rows >= 8:
        head = slab_rows - 2
        sizes = [2] * (head // 2) + [1] * (head % 2) + [1, 1]
        return sizes
    return [1] * slab_rows


def per_device(amplitudes, cycle_integrals, occ_irrep, virt_irrep):
    slab_rows, occ_count, virt_count, c_local = amplitudes.shape
    col_count = lax.axis_size("col")
    row_count = lax.axis_size("row")
    k_local = occ_count // col_count
    a_local = virt_count // row_count
    column_slab = cycle_integrals.shape[2]
    col_place = lax.axis_index("col")
    row_place = lax.axis_index("row")
    k_irrep = lax.dynamic_slice_in_dim(occ_irrep, col_place * k_local, k_local)
    a_irrep = lax.dynamic_slice_in_dim(virt_irrep, row_place * a_local, a_local)
    slab_irrep = occ_irrep[:slab_rows]
    column_irrep = occ_irrep[:column_slab]
    int_sym = (
        k_irrep[:, None, None, None]
        ^ virt_irrep[None, :, None, None]
        ^ (column_irrep[None, None, :, None] ^ virt_irrep[None, None, None, :])
    )
    masked_ints = jnp.where(int_sym == 0, cycle_integrals, 0.0)

    results = []
    start = 0
    for step, rows in enumerate(chunk_plan(slab_rows)):
        amps = amplitudes[start:start + rows]
        grouped = amps.reshape(rows, col_count, k_local, row_count, a_local, c_local)
        grouped = jnp.transpose(grouped, (0, 3, 1, 2, 4, 5)).reshape(
            rows, row_count * col_count, k_local, a_local, c_local
        )
        if step == 1:
            grouped, masked_ints = lax.optimization_barrier((grouped, masked_ints))
        if step >= 2:
            grouped, results[step - 2] = lax.optimization_barrier((grouped, results[step - 2]))
        items = lax.all_to_all(grouped, ("row", "col"), split_axis=1, concat_axis=4, tiled=True)
        blocks = items.reshape(rows, k_local, a_local, virt_count)
        amp_sym = (
            slab_irrep[start:start + rows, None, None, None]
            ^ k_irrep[None, :, None, None]
            ^ (a_irrep[None, None, :, None] ^ virt_irrep[None, None, None, :])
        )
        blocks = jnp.where(amp_sym == 0, blocks, 0.0)
        partial_value = jnp.einsum(
            "ikac,kcjb->iajb",
            blocks,
            masked_ints,
            precision=lax.Precision.HIGH,
            preferred_element_type=jnp.float32,
        )
        flat = partial_value.reshape(rows, a_local, column_slab * virt_count)
        results.append(lax.psum_scatter(flat, "col", scatter_dimension=2, tiled=True))
        start += rows
    return jnp.concatenate(results, axis=0)


def solution(mesh):
    placed = (P(None, None, None, ("row", "col")), P("col", None, None, None), P(), P())
    return jax.shard_map(
        per_device, mesh=mesh, in_specs=placed, out_specs=P(None, "row", "col"), check_vma=False
    )
```

time: 663 us -> 771 us (1.16)
  local copies, waits for them, and re-layouts: 100 us -> 160 us
  matrix products: 78.2 us -> 105 us
  other arithmetic: 38.3 us -> 55 us
    all_to_all x4 -> x5, waiting for transfers between devices: 245 us -> 146 us  [per_device(): lax.all_to_all(grouped, ('row', 'col'), split_axis=1, concat_axis=4, tile...]
    reduce_scatter x4 -> x5, waiting for transfers between devices: 165 us -> 261 us  [per_device(): lax.psum_scatter(flat, 'col', scatter_dimension=2, tiled=True)]
    dot_general x1 -> x2, local copies, waits for them, and re-layouts: 39.8 us -> 77.7 us  [per_device(): jnp.einsum('ikac,kcjb->iajb', blocks, masked_ints, precision=lax.Precisio...]
    dot_general x4 -> x5, matrix products: 78.2 us -> 105 us  [per_device(): jnp.einsum('ikac,kcjb->iajb', blocks, masked_ints, precision=lax.Precisio...]
    select_n x1 -> x3, other arithmetic: 11.3 us -> 30 us  [the longest x1 23.1 us: per_device(): masked_ints = jnp.where(int_sym == 0, cycle_integrals, 0.0)]
    slice x1 -> x4, local copies, waits for them, and re-layouts: 0.87 us -> 16.5 us  [the longest x2 15.7 us: per_device(): amps = amplitudes[start:start + rows]]
    reshape x8 -> x6, local copies, waits for them, and re-layouts: 40 us -> 25.6 us  [the longest x5 20.8 us: per_device(): amps.reshape(rows, col_count, k_local, row_count, a_local, c_local)]
    transpose x0 -> x4, local copies, waits for them, and re-layouts: none -> 14.2 us  [per_device(): jnp.transpose(grouped, (0, 3, 1, 2, 4, 5))]
  transfers between devices with their start and end apart: 8 -> 10, of which waited for: 6 -> 8; matrix products, arithmetic and copies ran while one was open for 29% -> 35% of each run, Pallas kernels for 0% -> 0%
where the time goes in v2:
time: 771 us; the launch traced here: 764 us
  waiting for transfers between devices  407 us (53%)
  local copies, waits for them, and re-layouts  160 us (21%)
  matrix products  105 us (14%)
  other arithmetic  55 us (7%)
  starting transfers between devices  23 us (3%)
  between operations  13.8 us (2%)
    reduce_scatter x5, waiting for transfers between devices, per_device(): lax.psum_scatter(flat, 'col', scatter_dimension=2, tiled=True)  261 us
    all_to_all x5, waiting for transfers between devices, per_device(): lax.all_to_all(grouped, ('row', 'col'), split_axis=1, concat_axis=4, tile...  146 us
    dot_general x5, matrix products, per_device(): jnp.einsum('ikac,kcjb->iajb', blocks, masked_ints, precision=lax.Precisio...  105 us
    dot_general x2, local copies, waits for them, and re-layouts, per_device(): jnp.einsum('ikac,kcjb->iajb', blocks, masked_ints, precision=lax.Precisio...  77.7 us
    select_n x1, other arithmetic, per_device(): masked_ints = jnp.where(int_sym == 0, cycle_integrals, 0.0)  23.1 us
    dot_general x1, other arithmetic, per_device(): jnp.einsum('ikac,kcjb->iajb', blocks, masked_ints, precision=lax.Precisio...  22.8 us
    all_to_all x5, starting transfers between devices, per_device(): lax.all_to_all(grouped, ('row', 'col'), split_axis=1, concat_axis=4, tile...  22.1 us
    reshape x5, local copies, waits for them, and re-layouts, per_device(): amps.reshape(rows, col_count, k_local, row_count, a_local, c_local)  20.8 us
  transfers between devices with their start and end apart: 10, of which 8 were waited for; matrix products, arithmetic and copies ran while one was open for 35% of the time, Pallas kernels for 0%

profile of v2, /device:TPU:0, one launch (start us, length us, event | category | flops | bytes accessed | tf_op | source)
XLA Modules:
  0.0 764.0 jit_solution(7293487511744157805)
XLA Ops:
  6.5 10.6 %fusion.28 = (f32[2,64,512,16]{2,3,1,0:T(8,128)}, f32[2,64,512,16]{2,3,1,0:T(8,128)}, f32[2,64,512,16]{2,3,1,0:T(8,128)}) fusion(f32[8,64,512,16]{2,3,1,0:T(8,128)} %param.4), kind=kLoop, calls=%fused_computation.49 | loop fusion | bytes 25165824 | tf_op jit(solution)/shard_map/slice | solution.py:38
  17.1 5.2 reshape.283
  22.3 4.8 copy.83
  27.2 7.4 all-to-all-start
  34.6 5.3 reshape.288
  46.7 23.1 %fusion.4 = f32[8,512,4,512]{3,2,1,0:T(4,128)} fusion(f32[8,512,4,512]{3,2,1,0:T(4,128)} %param.5, s32[4,512]{1,0:T(4,128)S(1)} %broadcast_xor_fusion.2, s32[8,512]{1,0:T(8,128)S(1)} %broadcast_xor_fusion.1), kind=kLoop, calls=%fused_computation.5 | loop fusion | flops 25165824 | bytes 67133440 | tf_op jit(solution)/shard_map/jit(_where)/select_n | solution.py:33
  74.4 56.1 %all-to-all-done = f32[2,32,8,128,16]{3,4,2,0,1:T(8,128)} async-done(((f32[2,32,8,128,16]{3,4,2,0,1:T(8,128)}), f32[2,32,8,128,16]{3,4,2,0,1:T(8,128)}, u32[]{:S(2)}, u32[]{:S(2)}) %all-to-all-start) | async-done | bytes 4194336 | tf_op jit(solution)/shard_map/all_to_all | solution.py:47
  134.4 22.8 %fusion.37 = f32[4,512,512,8]{1,0,2,3:T(4,128)} fusion(f32[8,512,4,512]{3,2,1,0:T(4,128)} %param.5, s32[4,512]{1,0:T(4,128)S(1)} %broadcast_xor_fusion.2, s32[8,512]{1,0:T(8,128)S(1)} %broadcast_xor_fusion.1), kind=kLoop, calls=%fused_computation.52 | loop fusion | flops 25165824 | bytes 67133440 | tf_op jit(solution)/shard_map/ikac,kcjb->iajb/dot_general | solution.py:55
  157.2 37.9 %copy.84 = f32[4,512,512,8]{2,1,0,3:T(8,128)} copy(f32[4,512,512,8]{1,0,2,3:T(4,128)} %fusion.37) | data formatting | bytes 67108864 | tf_op jit(solution)/shard_map/ikac,kcjb->iajb/dot_general | solution.py:55
  200.6 32.3 %convolution_bitcast_fusion = f32[2,128,2048]{2,1,0:T(8,128)} fusion(f32[2,8,128,512]{2,3,1,0:T(8,128)} %bitcast_select_fusion.2, f32[2048,512,8,1]{1,0,2,3:T(8,128)} %bitcast.110), kind=kOutput, calls=%fused_computation.14 | convolution fusion | flops 12884901888 | bytes 39845888 | tf_op jit(solution)/shard_map/ikac,kcjb->iajb/dot_general | solution.py:55
  232.9 5.3 reshape.281
  243.0 59.5 %reduce-scatter.6.cloned.1.call-done = f32[2,128,256]{2,1,0:T(8,128)} async-done(((f32[2,128,2048]{2,1,0:T(8,128)}), f32[2,128,256]{2,1,0:T(8,128)}) %reduce-scatter.6.cloned.1.call-update) | async-done | bytes 262160 | tf_op jit(solution)/shard_map/reduce_scatter | solution.py:63
  311.2 39.8 %dot_general.35 = f32[2048,512,8]{0,1,2:T(8,128)} reshape(f32[4,512,512,8]{1,0,2,3:T(4,128)} %bitcast.109) | data formatting | bytes 67108864 | tf_op jit(solution)/shard_map/ikac,kcjb->iajb/dot_general | solution.py:55
  355.6 51.3 %all-to-all-done.2 = f32[2,32,8,128,16]{3,4,2,0,1:T(8,128)} async-done(((f32[2,32,8,128,16]{3,4,2,0,1:T(8,128)}), f32[2,32,8,128,16]{3,4,2,0,1:T(8,128)}, u32[]{:S(2)}, u32[]{:S(2)}) %all-to-all-start.2) | async-done | bytes 4194336 | tf_op jit(solution)/shard_map/all_to_all | solution.py:47
  414.6 19.4 %fusion.5 = f32[2,128,2048]{2,1,0:T(8,128)} fusion(f32[2,8,128,512]{2,3,1,0:T(8,128)} %get-tuple-element.29, f32[2048,512,8]{0,1,2:T(8,128)} %dot_general.35), kind=kOutput, calls=%fused_computation.12 | convolution fusion | flops 12884901888 | bytes 39845888 | tf_op jit(solution)/shard_map/ikac,kcjb->iajb/dot_general | solution.py:55
  434.2 19.5 %fusion.8 = f32[2,128,2048]{2,1,0:T(8,128)} fusion(f32[2,8,128,512]{2,3,1,0:T(8,128)} %get-tuple-element.28, f32[2048,512,8]{0,1,2:T(8,128)} %dot_general.35), kind=kOutput, calls=%fused_computation.13 | convolution fusion | flops 12884901888 | bytes 39845888 | tf_op jit(solution)/shard_map/ikac,kcjb->iajb/dot_general | solution.py:55
  453.7 5.2 fusion.27
  462.5 37.3 %reduce-scatter.8.cloned.1.call-done = f32[2,128,256]{2,1,0:T(8,128)} async-done(((f32[2,128,2048]{2,1,0:T(8,128)}), f32[2,128,256]{2,1,0:T(8,128)}) %reduce-scatter.8.cloned.1.call-update) | async-done | bytes 262160 | tf_op jit(solution)/shard_map/reduce_scatter | solution.py:63
  509.5 86.0 %reduce-scatter.10.cloned.1.call-done = f32[2,128,256]{2,1,0:T(8,128)} async-done(((f32[2,128,2048]{2,1,0:T(8,128)}), f32[2,128,256]{2,1,0:T(8,128)}) %reduce-scatter.10.cloned.1.call-update) | async-done | bytes 262160 | tf_op jit(solution)/shard_map/reduce_scatter | solution.py:63
  602.0 16.9 %convolution_bitcast_fusion.2 = f32[1,128,2048]{2,1,0:T(8,128)} fusion(f32[2048,512,8]{0,1,2:T(8,128)} %dot_general.35, f32[8,128,512]{1,2,0:T(8,128)S(1)} %bitcast.118, s32[128,512]{0,1:T(8,128)S(1)} %broadcast_xor_fusion, s32[8]{0:T(128)S(1)} %broadcast_xor_fusion.7), kind=kOutput, calls=%fused_computation.16 | convolution fusion | flops 6444023808 | bytes 36962336 | tf_op jit(solution)/shard_map/ikac,kcjb->iajb/dot_general | solution.py:55
  619.0 38.8 %all-to-all-done.4 = f32[1,32,8,128,16]{3,4,2,0,1:T(8,128)} async-done(((f32[1,32,8,128,16]{3,4,2,0,1:T(8,128)}), f32[1,32,8,128,16]{3,4,2,0,1:T(8,128)}, u32[]{:S(2)}, u32[]{:S(2)}) %all-to-all-start.4) | async-done | bytes 2097184 | tf_op jit(solution)/shard_map/all_to_all | solution.py:47
  659.5 17.1 %convolution_bitcast_fusion.1 = f32[1,128,2048]{2,1,0:T(8,128)} fusion(f32[2048,512,8]{0,1,2:T(8,128)} %dot_general.35, f32[8,128,512]{1,2,0:T(8,128)S(1)} %bitcast.117, s32[8]{0:T(128)S(1)} %copy-done.8, s32[128,512]{0,1:T(8,128)S(1)} %broadcast_xor_fusion), kind=kOutput, calls=%fused_computation.15 | convolution fusion | flops 6444023808 | bytes 36962336 | tf_op jit(solution)/shard_map/ikac,kcjb->iajb/dot_general | solution.py:55
  676.7 12.2 %reduce-scatter.12.cloned.1.call-done = f32[1,128,256]{2,1,0:T(8,128)} async-done(((f32[1,128,2048]{2,1,0:T(8,128)}), f32[1,128,256]{2,1,0:T(8,128)}) %reduce-scatter.12.cloned.1.call-update) | async-done | bytes 131088 | tf_op jit(solution)/shard_map/reduce_scatter | solution.py:63
  689.9 65.6 %reduce-scatter.14.cloned.1.call-done = f32[1,128,256]{2,1,0:T(8,128)} async-done(((f32[1,128,2048]{2,1,0:T(8,128)}), f32[1,128,256]{2,1,0:T(8,128)}) %reduce-scatter.14.cloned.1.call-update) | async-done | bytes 131088 | tf_op jit(solution)/shard_map/reduce_scatter | solution.py:63
  (63 shorter events, 70.8 us)
Async XLA Ops:
  27.2 103.4 %all-to-all-start = ((f32[2,32,8,128,16]{3,4,2,0,1:T(8,128)}), f32[2,32,8,128,16]{3,4,2,0,1:T(8,128)}, u32[]{:S(2)}, u32[]{:S(2)}) async-start(f32[2,32,8,128,16]{3,4,2,0,1:T(8,128)} %bitcast.111), calls=%async_computation | async-start | bytes 8388608 | tf_op jit(solution)/shard_map/all_to_all | solution.py:47
  39.9 4.7 copy-start.6
  39.9 6.6 copy-start.7
  130.6 176.5 %all-to-all-start.1 = ((f32[2,32,8,128,16]{3,4,2,0,1:T(8,128)}), f32[2,32,8,128,16]{3,4,2,0,1:T(8,128)}, u32[]{:S(2)}, u32[]{:S(2)}) async-start(f32[2,32,8,128,16]{3,4,2,0,1:T(8,128)} %copy.53), calls=%async_computation.2 | async-start | bytes 8388608 | tf_op jit(solution)/shard_map/all_to_all | solution.py:47
  134.1 168.3 %reduce-scatter.6.cloned.1.call-start = ((), (), s32[]{:S(2)}) async-start(), calls=%async_computation.10 | async-start | bytes 2359296 | tf_op jit(solution)/shard_map/reduce_scatter | solution.py:63
  307.1 99.8 %all-to-all-start.2 = ((f32[2,32,8,128,16]{3,4,2,0,1:T(8,128)}), f32[2,32,8,128,16]{3,4,2,0,1:T(8,128)}, u32[]{:S(2)}, u32[]{:S(2)}) async-start(f32[2,32,8,128,16]{3,4,2,0,1:T(8,128)} %copy.58), calls=%async_computation.4 | async-start | bytes 8388608 | tf_op jit(solution)/shard_map/all_to_all | solution.py:47
  310.9 188.9 %reduce-scatter.8.cloned.1.call-start = ((), (), s32[]{:S(2)}) async-start(), calls=%async_computation.11 | async-start | bytes 2359296 | tf_op jit(solution)/shard_map/reduce_scatter | solution.py:63
  406.9 3.4 copy-start
  434.1 161.4 %reduce-scatter.10.cloned.1.call-start = ((), (), s32[]{:S(2)}) async-start(), calls=%async_computation.12 | async-start | bytes 2359296 | tf_op jit(solution)/shard_map/reduce_scatter | solution.py:63
  499.8 95.7 %all-to-all-start.3 = ((f32[1,32,8,128,16]{3,4,2,0,1:T(8,128)}), f32[1,32,8,128,16]{3,4,2,0,1:T(8,128)S(1)}, u32[]{:S(2)}, u32[]{:S(2)}) async-start(f32[1,32,8,128,16]{3,4,2,0,1:T(8,128)} %bitcast.119), calls=%async_computation.6 | async-start | bytes 4194304 | tf_op jit(solution)/shard_map/all_to_all | solution.py:47
  595.5 4.1 copy-start.1
  595.5 62.2 %all-to-all-start.4 = ((f32[1,32,8,128,16]{3,4,2,0,1:T(8,128)}), f32[1,32,8,128,16]{3,4,2,0,1:T(8,128)}, u32[]{:S(2)}, u32[]{:S(2)}) async-start(f32[1,32,8,128,16]{3,4,2,0,1:T(8,128)} %bitcast.41), calls=%async_computation.8 | async-start | bytes 4194304 | tf_op jit(solution)/shard_map/all_to_all | solution.py:47
  599.2 89.7 %reduce-scatter.12.cloned.1.call-start = ((), (), s32[]{:S(2)}) async-start(), calls=%async_computation.13 | async-start | bytes 1179648 | tf_op jit(solution)/shard_map/reduce_scatter | solution.py:63
  618.9 40.6 %copy-start.8 = (s32[8]{0:T(128)S(1)}, s32[8]{0:T(128)}, u32[]{:S(2)}) copy-start(s32[8]{0:T(128)} %get-tuple-element.21) | copy-start | bytes 100
  618.9 136.6 %reduce-scatter.14.cloned.1.call-start = ((), (), s32[]{:S(2)}) async-start(), calls=%async_computation.14 | async-start | bytes 1179648 | tf_op jit(solution)/shard_map/reduce_scatter | solution.py:63
  659.5 17.1 %copy-start.2 = (f32[2,128,256]{2,1,0:T(8,128)S(1)}, f32[2,128,256]{2,1,0:T(8,128)}, u32[]{:S(2)}) copy-start(f32[2,128,256]{2,1,0:T(8,128)} %reduce-scatter.6.cloned.1.call-done) | copy-start | bytes 786436
  659.5 17.2 %copy-start.3 = (f32[2,128,256]{2,1,0:T(8,128)S(1)}, f32[2,128,256]{2,1,0:T(8,128)}, u32[]{:S(2)}) copy-start(f32[2,128,256]{2,1,0:T(8,128)} %reduce-scatter.8.cloned.1.call-done) | copy-start | bytes 786436
  659.5 17.2 %copy-start.4 = (f32[2,128,256]{2,1,0:T(8,128)S(1)}, f32[2,128,256]{2,1,0:T(8,128)}, u32[]{:S(2)}) copy-start(f32[2,128,256]{2,1,0:T(8,128)} %reduce-scatter.10.cloned.1.call-done) | copy-start | bytes 786436
  689.8 65.6 %copy-start.5 = (f32[8,128,256]{2,1,0:T(8,128)}, f32[8,128,256]{2,1,0:T(8,128)S(1)}, u32[]{:S(2)}) copy-start(f32[8,128,256]{2,1,0:T(8,128)S(1)} %constant_dynamic-update-slice_fusion.1) | copy-start | bytes 3145732
Sparse Core Ops, SparseCore 0:
  233.0 69.3 reduce-scatter.5
  434.2 65.4 reduce-scatter.7
  503.3 92.1 reduce-scatter.9
  619.0 69.8 reduce-scatter.11
  692.6 62.8 reduce-scatter.13

commit v3 on v1

--- a/solution.py
+++ b/solution.py
@@ -26,22 +26,27 @@
     )
     masked_ints = jnp.where(int_sym == 0, cycle_integrals, 0.0)
 
-    chunks = 4 if slab_rows % 4 == 0 else 1
-    rows = slab_rows // chunks
-    results = []
-    for step in range(chunks):
-        amps = amplitudes[step * rows:(step + 1) * rows]
+    rows = 1
+    chunks = slab_rows // rows
+
+    def prepare(step):
+        amps = lax.dynamic_slice_in_dim(amplitudes, step * rows, rows, axis=0)
+        row_irrep = lax.dynamic_slice_in_dim(slab_irrep, step * rows, rows)
         amp_sym = (
-            slab_irrep[step * rows:(step + 1) * rows, None, None, None]
+            row_irrep[:, None, None, None]
             ^ occ_irrep[None, :, None, None]
             ^ (virt_irrep[None, None, :, None] ^ c_irrep[None, None, None, :])
         )
         masked_amps = jnp.where(amp_sym == 0, amps, 0.0)
         grouped = masked_amps.reshape(rows, col_count, k_local, row_count, a_local, c_local)
-        grouped = jnp.transpose(grouped, (0, 3, 1, 2, 4, 5)).reshape(
+        return jnp.transpose(grouped, (0, 3, 1, 2, 4, 5)).reshape(
             rows, row_count * col_count, k_local, a_local, c_local
         )
-        items = lax.all_to_all(grouped, ("row", "col"), split_axis=1, concat_axis=4, tiled=True)
+
+    def exchange(grouped):
+        return lax.all_to_all(grouped, ("row", "col"), split_axis=1, concat_axis=4, tiled=True)
+
+    def contract(items):
         blocks = items.reshape(rows, k_local, a_local, virt_count)
         partial_value = jnp.einsum(
             "ikac,kcjb->iajb",
@@ -51,8 +56,21 @@
             preferred_element_type=jnp.float32,
         )
         flat = partial_value.reshape(rows, a_local, column_slab * virt_count)
-        results.append(lax.psum_scatter(flat, "col", scatter_dimension=2, tiled=True))
-    return jnp.concatenate(results, axis=0)
+        return lax.psum_scatter(flat, "col", scatter_dimension=2, tiled=True)
+
+    out = jnp.zeros((slab_rows, a_local, column_slab * virt_count // col_count), jnp.float32)
+    received = exchange(prepare(0))
+    upcoming = prepare(min(1, chunks - 1))
+
+    def body(step, carry):
+        received, upcoming, out = carry
+        next_received = exchange(upcoming)
+        next_upcoming = prepare(jnp.minimum(step + 2, chunks - 1))
+        out = lax.dynamic_update_slice_in_dim(out, contract(received), step * rows, axis=0)
+        return next_received, next_upcoming, out
+
+    received, upcoming, out = lax.fori_loop(0, chunks - 1, body, (received, upcoming, out))
+    return lax.dynamic_update_slice_in_dim(out, contract(received), (chunks - 1) * rows, axis=0)
 
 
 def solution(mesh):

time: 663 us -> 974 us (1.47)
  local copies, waits for them, and re-layouts: 100 us -> 230 us
  matrix products: 78.2 us -> 191 us
  waiting for transfers between devices: 410 us -> 439 us
  other arithmetic: 38.3 us -> 58.5 us
  starting transfers between devices: 21.1 us -> 36.3 us
    reduce_scatter x4 -> x8, waiting for transfers between devices: 165 us -> 439 us  [contract(): return lax.psum_scatter(flat, 'col', scatter_dimension=2, tiled=True)]
    all_to_all x4 -> x8, waiting for transfers between devices: 245 us -> 0.02 us  [exchange(): lax.all_to_all(grouped, ('row', 'col'), split_axis=1, concat_axis=4, tile...]
    dot_general x4 -> x8, matrix products: 78.2 us -> 191 us  [contract(): jnp.einsum('ikac,kcjb->iajb', blocks, masked_ints, precision=lax.Precisio...]
    another operation x0 -> x7, local copies, waits for them, and re-layouts: none -> 74.1 us
    reshape x8 -> x18, local copies, waits for them, and re-layouts: 40 us -> 89.5 us  [prepare(): masked_amps.reshape(rows, col_count, k_local, row_count, a_local, c_local)]
    dot_general x1 -> x0, local copies, waits for them, and re-layouts: 39.8 us -> none  [per_device(): jnp.einsum('ikac,kcjb->iajb', blocks, masked_ints, precision=lax.Precisio...]
    select_n x1 -> x9, other arithmetic: 11.3 us -> 50.7 us  [the longest x8 26.4 us: prepare(): masked_amps = jnp.where(amp_sym == 0, amps, 0.0)]
    unnamed x4 -> x7, local copies, waits for them, and re-layouts: 0.01 us -> 37.9 us
  transfers between devices with their start and end apart: 8 -> 16, of which waited for: 6 -> 8; matrix products, arithmetic and copies ran while one was open for 29% -> 36% of each run, Pallas kernels for 0% -> 0%
where the time goes in v3:
time: 974 us; the launch traced here: 970 us
  waiting for transfers between devices  439 us (45%)
  local copies, waits for them, and re-layouts  230 us (24%)
  matrix products  191 us (20%)
  other arithmetic  58.5 us (6%)
  starting transfers between devices  36.3 us (4%)
  between operations  14.9 us (2%)
    reduce_scatter x8, waiting for transfers between devices, contract(): return lax.psum_scatter(flat, 'col', scatter_dimension=2, tiled=True)  439 us
    dot_general x8, matrix products, contract(): jnp.einsum('ikac,kcjb->iajb', blocks, masked_ints, precision=lax.Precisio...  191 us
    reshape x18, local copies, waits for them, and re-layouts, prepare(): masked_amps.reshape(rows, col_count, k_local, row_count, a_local, c_local)  89.5 us
    another operation x7, local copies, waits for them, and re-layouts  74.1 us
    unnamed x7, local copies, waits for them, and re-layouts  37.9 us
    all_to_all x8, starting transfers between devices, exchange(): lax.all_to_all(grouped, ('row', 'col'), split_axis=1, concat_axis=4, tile...  35.8 us
    select_n x8, other arithmetic, prepare(): masked_amps = jnp.where(amp_sym == 0, amps, 0.0)  26.4 us
    select_n x1, other arithmetic, per_device(): masked_ints = jnp.where(int_sym == 0, cycle_integrals, 0.0)  24.3 us
  transfers between devices with their start and end apart: 16, of which 8 were waited for; matrix products, arithmetic and copies ran while one was open for 36% of the time, Pallas kernels for 0%

profile of v3, /device:TPU:0, one launch (start us, length us, event | category | flops | bytes accessed | tf_op | source)
XLA Modules:
  0.0 970.2 jit_solution(1145300672956576604)
XLA Ops:
  41.1 37.9 %copy.33 = f32[8,512,4,512]{1,3,2,0:T(8,128)} copy(f32[8,512,4,512]{3,2,1,0:T(4,128)} %param.7) | data formatting | bytes 67108864 | tf_op args[1]
  79.2 24.3 %fusion.1 = f32[8,512,4,512]{1,3,2,0:T(8,128)} fusion(f32[8,512,4,512]{1,3,2,0:T(8,128)} %copy.33, s32[4,512]{1,0:T(4,128)S(1)} %broadcast_xor_fusion.4, s32[8,512]{1,0:T(8,128)S(1)} %broadcast_xor_fusion.3), kind=kLoop, calls=%fused_computation.8 | loop fusion | flops 25165824 | bytes 67133440 | tf_op jit(solution)/shard_map/jit(_where)/select_n | solution.py:27
  105.3 768.3 %while.17 = (s32[]{:T(128)}, f32[1,1,8,128,512]{3,4,2,1,0:T(8,128)S(1)}, f32[1,32,8,128,16]{4,3,2,1,0:T(8,128)}, f32[8,128,256]{2,1,0:T(8,128)S(1)}, s32[8]{0:T(...) while((s32[]{:T(128)}, ...), condition=%wide.region_2.3_spmd, body=%wide.region_0.2_spmd.sunk | while | flops 6444032000 | bytes 67832944 | solution.py:72
  105.3 10.6 %copy.40 = f32[1,32,8,128,16]{3,4,2,0,1:T(8,128)} copy(f32[1,32,8,128,16]{4,3,2,1,0:T(8,128)} %get-tuple-element.283) | data formatting | bytes 4194304 | tf_op jit(solution)/shard_map
  121.9 23.8 %convolution_bitcast_fusion.3 = f32[1,128,2048]{2,1,0:T(8,128)} fusion(f32[2048,512,8]{1,0,2:T(8,128)} %bitcast.73, f32[1,1,8,128,512]{3,4,2,1,0:T(8,128)S(1)} %get-tuple-element.282), kind=kOutput, calls=%fused_computation.clone.1 | convolution fusion | flops 6442450944 | bytes 36700160 | tf_op jit(solution)/shard_map/while/body/eval_jaxpr/ikac,kcjb->iajb/dot_general | solution.py:51
  160.6 53.6 %reduce-scatter.5.cloned.1.call-done = f32[1,128,256]{2,1,0:T(8,128)} async-done(((f32[1,128,2048]{2,1,0:T(8,128)}), f32[1,128,256]{2,1,0:T(8,128)}) %reduce-scatter.5.cloned.1.call-update) | async-done | bytes 131088 | tf_op jit(solution)/shard_map/while/body/eval_jaxpr/reduce_scatter | solution.py:59
  216.9 10.6 %copy.40 = f32[1,32,8,128,16]{3,4,2,0,1:T(8,128)} copy(f32[1,32,8,128,16]{4,3,2,1,0:T(8,128)} %get-tuple-element.283) | data formatting | bytes 4194304 | tf_op jit(solution)/shard_map
  231.3 23.8 %convolution_bitcast_fusion.3 = f32[1,128,2048]{2,1,0:T(8,128)} fusion(f32[2048,512,8]{1,0,2:T(8,128)} %bitcast.73, f32[1,1,8,128,512]{3,4,2,1,0:T(8,128)S(1)} %get-tuple-element.282), kind=kOutput, calls=%fused_computation.clone.1 | convolution fusion | flops 6442450944 | bytes 36700160 | tf_op jit(solution)/shard_map/while/body/eval_jaxpr/ikac,kcjb->iajb/dot_general | solution.py:51
  270.0 53.7 %reduce-scatter.5.cloned.1.call-done = f32[1,128,256]{2,1,0:T(8,128)} async-done(((f32[1,128,2048]{2,1,0:T(8,128)}), f32[1,128,256]{2,1,0:T(8,128)}) %reduce-scatter.5.cloned.1.call-update) | async-done | bytes 131088 | tf_op jit(solution)/shard_map/while/body/eval_jaxpr/reduce_scatter | solution.py:59
  326.4 10.6 %copy.40 = f32[1,32,8,128,16]{3,4,2,0,1:T(8,128)} copy(f32[1,32,8,128,16]{4,3,2,1,0:T(8,128)} %get-tuple-element.283) | data formatting | bytes 4194304 | tf_op jit(solution)/shard_map
  340.8 23.8 %convolution_bitcast_fusion.3 = f32[1,128,2048]{2,1,0:T(8,128)} fusion(f32[2048,512,8]{1,0,2:T(8,128)} %bitcast.73, f32[1,1,8,128,512]{3,4,2,1,0:T(8,128)S(1)} %get-tuple-element.282), kind=kOutput, calls=%fused_computation.clone.1 | convolution fusion | flops 6442450944 | bytes 36700160 | tf_op jit(solution)/shard_map/while/body/eval_jaxpr/ikac,kcjb->iajb/dot_general | solution.py:51
  379.5 53.6 %reduce-scatter.5.cloned.1.call-done = f32[1,128,256]{2,1,0:T(8,128)} async-done(((f32[1,128,2048]{2,1,0:T(8,128)}), f32[1,128,256]{2,1,0:T(8,128)}) %reduce-scatter.5.cloned.1.call-update) | async-done | bytes 131088 | tf_op jit(solution)/shard_map/while/body/eval_jaxpr/reduce_scatter | solution.py:59
  435.9 10.6 %copy.40 = f32[1,32,8,128,16]{3,4,2,0,1:T(8,128)} copy(f32[1,32,8,128,16]{4,3,2,1,0:T(8,128)} %get-tuple-element.283) | data formatting | bytes 4194304 | tf_op jit(solution)/shard_map
  450.3 23.8 %convolution_bitcast_fusion.3 = f32[1,128,2048]{2,1,0:T(8,128)} fusion(f32[2048,512,8]{1,0,2:T(8,128)} %bitcast.73, f32[1,1,8,128,512]{3,4,2,1,0:T(8,128)S(1)} %get-tuple-element.282), kind=kOutput, calls=%fused_computation.clone.1 | convolution fusion | flops 6442450944 | bytes 36700160 | tf_op jit(solution)/shard_map/while/body/eval_jaxpr/ikac,kcjb->iajb/dot_general | solution.py:51
  489.0 53.6 %reduce-scatter.5.cloned.1.call-done = f32[1,128,256]{2,1,0:T(8,128)} async-done(((f32[1,128,2048]{2,1,0:T(8,128)}), f32[1,128,256]{2,1,0:T(8,128)}) %reduce-scatter.5.cloned.1.call-update) | async-done | bytes 131088 | tf_op jit(solution)/shard_map/while/body/eval_jaxpr/reduce_scatter | solution.py:59
  545.3 10.6 %copy.40 = f32[1,32,8,128,16]{3,4,2,0,1:T(8,128)} copy(f32[1,32,8,128,16]{4,3,2,1,0:T(8,128)} %get-tuple-element.283) | data formatting | bytes 4194304 | tf_op jit(solution)/shard_map
  559.7 23.8 %convolution_bitcast_fusion.3 = f32[1,128,2048]{2,1,0:T(8,128)} fusion(f32[2048,512,8]{1,0,2:T(8,128)} %bitcast.73, f32[1,1,8,128,512]{3,4,2,1,0:T(8,128)S(1)} %get-tuple-element.282), kind=kOutput, calls=%fused_computation.clone.1 | convolution fusion | flops 6442450944 | bytes 36700160 | tf_op jit(solution)/shard_map/while/body/eval_jaxpr/ikac,kcjb->iajb/dot_general | solution.py:51
  598.4 53.6 %reduce-scatter.5.cloned.1.call-done = f32[1,128,256]{2,1,0:T(8,128)} async-done(((f32[1,128,2048]{2,1,0:T(8,128)}), f32[1,128,256]{2,1,0:T(8,128)}) %reduce-scatter.5.cloned.1.call-update) | async-done | bytes 131088 | tf_op jit(solution)/shard_map/while/body/eval_jaxpr/reduce_scatter | solution.py:59
  669.1 23.8 %convolution_bitcast_fusion.3 = f32[1,128,2048]{2,1,0:T(8,128)} fusion(f32[2048,512,8]{1,0,2:T(8,128)} %bitcast.73, f32[1,1,8,128,512]{3,4,2,1,0:T(8,128)S(1)} %get-tuple-element.282), kind=kOutput, calls=%fused_computation.clone.1 | convolution fusion | flops 6442450944 | bytes 36700160 | tf_op jit(solution)/shard_map/while/body/eval_jaxpr/ikac,kcjb->iajb/dot_general | solution.py:51
  707.8 53.6 %reduce-scatter.5.cloned.1.call-done = f32[1,128,256]{2,1,0:T(8,128)} async-done(((f32[1,128,2048]{2,1,0:T(8,128)}), f32[1,128,256]{2,1,0:T(8,128)}) %reduce-scatter.5.cloned.1.call-update) | async-done | bytes 131088 | tf_op jit(solution)/shard_map/while/body/eval_jaxpr/reduce_scatter | solution.py:59
  778.6 23.8 %convolution_bitcast_fusion.3 = f32[1,128,2048]{2,1,0:T(8,128)} fusion(f32[2048,512,8]{1,0,2:T(8,128)} %bitcast.73, f32[1,1,8,128,512]{3,4,2,1,0:T(8,128)S(1)} %get-tuple-element.282), kind=kOutput, calls=%fused_computation.clone.1 | convolution fusion | flops 6442450944 | bytes 36700160 | tf_op jit(solution)/shard_map/while/body/eval_jaxpr/ikac,kcjb->iajb/dot_general | solution.py:51
  817.3 53.6 %reduce-scatter.5.cloned.1.call-done = f32[1,128,256]{2,1,0:T(8,128)} async-done(((f32[1,128,2048]{2,1,0:T(8,128)}), f32[1,128,256]{2,1,0:T(8,128)}) %reduce-scatter.5.cloned.1.call-update) | async-done | bytes 131088 | tf_op jit(solution)/shard_map/while/body/eval_jaxpr/reduce_scatter | solution.py:59
  873.9 24.0 %convolution_bitcast_fusion.1 = f32[1,128,2048]{2,1,0:T(8,128)} fusion(f32[2048,512,8]{1,0,2:T(8,128)} %bitcast.74, f32[1,1,8,128,512]{3,4,2,1,0:T(8,128)S(1)} %get-tuple-element.176), kind=kOutput, calls=%fused_computation.9 | convolution fusion | flops 6442450944 | bytes 36700160 | tf_op jit(solution)/shard_map/ikac,kcjb->iajb/dot_general | solution.py:51
  897.9 63.2 %reduce-scatter.3.cloned.1.call-done = f32[1,128,256]{2,1,0:T(8,128)} async-done(((f32[1,128,2048]{2,1,0:T(8,128)}), f32[1,128,256]{2,1,0:T(8,128)}) %reduce-scatter.3.cloned.1.call-update) | async-done | bytes 131088 | tf_op jit(solution)/shard_map/reduce_scatter | solution.py:59
  (111 shorter events, 210.1 us)
Async XLA Ops:
  22.2 81.2 %all-to-all-start.1 = ((f32[1,32,8,128,16]{3,4,2,0,1:T(8,128)}), f32[1,32,8,128,16]{3,4,2,0,1:T(8,128)}, u32[]{:S(2)}, u32[]{:S(2)}) async-start(f32[1,32,8,128,16]{3,4,2,0,1:T(8,128)} %bitcast.79), calls=%async_computation.2 | async-start | bytes 4194304 | tf_op jit(solution)/shard_map/all_to_all | solution.py:47
  41.1 37.9 %copy-start.2 = (s32[64]{0:T(128)S(1)}, s32[64]{0:T(128)}, u32[]{:S(2)}) copy-start(s32[64]{0:T(128)} %param.8) | copy-start | bytes 772
  41.1 38.0 %copy-start.1 = (s32[512]{0:T(512)S(1)}, s32[512]{0:T(512)}, u32[]{:S(2)}) copy-start(s32[512]{0:T(512)} %param.9) | copy-start | bytes 6148
  115.9 99.2 %all-to-all-start = ((f32[1,32,8,128,16]{3,4,2,0,1:T(8,128)}), f32[1,32,8,128,16]{3,4,2,0,1:T(8,128)}, u32[]{:S(2)}, u32[]{:S(2)}) async-start(f32[1,32,8,128,16]{3,4,2,0,1:T(8,128)} %copy.40), calls=%async_computation | async-start | bytes 4194304 | tf_op jit(solution)/shard_map/while/body/eval_jaxpr/all_to_all | solution.py:47
  121.8 92.4 %reduce-scatter.5.cloned.1.call-start = ((), (), s32[]{:S(2)}) async-start(), calls=%async_computation.5 | async-start | bytes 1179648 | tf_op jit(solution)/shard_map/while/body/eval_jaxpr/reduce_scatter | solution.py:59
  227.5 97.1 %all-to-all-start = ((f32[1,32,8,128,16]{3,4,2,0,1:T(8,128)}), f32[1,32,8,128,16]{3,4,2,0,1:T(8,128)}, u32[]{:S(2)}, u32[]{:S(2)}) async-start(f32[1,32,8,128,16]{3,4,2,0,1:T(8,128)} %copy.40), calls=%async_computation | async-start | bytes 4194304 | tf_op jit(solution)/shard_map/while/body/eval_jaxpr/all_to_all | solution.py:47
  231.3 92.4 %reduce-scatter.5.cloned.1.call-start = ((), (), s32[]{:S(2)}) async-start(), calls=%async_computation.5 | async-start | bytes 1179648 | tf_op jit(solution)/shard_map/while/body/eval_jaxpr/reduce_scatter | solution.py:59
  337.0 97.1 %all-to-all-start = ((f32[1,32,8,128,16]{3,4,2,0,1:T(8,128)}), f32[1,32,8,128,16]{3,4,2,0,1:T(8,128)}, u32[]{:S(2)}, u32[]{:S(2)}) async-start(f32[1,32,8,128,16]{3,4,2,0,1:T(8,128)} %copy.40), calls=%async_computation | async-start | bytes 4194304 | tf_op jit(solution)/shard_map/while/body/eval_jaxpr/all_to_all | solution.py:47
  340.7 92.4 %reduce-scatter.5.cloned.1.call-start = ((), (), s32[]{:S(2)}) async-start(), calls=%async_computation.5 | async-start | bytes 1179648 | tf_op jit(solution)/shard_map/while/body/eval_jaxpr/reduce_scatter | solution.py:59
  446.4 97.1 %all-to-all-start = ((f32[1,32,8,128,16]{3,4,2,0,1:T(8,128)}), f32[1,32,8,128,16]{3,4,2,0,1:T(8,128)}, u32[]{:S(2)}, u32[]{:S(2)}) async-start(f32[1,32,8,128,16]{3,4,2,0,1:T(8,128)} %copy.40), calls=%async_computation | async-start | bytes 4194304 | tf_op jit(solution)/shard_map/while/body/eval_jaxpr/all_to_all | solution.py:47
  450.2 92.4 %reduce-scatter.5.cloned.1.call-start = ((), (), s32[]{:S(2)}) async-start(), calls=%async_computation.5 | async-start | bytes 1179648 | tf_op jit(solution)/shard_map/while/body/eval_jaxpr/reduce_scatter | solution.py:59
  555.9 97.0 %all-to-all-start = ((f32[1,32,8,128,16]{3,4,2,0,1:T(8,128)}), f32[1,32,8,128,16]{3,4,2,0,1:T(8,128)}, u32[]{:S(2)}, u32[]{:S(2)}) async-start(f32[1,32,8,128,16]{3,4,2,0,1:T(8,128)} %copy.40), calls=%async_computation | async-start | bytes 4194304 | tf_op jit(solution)/shard_map/while/body/eval_jaxpr/all_to_all | solution.py:47
  559.7 92.4 %reduce-scatter.5.cloned.1.call-start = ((), (), s32[]{:S(2)}) async-start(), calls=%async_computation.5 | async-start | bytes 1179648 | tf_op jit(solution)/shard_map/while/body/eval_jaxpr/reduce_scatter | solution.py:59
  665.3 97.1 %all-to-all-start = ((f32[1,32,8,128,16]{3,4,2,0,1:T(8,128)}), f32[1,32,8,128,16]{3,4,2,0,1:T(8,128)}, u32[]{:S(2)}, u32[]{:S(2)}) async-start(f32[1,32,8,128,16]{3,4,2,0,1:T(8,128)} %copy.40), calls=%async_computation | async-start | bytes 4194304 | tf_op jit(solution)/shard_map/while/body/eval_jaxpr/all_to_all | solution.py:47
  669.1 92.4 %reduce-scatter.5.cloned.1.call-start = ((), (), s32[]{:S(2)}) async-start(), calls=%async_computation.5 | async-start | bytes 1179648 | tf_op jit(solution)/shard_map/while/body/eval_jaxpr/reduce_scatter | solution.py:59
  774.8 97.1 %all-to-all-start = ((f32[1,32,8,128,16]{3,4,2,0,1:T(8,128)}), f32[1,32,8,128,16]{3,4,2,0,1:T(8,128)}, u32[]{:S(2)}, u32[]{:S(2)}) async-start(f32[1,32,8,128,16]{3,4,2,0,1:T(8,128)} %copy.40), calls=%async_computation | async-start | bytes 4194304 | tf_op jit(solution)/shard_map/while/body/eval_jaxpr/all_to_all | solution.py:47
  778.5 92.4 %reduce-scatter.5.cloned.1.call-start = ((), (), s32[]{:S(2)}) async-start(), calls=%async_computation.5 | async-start | bytes 1179648 | tf_op jit(solution)/shard_map/while/body/eval_jaxpr/reduce_scatter | solution.py:59
  873.7 24.3 %copy-start = (f32[8,128,256]{2,1,0:T(8,128)}, f32[8,128,256]{2,1,0:T(8,128)S(1)}, u32[]{:S(2)}) copy-start(f32[8,128,256]{2,1,0:T(8,128)S(1)} %get-tuple-element.175) | copy-start | bytes 3145732
  873.7 87.5 %reduce-scatter.3.cloned.1.call-start = ((), (), s32[]{:S(2)}) async-start(), calls=%async_computation.4 | async-start | bytes 1179648 | tf_op jit(solution)/shard_map/reduce_scatter | solution.py:59
Sparse Core Ops, SparseCore 0:
  145.9 68.2 reduce-scatter.4
  255.3 68.3 reduce-scatter.4
  364.8 68.3 reduce-scatter.4
  474.2 68.3 reduce-scatter.4
  583.7 68.2 reduce-scatter.4
  693.1 68.3 reduce-scatter.4
  802.6 68.3 reduce-scatter.4
Sparse Core Ops, SparseCore 1:
  898.0 63.1 reduce-scatter.2

commit v4 on v1

--- a/solution.py
+++ b/solution.py
@@ -24,11 +24,13 @@
         ^ virt_irrep[None, :, None, None]
         ^ (column_irrep[None, None, :, None] ^ virt_irrep[None, None, None, :])
     )
-    masked_ints = jnp.where(int_sym == 0, cycle_integrals, 0.0)
+    masked_ints = jnp.where(int_sym == 0, cycle_integrals, 0.0).reshape(
+        k_local * virt_count, column_slab * virt_count
+    )
 
     chunks = 4 if slab_rows % 4 == 0 else 1
     rows = slab_rows // chunks
-    results = []
+    partials = []
     for step in range(chunks):
         amps = amplitudes[step * rows:(step + 1) * rows]
         amp_sym = (
@@ -41,17 +43,22 @@
         grouped = jnp.transpose(grouped, (0, 3, 1, 2, 4, 5)).reshape(
             rows, row_count * col_count, k_local, a_local, c_local
         )
+        if step == 1:
+            grouped, masked_ints = lax.optimization_barrier((grouped, masked_ints))
+        if step >= 2:
+            grouped, partials[step - 2] = lax.optimization_barrier((grouped, partials[step - 2]))
         items = lax.all_to_all(grouped, ("row", "col"), split_axis=1, concat_axis=4, tiled=True)
-        blocks = items.reshape(rows, k_local, a_local, virt_count)
+        blocks = jnp.transpose(items.reshape(rows, k_local, a_local, virt_count), (0, 2, 1, 3))
+        blocks = blocks.reshape(rows, a_local, k_local * virt_count)
         partial_value = jnp.einsum(
-            "ikac,kcjb->iajb",
+            "iap,pq->iaq",
             blocks,
             masked_ints,
             precision=lax.Precision.HIGH,
             preferred_element_type=jnp.float32,
         )
-        flat = partial_value.reshape(rows, a_local, column_slab * virt_count)
-        results.append(lax.psum_scatter(flat, "col", scatter_dimension=2, tiled=True))
+        partials.append(partial_value.reshape(rows, a_local, column_slab * virt_count))
+    results = [lax.psum_scatter(flat, "col", scatter_dimension=2, tiled=True) for flat in partials]
     return jnp.concatenate(results, axis=0)
 
 

time: 663 us -> 634 us (0.956)
  waiting for transfers between devices: 410 us -> 341 us
  local copies, waits for them, and re-layouts: 100 us -> 142 us
    reduce_scatter x4, waiting for transfers between devices: 165 us -> 115 us  [per_device(): lax.psum_scatter(flat, 'col', scatter_dimension=2, tiled=True)]
    reshape x0 -> x2, local copies, waits for them, and re-layouts: none -> 44.6 us  [the longest x1 39.8 us: per_device(): jnp.where(int_sym == 0, cycle_integrals, 0.0)]
    dot_general x1 -> x0, local copies, waits for them, and re-layouts: 39.8 us -> none  [per_device(): jnp.einsum('ikac,kcjb->iajb', blocks, masked_ints, precision=lax.Precisio...]
    unnamed x4 -> x7, local copies, waits for them, and re-layouts: 0.01 us -> 30.1 us
    dot_general x1 -> x0, other arithmetic: 23.1 us -> none  [per_device(): jnp.einsum('ikac,kcjb->iajb', blocks, masked_ints, precision=lax.Precisio...]
    select_n x0 -> x1, other arithmetic: none -> 23.1 us  [per_device(): jnp.where(int_sym == 0, cycle_integrals, 0.0)]
    all_to_all x4, waiting for transfers between devices: 245 us -> 225 us  [per_device(): lax.all_to_all(grouped, ('row', 'col'), split_axis=1, concat_axis=4, tile...]
    reshape x8 -> x4, local copies, waits for them, and re-layouts: 40 us -> 21.1 us  [per_device(): masked_amps.reshape(rows, col_count, k_local, row_count, a_local, c_local)]
  transfers between devices with their start and end apart: 8 -> 8, of which waited for: 6 -> 6; matrix products, arithmetic and copies ran while one was open for 29% -> 37% of each run, Pallas kernels for 0% -> 0%
where the time goes in v4:
time: 634 us; the launch traced here: 631 us
  waiting for transfers between devices  341 us (54%)
  local copies, waits for them, and re-layouts  142 us (22%)
  matrix products  78.1 us (12%)
  other arithmetic  38.1 us (6%)
  starting transfers between devices  18.7 us (3%)
  between operations  13.2 us (2%)
    all_to_all x4, waiting for transfers between devices, per_device(): lax.all_to_all(grouped, ('row', 'col'), split_axis=1, concat_axis=4, tile...  225 us
    reduce_scatter x4, waiting for transfers between devices, per_device(): lax.psum_scatter(flat, 'col', scatter_dimension=2, tiled=True)  115 us
    dot_general x4, matrix products, per_device(): jnp.einsum('iap,pq->iaq', blocks, masked_ints, precision=lax.Precision.HI...  78.1 us
    reshape x1, local copies, waits for them, and re-layouts, per_device(): jnp.where(int_sym == 0, cycle_integrals, 0.0)  39.8 us
    unnamed x7, local copies, waits for them, and re-layouts  30.1 us
    select_n x1, other arithmetic, per_device(): jnp.where(int_sym == 0, cycle_integrals, 0.0)  23.1 us
    reshape x4, local copies, waits for them, and re-layouts, per_device(): masked_amps.reshape(rows, col_count, k_local, row_count, a_local, c_local)  21.1 us
    all_to_all x4, local copies, waits for them, and re-layouts, per_device(): lax.all_to_all(grouped, ('row', 'col'), split_axis=1, concat_axis=4, tile...  18.6 us
  transfers between devices with their start and end apart: 8, of which 6 were waited for; matrix products, arithmetic and copies ran while one was open for 37% of the time, Pallas kernels for 0%

profile of v4, /device:TPU:0, one launch (start us, length us, event | category | flops | bytes accessed | tf_op | source)
XLA Modules:
  0.0 631.4 jit_solution(11289657774506263178)
XLA Ops:
  9.6 11.2 %slice_select_fusion.2 = (f32[2,64,512,16]{2,3,1,0:T(8,128)}, f32[2,64,512,16]{2,3,1,0:T(8,128)}, f32[2,64,512,16]{2,3,1,0:T(8,128)}, f32[2,64,512,16]{2,3,1,0:T(8,128)}) fusion(f32[8,64,512,16]{2,3,1,0:T(8,128)} %param.4, s32[2,64]{1,0:T(2,128)S(1)} %get-tuple-element.21, s32[512,16]{0,1:T(8,128)S(1)} %broadcast_xor_fusion, ...), kind=kLoop, calls=%fused_computation.12 | loop fusion | flops 12582912 | bytes 33589248 | tf_op jit(solution)/shard_map/jit(_where)/select_n | solution.py:41
  20.9 5.3 reshape.269
  26.1 4.8 copy.41
  30.9 7.4 %all-to-all-start = ((f32[2,32,8,128,16]{3,4,2,0,1:T(8,128)}), f32[2,32,8,128,16]{3,4,2,0,1:T(8,128)}, u32[]{:S(2)}, u32[]{:S(2)}) async-start(f32[2,32,8,128,16]{3,4,2,0,1:T(8,128)} %bitcast.85), calls=%async_computation | async-start | bytes 8388608 | tf_op jit(solution)/shard_map/all_to_all | solution.py:50
  38.5 5.3 reshape.276
  43.7 4.8 copy.31
  48.7 23.1 %fusion.6 = f32[8,512,4,512]{3,2,1,0:T(4,128)} fusion(f32[8,512,4,512]{3,2,1,0:T(4,128)} %param.5, s32[4,512]{1,0:T(4,128)S(1)} %broadcast_xor_fusion.2, s32[8,512]{1,0:T(8,128)S(1)} %broadcast_xor_fusion.1), kind=kLoop, calls=%fused_computation.7 | loop fusion | flops 25165824 | bytes 67133440 | tf_op jit(solution)/shard_map/jit(_where)/select_n | solution.py:27
  71.8 30.1 %copy.46 = f32[512,8,4,512]{3,1,2,0:T(8,128)} copy(f32[512,8,4,512]{3,2,1,0:T(4,128)} %bitcast.80) | data formatting | bytes 67108864
  104.2 30.2 %all-to-all-done = f32[2,32,8,128,16]{3,4,2,0,1:T(8,128)} async-done(((f32[2,32,8,128,16]{3,4,2,0,1:T(8,128)}), f32[2,32,8,128,16]{3,4,2,0,1:T(8,128)}, u32[]{:S(2)}, u32[]{:S(2)}) %all-to-all-start) | async-done | bytes 4194336 | tf_op jit(solution)/shard_map/all_to_all | solution.py:50
  138.1 39.8 %reshape.284 = f32[4096,2048,1]{1,0,2:T(8,128)} reshape(f32[8,512,4,512]{3,2,1,0:T(4,128)} %fusion.6) | data formatting | bytes 67108864 | tf_op jit(solution)/shard_map/reshape | solution.py:27
  177.9 5.3 reshape.267
  183.1 4.7 copy.25
  192.5 19.5 %fusion.8 = f32[2,128,2048]{2,1,0:T(8,128)} fusion(f32[2,128,4096]{1,2,0:T(8,128)} %bitcast.81, f32[4096,2048,1]{1,0,2:T(8,128)} %reshape.284), kind=kOutput, calls=%fused_computation.25 | convolution fusion | flops 12884901888 | bytes 39845888 | tf_op jit(solution)/shard_map/iap,pq->iaq/dot_general | solution.py:53
  216.6 17.3 %all-to-all-done.1 = f32[2,32,8,128,16]{3,4,2,0,1:T(8,128)} async-done(((f32[2,32,8,128,16]{3,4,2,0,1:T(8,128)}), f32[2,32,8,128,16]{3,4,2,0,1:T(8,128)}, u32[]{:S(2)}, u32[]{:S(2)}) %all-to-all-start.1) | async-done | bytes 4194336 | tf_op jit(solution)/shard_map/all_to_all | solution.py:50
  238.2 5.3 reshape.274
  248.2 4.7 copy.33
  252.9 19.5 %fusion.4 = f32[2,128,2048]{2,1,0:T(8,128)} fusion(f32[2,128,4096]{1,2,0:T(8,128)} %bitcast.83, f32[4096,2048]{1,0:T(8,128)} %bitcast.77), kind=kOutput, calls=%fused_computation.4 | convolution fusion | flops 12884901888 | bytes 39845888 | tf_op jit(solution)/shard_map/iap,pq->iaq/dot_general | solution.py:53
  277.1 81.6 %all-to-all-done.2 = f32[2,32,8,128,16]{3,4,2,0,1:T(8,128)} async-done(((f32[2,32,8,128,16]{3,4,2,0,1:T(8,128)}), f32[2,32,8,128,16]{3,4,2,0,1:T(8,128)}, u32[]{:S(2)}, u32[]{:S(2)}) %all-to-all-start.2) | async-done | bytes 4194336 | tf_op jit(solution)/shard_map/all_to_all | solution.py:50
  367.8 19.5 %fusion.2 = f32[2,128,2048]{2,1,0:T(8,128)} fusion(f32[2,128,4096]{1,2,0:T(8,128)} %bitcast.84, f32[4096,2048]{1,0:T(8,128)} %bitcast.78), kind=kOutput, calls=%fused_computation.2 | convolution fusion | flops 12884901888 | bytes 39845888 | tf_op jit(solution)/shard_map/iap,pq->iaq/dot_general | solution.py:53
  387.4 96.1 %all-to-all-done.3 = f32[2,32,8,128,16]{3,4,2,0,1:T(8,128)} async-done(((f32[2,32,8,128,16]{3,4,2,0,1:T(8,128)}), f32[2,32,8,128,16]{3,4,2,0,1:T(8,128)}, u32[]{:S(2)}, u32[]{:S(2)}) %all-to-all-start.3) | async-done | bytes 4194336 | tf_op jit(solution)/shard_map/all_to_all | solution.py:50
  483.4 4.7 copy.39
  488.2 19.7 %fusion = f32[2,128,2048]{2,1,0:T(8,128)} fusion(f32[2,128,4096]{1,2,0:T(8,128)} %bitcast.82, f32[4096,2048]{1,0:T(8,128)} %bitcast.79), kind=kOutput, calls=%fused_computation | convolution fusion | flops 12884901888 | bytes 39845888 | tf_op jit(solution)/shard_map/iap,pq->iaq/dot_general | solution.py:53
  507.9 44.1 %reduce-scatter.9.cloned.1.call-done = f32[2,128,256]{2,1,0:T(8,128)} async-done(((f32[2,128,2048]{2,1,0:T(8,128)}), f32[2,128,256]{2,1,0:T(8,128)}) %reduce-scatter.9.cloned.1.call-update) | async-done | bytes 262160 | tf_op jit(solution)/shard_map/reduce_scatter | solution.py:61
  552.0 70.6 %reduce-scatter.11.cloned.1.call-done = f32[2,128,256]{2,1,0:T(8,128)} async-done(((f32[2,128,2048]{2,1,0:T(8,128)}), f32[2,128,256]{2,1,0:T(8,128)}) %reduce-scatter.11.cloned.1.call-update) | async-done | bytes 262160 | tf_op jit(solution)/shard_map/reduce_scatter | solution.py:61
  (33 shorter events, 43.8 us)
Async XLA Ops:
  30.9 7.4 %copy-start.2 = (s32[64]{0:T(128)S(1)}, s32[64]{0:T(128)}, u32[]{:S(2)}) copy-start(s32[64]{0:T(128)} %param.6) | copy-start | bytes 772
  30.9 103.4 %all-to-all-start = ((f32[2,32,8,128,16]{3,4,2,0,1:T(8,128)}), f32[2,32,8,128,16]{3,4,2,0,1:T(8,128)}, u32[]{:S(2)}, u32[]{:S(2)}) async-start(f32[2,32,8,128,16]{3,4,2,0,1:T(8,128)} %bitcast.85), calls=%async_computation | async-start | bytes 8388608 | tf_op jit(solution)/shard_map/all_to_all | solution.py:50
  43.7 4.8 copy-start.1
  71.8 30.1 %copy-start = (f32[2,4,8,8,128,16]{4,5,3,2,1,0:T(8,128)S(1)}, f32[2,4,8,8,128,16]{4,5,3,2,1,0:T(8,128)}, u32[]{:S(2)}) copy-start(f32[2,4,8,8,128,16]{4,5,3,2,1,0:T(8,128)} %copy.31) | copy-start | bytes 12582916
  134.3 99.5 %all-to-all-start.1 = ((f32[2,32,8,128,16]{3,4,2,0,1:T(8,128)}), f32[2,32,8,128,16]{3,4,2,0,1:T(8,128)}, u32[]{:S(2)}, u32[]{:S(2)}) async-start(f32[2,32,8,128,16]{3,4,2,0,1:T(8,128)} %copy.32), calls=%async_computation.2 | async-start | bytes 8388608 | tf_op jit(solution)/shard_map/all_to_all | solution.py:50
  233.9 124.8 %all-to-all-start.2 = ((f32[2,32,8,128,16]{3,4,2,0,1:T(8,128)}), f32[2,32,8,128,16]{3,4,2,0,1:T(8,128)}, u32[]{:S(2)}, u32[]{:S(2)}) async-start(f32[2,32,8,128,16]{3,4,2,0,1:T(8,128)} %copy.35), calls=%async_computation.4 | async-start | bytes 8388608 | tf_op jit(solution)/shard_map/all_to_all | solution.py:50
  237.5 270.4 %reduce-scatter.5.cloned.1.call-start = ((), (), s32[]{:S(2)}) async-start(), calls=%async_computation.8 | async-start | bytes 2359296 | tf_op jit(solution)/shard_map/reduce_scatter | solution.py:61
  358.7 124.8 %all-to-all-start.3 = ((f32[2,32,8,128,16]{3,4,2,0,1:T(8,128)}), f32[2,32,8,128,16]{3,4,2,0,1:T(8,128)}, u32[]{:S(2)}, u32[]{:S(2)}) async-start(f32[2,32,8,128,16]{3,4,2,0,1:T(8,128)} %copy.38), calls=%async_computation.6 | async-start | bytes 8388608 | tf_op jit(solution)/shard_map/all_to_all | solution.py:50
  362.2 145.7 %reduce-scatter.7.cloned.1.call-start = ((), (), s32[]{:S(2)}) async-start(), calls=%async_computation.9 | async-start | bytes 2359296 | tf_op jit(solution)/shard_map/reduce_scatter | solution.py:61
  363.0 189.0 %reduce-scatter.9.cloned.1.call-start = ((), (), s32[]{:S(2)}) async-start(), calls=%async_computation.10 | async-start | bytes 2359296 | tf_op jit(solution)/shard_map/reduce_scatter | solution.py:61
  387.3 235.3 %reduce-scatter.11.cloned.1.call-start = ((), (), s32[]{:S(2)}) async-start(), calls=%async_computation.11 | async-start | bytes 2359296 | tf_op jit(solution)/shard_map/reduce_scatter | solution.py:61
Sparse Core Ops, SparseCore 0:
  241.8 115.5 reduce-scatter.4
  366.6 115.5 reduce-scatter.6
  485.8 66.1 reduce-scatter.8
  555.4 67.1 reduce-scatter.10

commit v5 on v4

--- a/solution.py
+++ b/solution.py
@@ -2,6 +2,38 @@
 import jax.numpy as jnp
 from jax import lax
 from jax.sharding import PartitionSpec as P
+
+
+def scatter_sum(flat, col_count, col_place):
+    rows, a_local, width = flat.shape
+    shard = width // col_count
+    pairs_n = col_count // 2
+    side = col_place % 2
+    line = col_place // 2
+    parts = flat.reshape(rows, a_local, pairs_n, 2, shard)
+    keep = jnp.where(side == 0, parts[:, :, :, 0], parts[:, :, :, 1])
+    give = jnp.where(side == 0, parts[:, :, :, 1], parts[:, :, :, 0])
+    swap = [(q, q ^ 1) for q in range(col_count)]
+    line_sum = keep + lax.ppermute(give, "col", swap)
+    total = lax.dynamic_index_in_dim(line_sum, line, axis=2, keepdims=False)
+    up_prev = None
+    down_prev = None
+    for t in range(pairs_n - 1):
+        up_send = line_sum[:, :, t + 1:]
+        down_send = line_sum[:, :, :pairs_n - 1 - t]
+        if up_prev is not None:
+            up_send = up_send + up_prev[:, :, 1:]
+            down_send = down_send + down_prev[:, :, :-1]
+        payload = jnp.where(line == t, up_send, down_send)
+        links = []
+        for v in range(2):
+            links.append((2 * t + v, 2 * (t + 1) + v))
+            links.append((2 * (pairs_n - 1 - t) + v, 2 * (pairs_n - 2 - t) + v))
+        got = lax.ppermute(payload, "col", links)
+        up_prev = jnp.where(line == t + 1, got, 0.0)
+        down_prev = jnp.where(line == pairs_n - 2 - t, got, 0.0)
+        total = total + up_prev[:, :, 0] + down_prev[:, :, -1]
+    return total
 
 
 def per_device(amplitudes, cycle_integrals, occ_irrep, virt_irrep):
@@ -58,7 +90,10 @@
             preferred_element_type=jnp.float32,
         )
         partials.append(partial_value.reshape(rows, a_local, column_slab * virt_count))
-    results = [lax.psum_scatter(flat, "col", scatter_dimension=2, tiled=True) for flat in partials]
+    if col_count % 4 == 0:
+        results = [scatter_sum(flat, col_count, col_place) for flat in partials]
+    else:
+        results = [lax.psum_scatter(flat, "col", scatter_dimension=2, tiled=True) for flat in partials]
     return jnp.concatenate(results, axis=0)
 
 

time: 634 us -> 647 us (1.021); the launches traced: 631 us -> 635 us
  waiting for transfers between devices: 341 us -> 221 us
  local copies, waits for them, and re-layouts: 142 us -> 191 us
  starting transfers between devices: 18.7 us -> 58.8 us
  matrix products: 78.1 us -> 103 us
  other arithmetic: 38.1 us -> 60.6 us
  between operations: 13.2 us -> 0.8 us
    all_to_all x4, waiting for transfers between devices: 225 us -> 103 us  [per_device(): lax.all_to_all(grouped, ('row', 'col'), split_axis=1, concat_axis=4, tile...]
    ppermute x0 -> x16, waiting for transfers between devices: none -> 117 us  [the longest x4 77.4 us: scatter_sum(): line_sum = keep + lax.ppermute(give, 'col', swap)]
    reduce_scatter x4 -> x0, waiting for transfers between devices: 115 us -> none  [per_device(): lax.psum_scatter(flat, 'col', scatter_dimension=2, tiled=True)]
    ppermute x0 -> x16, starting transfers between devices: none -> 40.3 us  [the longest x12 35.8 us: scatter_sum(): got = lax.ppermute(payload, 'col', links)]
    dot_general x0 -> x1, local copies, waits for them, and re-layouts: none -> 31.2 us  [per_device(): jnp.einsum('iap,pq->iaq', blocks, masked_ints, precision=lax.Precision.HI...]
    dot_general x4, matrix products: 78.1 us -> 103 us  [per_device(): jnp.einsum('iap,pq->iaq', blocks, masked_ints, precision=lax.Precision.HI...]
    select_n x0 -> x23, other arithmetic: none -> 12.2 us  [the longest x12 4.64 us: scatter_sum(): payload = jnp.where(line == t, up_send, down_send)]
    slice x0 -> x4, local copies, waits for them, and re-layouts: none -> 8.22 us  [the longest x2 8.04 us: scatter_sum(): keep = jnp.where(side == 0, parts[:, :, :, 0], parts[:, :, :, 1])]
  transfers between devices with their start and end apart: 8 -> 20, of which waited for: 6 -> 10; matrix products, arithmetic and copies ran while one was open for 37% -> 51% of each run, Pallas kernels for 0% -> 0%
where the time goes in v5:
time: 647 us; the launch traced here: 635 us
  waiting for transfers between devices  221 us (34%)
  local copies, waits for them, and re-layouts  191 us (30%)
  matrix products  103 us (16%)
  other arithmetic  60.6 us (9%)
  starting transfers between devices  58.8 us (9%)
    all_to_all x4, waiting for transfers between devices, per_device(): lax.all_to_all(grouped, ('row', 'col'), split_axis=1, concat_axis=4, tile...  103 us
    dot_general x4, matrix products, per_device(): jnp.einsum('iap,pq->iaq', blocks, masked_ints, precision=lax.Precision.HI...  103 us
    ppermute x4, waiting for transfers between devices, scatter_sum(): line_sum = keep + lax.ppermute(give, 'col', swap)  77.4 us
    ppermute x12, waiting for transfers between devices, scatter_sum(): got = lax.ppermute(payload, 'col', links)  39.8 us
    reshape x1, local copies, waits for them, and re-layouts, per_device(): jnp.where(int_sym == 0, cycle_integrals, 0.0)  39.8 us
    ppermute x12, starting transfers between devices, scatter_sum(): got = lax.ppermute(payload, 'col', links)  35.8 us
    unnamed x37, local copies, waits for them, and re-layouts  33.9 us
    dot_general x1, local copies, waits for them, and re-layouts, per_device(): jnp.einsum('iap,pq->iaq', blocks, masked_ints, precision=lax.Precision.HI...  31.2 us
  transfers between devices with their start and end apart: 20, of which 10 were waited for; matrix products, arithmetic and copies ran while one was open for 51% of the time, Pallas kernels for 0%

profile of v5, /device:TPU:0, one launch (start us, length us, event | category | flops | bytes accessed | tf_op | source)
XLA Modules:
  0.0 635.1 jit_solution(8314287211141909948)
XLA Ops:
  3.1 11.3 %slice_select_fusion.2 = (f32[2,64,512,16]{2,3,1,0:T(8,128)}, f32[2,64,512,16]{2,3,1,0:T(8,128)}, f32[2,64,512,16]{2,3,1,0:T(8,128)}, f32[2,64,512,16]{2,3,1,0:T(8,128)}) fusion(f32[8,64,512,16]{2,3,1,0:T(8,128)} %param.4, s32[2,64]{1,0:T(2,128)S(1)} %get-tuple-element.48, s32[512,16]{0,1:T(8,128)S(1)} %broadcast_xor_fusion, ...), kind=kLoop, calls=%fused_computation.10 | loop fusion | flops 12582912 | bytes 33589248 | tf_op jit(solution)/shard_map/jit(_where)/select_n | solution.py:73
  24.5 7.4 %all-to-all-start = ((f32[2,32,8,128,16]{3,4,2,0,1:T(8,128)}), f32[2,32,8,128,16]{3,4,2,0,1:T(8,128)}, u32[]{:S(2)}, u32[]{:S(2)}) async-start(f32[2,32,8,128,16]{3,4,2,0,1:T(8,128)} %bitcast.153), calls=%async_computation | async-start | bytes 8388608 | tf_op jit(solution)/shard_map/all_to_all | solution.py:82
  42.3 23.1 %fusion.4 = f32[8,512,4,512]{3,2,1,0:T(4,128)} fusion(f32[8,512,4,512]{3,2,1,0:T(4,128)} %param.5, s32[4,512]{1,0:T(4,128)S(1)} %broadcast_xor_fusion.2, s32[8,512]{1,0:T(8,128)S(1)} %broadcast_xor_fusion.1), kind=kLoop, calls=%fused_computation.5 | loop fusion | flops 25165824 | bytes 67133440 | tf_op jit(solution)/shard_map/jit(_where)/select_n | solution.py:59
  65.4 30.1 %copy.162 = f32[512,8,4,512]{3,1,2,0:T(8,128)} copy(f32[512,8,4,512]{3,2,1,0:T(4,128)} %bitcast.146) | data formatting | bytes 67108864
  97.9 30.0 %all-to-all-done = f32[2,32,8,128,16]{3,4,2,0,1:T(8,128)} async-done(((f32[2,32,8,128,16]{3,4,2,0,1:T(8,128)}), f32[2,32,8,128,16]{3,4,2,0,1:T(8,128)}, u32[]{:S(2)}, u32[]{:S(2)}) %all-to-all-start) | async-done | bytes 4194336 | tf_op jit(solution)/shard_map/all_to_all | solution.py:82
  131.5 39.8 %reshape.336 = f32[4096,2048,1]{1,0,2:T(8,128)} reshape(f32[8,512,4,512]{3,2,1,0:T(4,128)} %fusion.4) | data formatting | bytes 67108864 | tf_op jit(solution)/shard_map/reshape | solution.py:59
  186.0 18.5 %fusion.35 = f32[2,128,2048]{2,1,0:T(8,128)S(1)} fusion(f32[2,128,4096]{1,2,0:T(8,128)} %bitcast.149, f32[4096,2048,1]{1,0,2:T(8,128)} %reshape.336), kind=kOutput, calls=%fused_computation.116 | convolution fusion | flops 12884901888 | bytes 39845888 | tf_op jit(solution)/shard_map/iap,pq->iaq/dot_general | solution.py:85
  209.2 18.3 %all-to-all-done.1 = f32[2,32,8,128,16]{3,4,2,0,1:T(8,128)} async-done(((f32[2,32,8,128,16]{3,4,2,0,1:T(8,128)}), f32[2,32,8,128,16]{3,4,2,0,1:T(8,128)}, u32[]{:S(2)}, u32[]{:S(2)}) %all-to-all-start.1) | async-done | bytes 4194336 | tf_op jit(solution)/shard_map/all_to_all | solution.py:82
  231.4 5.3 reshape.317
  249.0 18.5 %fusion = f32[2,128,2048]{2,1,0:T(8,128)S(1)} fusion(f32[2,128,4096]{1,2,0:T(8,128)} %bitcast.150, f32[4096,2048]{1,0:T(8,128)} %bitcast.144), kind=kOutput, calls=%fused_computation | convolution fusion | flops 12884901888 | bytes 39845888 | tf_op jit(solution)/shard_map/iap,pq->iaq/dot_general | solution.py:85
  272.2 55.1 %all-to-all-done.2 = f32[2,32,8,128,16]{3,4,2,0,1:T(8,128)} async-done(((f32[2,32,8,128,16]{3,4,2,0,1:T(8,128)}), f32[2,32,8,128,16]{3,4,2,0,1:T(8,128)}, u32[]{:S(2)}, u32[]{:S(2)}) %all-to-all-start.2) | async-done | bytes 4194336 | tf_op jit(solution)/shard_map/all_to_all | solution.py:82
  348.3 50.4 %collective-permute-done = f32[2,128,4,256]{3,1,0,2:T(8,128)} collective-permute-done((f32[2,128,4,256]{3,1,0,2:T(8,128)}, f32[2,128,4,256]{3,1,0,2:T(8,128)}, u32[]{:S(2)}, u32[]{:S(2)}) %collective-permute-start) | collective-permute-done | bytes 1048608 | tf_op jit(solution)/shard_map/ppermute | solution.py:17
  403.8 17.0 %collective-permute-done.4 = f32[2,128,4,256]{3,1,0,2:T(8,128)} collective-permute-done((f32[2,128,4,256]{3,1,0,2:T(8,128)}, f32[2,128,4,256]{3,1,0,2:T(8,128)}, u32[]{:S(2)}, u32[]{:S(2)}) %collective-permute-start.4) | collective-permute-done | bytes 1048608 | tf_op jit(solution)/shard_map/ppermute | solution.py:17
  422.5 6.9 %collective-permute-start.5 = (f32[2,128,3,256]{3,1,0,2:T(8,128)S(1)}, f32[2,128,3,256]{3,1,0,2:T(8,128)}, u32[]{:S(2)}, u32[]{:S(2)}) collective-permute-start(f32[2,128,3,256]{3,1,0,2:T(8,128)S(1)} %slice_select_fusion.5), channel_id=1, source_target_pairs={{0,2},{6,4},{1,3},{7,5},{8,10},{14,12},{9,11},{15,13},{16,18},{22,... | collective-permute-start | bytes 2359304 | tf_op jit(solution)/shard_map/ppermute | solution.py:32
  432.5 10.8 %collective-permute-done.5 = f32[2,128,3,256]{3,1,0,2:T(8,128)} collective-permute-done((f32[2,128,3,256]{3,1,0,2:T(8,128)S(1)}, f32[2,128,3,256]{3,1,0,2:T(8,128)}, u32[]{:S(2)}, u32[]{:S(2)}) %collective-permute-start.5) | collective-permute-done | bytes 786464 | tf_op jit(solution)/shard_map/ppermute | solution.py:32
  447.1 31.2 %copy.117 = f32[2048,4096]{1,0:T(8,128)} copy(f32[2048,4096]{0,1:T(8,128)} %bitcast.145) | data formatting | bytes 67108864 | tf_op jit(solution)/shard_map/iap,pq->iaq/dot_general | solution.py:85
  487.8 33.7 %fusion.36 = f32[2,128,4,2,256]{4,1,3,2,0:T(8,128)} fusion(f32[2,128,4096,1,1]{1,2,4,3,0:T(8,128)} %bitcast.152, f32[4,2,256,4096,1]{3,2,1,0,4:T(8,128)} %bitcast.147), kind=kOutput, calls=%fused_computation.117 | convolution fusion | flops 12884901888 | bytes 39845888 | tf_op jit(solution)/shard_map/iap,pq->iaq/dot_general | solution.py:85
  531.9 32.5 %fusion.2 = f32[2,128,4,2,256]{4,1,0,2,3:T(8,128)} fusion(f32[2,128,4096,1,1]{1,2,0,3,4:T(8,128)} %bitcast.151, f32[4,2,256,4096,1]{3,2,1,0,4:T(8,128)} %bitcast.148), kind=kOutput, calls=%fused_computation.2 | convolution fusion | flops 12884901888 | bytes 39845888 | tf_op jit(solution)/shard_map/iap,pq->iaq/dot_general | solution.py:85
  569.4 10.2 %collective-permute-start.9 = (f32[2,128,3,256]{3,1,0,2:T(8,128)S(1)}, f32[2,128,3,256]{3,1,0,2:T(8,128)S(1)}, u32[]{:S(2)}, u32[]{:S(2)}) collective-permute-start(f32[2,128,3,256]{3,1,0,2:T(8,128)S(1)} %copy_select_fusion.1), channel_id=1, source_target_pairs={{0,2},{6,4},{1,3},{7,5},{8,10},{14,12},{9,11},{15,13},{16,18},{22,... | collective-permute-start | bytes 2359304 | tf_op jit(solution)/shard_map/ppermute | solution.py:32
  579.7 10.0 %collective-permute-done.12 = f32[2,128,4,256]{3,1,0,2:T(8,128)S(1)} collective-permute-done((f32[2,128,4,256]{3,1,0,2:T(8,128)S(1)}, f32[2,128,4,256]{3,1,0,2:T(8,128)S(1)}, u32[]{:S(2)}, u32[]{:S(2)}) %collective-permute-start.12) | collective-permute-done | bytes 1048608 | tf_op jit(solution)/shard_map/ppermute | solution.py:17
  590.0 8.3 %collective-permute-start.13 = (f32[2,128,3,256]{3,1,0,2:T(8,128)S(1)}, f32[2,128,3,256]{3,1,0,2:T(8,128)S(1)}, u32[]{:S(2)}, u32[]{:S(2)}) collective-permute-start(f32[2,128,3,256]{3,1,0,2:T(8,128)S(1)} %slice_select_fusion.4), channel_id=1, source_target_pairs={{0,2},{6,4},{1,3},{7,5},{8,10},{14,12},{9,11},{15,13},{16,18},{22,... | collective-permute-start | bytes 2359304 | tf_op jit(solution)/shard_map/ppermute | solution.py:32
  599.5 13.3 %collective-permute-done.13 = f32[2,128,3,256]{3,1,0,2:T(8,128)S(1)} collective-permute-done((f32[2,128,3,256]{3,1,0,2:T(8,128)S(1)}, f32[2,128,3,256]{3,1,0,2:T(8,128)S(1)}, u32[]{:S(2)}, u32[]{:S(2)}) %collective-permute-start.13) | collective-permute-done | bytes 786464 | tf_op jit(solution)/shard_map/ppermute | solution.py:32
  618.0 6.8 %collective-permute-done.11 = f32[2,128,1,256]{3,1,2,0:T(8,128)S(1)} collective-permute-done((f32[2,128,1,256]{3,1,2,0:T(8,128)S(1)}, f32[2,128,1,256]{3,1,2,0:T(8,128)S(1)}, u32[]{:S(2)}, u32[]{:S(2)}) %collective-permute-start.11) | collective-permute-done | bytes 262176 | tf_op jit(solution)/shard_map/ppermute | solution.py:32
  624.9 8.8 %collective-permute-done.15 = f32[2,128,1,256]{3,1,0,2:T(8,128)S(1)} collective-permute-done((f32[2,128,1,256]{3,1,0,2:T(8,128)S(1)}, f32[2,128,1,256]{3,1,0,2:T(8,128)S(1)}, u32[]{:S(2)}, u32[]{:S(2)}) %collective-permute-start.15) | collective-permute-done | bytes 262176 | tf_op jit(solution)/shard_map/ppermute | solution.py:32
  (122 shorter events, 136.9 us)
Async XLA Ops:
  24.5 103.4 %all-to-all-start = ((f32[2,32,8,128,16]{3,4,2,0,1:T(8,128)}), f32[2,32,8,128,16]{3,4,2,0,1:T(8,128)}, u32[]{:S(2)}, u32[]{:S(2)}) async-start(f32[2,32,8,128,16]{3,4,2,0,1:T(8,128)} %bitcast.153), calls=%async_computation | async-start | bytes 8388608 | tf_op jit(solution)/shard_map/all_to_all | solution.py:82
  65.4 30.1 %copy-start.1 = (f32[2,4,8,8,128,16]{4,5,3,2,1,0:T(8,128)S(1)}, f32[2,4,8,8,128,16]{4,5,3,2,1,0:T(8,128)}, u32[]{:S(2)}) copy-start(f32[2,4,8,8,128,16]{4,5,3,2,1,0:T(8,128)} %copy.108) | copy-start | bytes 12582916
  127.9 99.5 %all-to-all-start.1 = ((f32[2,32,8,128,16]{3,4,2,0,1:T(8,128)}), f32[2,32,8,128,16]{3,4,2,0,1:T(8,128)}, u32[]{:S(2)}, u32[]{:S(2)}) async-start(f32[2,32,8,128,16]{3,4,2,0,1:T(8,128)} %copy.109), calls=%async_computation.1 | async-start | bytes 8388608 | tf_op jit(solution)/shard_map/all_to_all | solution.py:82
  227.4 99.9 %all-to-all-start.2 = ((f32[2,32,8,128,16]{3,4,2,0,1:T(8,128)}), f32[2,32,8,128,16]{3,4,2,0,1:T(8,128)}, u32[]{:S(2)}, u32[]{:S(2)}) async-start(f32[2,32,8,128,16]{3,4,2,0,1:T(8,128)} %copy.114), calls=%async_computation.2 | async-start | bytes 8388608 | tf_op jit(solution)/shard_map/all_to_all | solution.py:82
  327.3 199.9 %all-to-all-start.3 = ((f32[2,32,8,128,16]{3,4,2,0,1:T(8,128)}), f32[2,32,8,128,16]{3,4,2,0,1:T(8,128)}, u32[]{:S(2)}, u32[]{:S(2)}) async-start(f32[2,32,8,128,16]{3,4,2,0,1:T(8,128)} %copy.136), calls=%async_computation.3 | async-start | bytes 8388608 | tf_op jit(solution)/shard_map/all_to_all | solution.py:82
  337.3 61.5 %collective-permute-start = (f32[2,128,4,256]{3,1,0,2:T(8,128)}, f32[2,128,4,256]{3,1,0,2:T(8,128)}, u32[]{:S(2)}, u32[]{:S(2)}) collective-permute-start(f32[2,128,4,256]{3,1,0,2:T(8,128)} %select_bitcast_fusion.3), channel_id=1, source_target_pairs={{0,1},{1,0},{2,3},{3,2},{4,5},{5,4},{6,7},{7,6},{8,9},{9,8},{10,11... | collective-permute-start | bytes 3145736 | tf_op jit(solution)/shard_map/ppermute | solution.py:17
  347.9 72.9 %collective-permute-start.4 = (f32[2,128,4,256]{3,1,0,2:T(8,128)}, f32[2,128,4,256]{3,1,0,2:T(8,128)}, u32[]{:S(2)}, u32[]{:S(2)}) collective-permute-start(f32[2,128,4,256]{3,1,0,2:T(8,128)} %select_bitcast_fusion.2), channel_id=1, source_target_pairs={{0,1},{1,0},{2,3},{3,2},{4,5},{5,4},{6,7},{7,6},{8,9},{9,8},{10,11... | collective-permute-start | bytes 3145736 | tf_op jit(solution)/shard_map/ppermute | solution.py:17
  348.3 72.4 %copy-start.3 = (f32[2,128,4,1,256]{4,3,2,1,0:T(1,128)S(1)}, f32[2,128,4,1,256]{4,3,2,1,0:T(1,128)}, u32[]{:S(2)}) copy-start(f32[2,128,4,1,256]{4,3,2,1,0:T(1,128)} %copy-done.2) | copy-start | bytes 3145732
  401.6 27.7 %collective-permute-start.1 = (f32[2,128,3,256]{3,1,0,2:T(8,128)}, f32[2,128,3,256]{3,1,0,2:T(8,128)}, u32[]{:S(2)}, u32[]{:S(2)}) collective-permute-start(f32[2,128,3,256]{3,1,0,2:T(8,128)} %slice_select_fusion.6), channel_id=1, source_target_pairs={{0,2},{6,4},{1,3},{7,5},{8,10},{14,12},{9,11},{15,13},{16,18},{22,... | collective-permute-start | bytes 2359304 | tf_op jit(solution)/shard_map/ppermute | solution.py:32
  422.5 20.8 %collective-permute-start.5 = (f32[2,128,3,256]{3,1,0,2:T(8,128)S(1)}, f32[2,128,3,256]{3,1,0,2:T(8,128)}, u32[]{:S(2)}, u32[]{:S(2)}) collective-permute-start(f32[2,128,3,256]{3,1,0,2:T(8,128)S(1)} %slice_select_fusion.5), channel_id=1, source_target_pairs={{0,2},{6,4},{1,3},{7,5},{8,10},{14,12},{9,11},{15,13},{16,18},{22,... | collective-permute-start | bytes 2359304 | tf_op jit(solution)/shard_map/ppermute | solution.py:32
  431.8 46.5 %collective-permute-start.2 = (f32[2,128,2,256]{3,1,0,2:T(8,128)}, f32[2,128,2,256]{3,1,0,2:T(8,128)S(1)}, u32[]{:S(2)}, u32[]{:S(2)}) collective-permute-start(f32[2,128,2,256]{3,1,0,2:T(8,128)} %fusion.9), channel_id=1, source_target_pairs={{2,4},{4,2},{3,5},{5,3},{10,12},{12,10},{11,13},{13,11},{18,20},{2... | collective-permute-start | bytes 1572872 | tf_op jit(solution)/shard_map/ppermute | solution.py:32
  446.4 34.2 %collective-permute-start.6 = (f32[2,128,2,256]{3,1,0,2:T(8,128)}, f32[2,128,2,256]{3,1,0,2:T(8,128)S(1)}, u32[]{:S(2)}, u32[]{:S(2)}) collective-permute-start(f32[2,128,2,256]{3,1,0,2:T(8,128)} %fusion.8), channel_id=1, source_target_pairs={{2,4},{4,2},{3,5},{5,3},{10,12},{12,10},{11,13},{13,11},{18,20},{2... | collective-permute-start | bytes 1572872 | tf_op jit(solution)/shard_map/ppermute | solution.py:32
  479.3 86.9 %collective-permute-start.3 = (f32[2,128,1,256]{3,1,0,2:T(8,128)}, f32[2,128,1,256]{3,1,0,2:T(8,128)}, u32[]{:S(2)}, u32[]{:S(2)}) collective-permute-start(f32[2,128,1,256]{3,1,0,2:T(8,128)} %fusion.25), channel_id=1, source_target_pairs={{4,6},{2,0},{5,7},{3,1},{12,14},{10,8},{13,15},{11,9},{20,22},{18,... | collective-permute-start | bytes 786440 | tf_op jit(solution)/shard_map/ppermute | solution.py:32
  481.7 132.1 %collective-permute-start.7 = (f32[2,128,1,256]{3,1,0,2:T(8,128)S(1)}, f32[2,128,1,256]{3,1,0,2:T(8,128)}, u32[]{:S(2)}, u32[]{:S(2)}) collective-permute-start(f32[2,128,1,256]{3,1,0,2:T(8,128)S(1)} %fusion.21), channel_id=1, source_target_pairs={{4,6},{2,0},{5,7},{3,1},{12,14},{10,8},{13,15},{11,9},{20,22},{18,... | collective-permute-start | bytes 786440 | tf_op jit(solution)/shard_map/ppermute | solution.py:32
  524.7 42.9 %collective-permute-start.8 = (f32[2,128,4,256]{3,1,2,0:T(8,128)}, f32[2,128,4,256]{3,1,2,0:T(8,128)}, u32[]{:S(2)}, u32[]{:S(2)}) collective-permute-start(f32[2,128,4,256]{3,1,2,0:T(8,128)} %get-tuple-element.26), channel_id=1, source_target_pairs={{0,1},{1,0},{2,3},{3,2},{4,5},{5,4},{6,7},{7,6},{8,9},{9,8},{10,11... | collective-permute-start | bytes 3145736 | tf_op jit(solution)/shard_map/ppermute | solution.py:17
  566.1 23.6 %collective-permute-start.12 = (f32[2,128,4,256]{3,1,0,2:T(8,128)S(1)}, f32[2,128,4,256]{3,1,0,2:T(8,128)S(1)}, u32[]{:S(2)}, u32[]{:S(2)}) collective-permute-start(f32[2,128,4,256]{3,1,0,2:T(8,128)S(1)} %select_bitcast_fusion), channel_id=1, source_target_pairs={{0,1},{1,0},{2,3},{3,2},{4,5},{5,4},{6,7},{7,6},{8,9},{9,8},{10,11... | collective-permute-start | bytes 3145736 | tf_op jit(solution)/shard_map/ppermute | solution.py:17
  567.6 22.1 %copy-start = (f32[2,128,4,2,256]{4,1,0,2,3:T(8,128)S(1)}, f32[2,128,4,2,256]{4,1,0,2,3:T(8,128)}, u32[]{:S(2)}) copy-start(f32[2,128,4,2,256]{4,1,0,2,3:T(8,128)} %fusion.2) | copy-start | bytes 6291460
  569.4 29.0 %collective-permute-start.9 = (f32[2,128,3,256]{3,1,0,2:T(8,128)S(1)}, f32[2,128,3,256]{3,1,0,2:T(8,128)S(1)}, u32[]{:S(2)}, u32[]{:S(2)}) collective-permute-start(f32[2,128,3,256]{3,1,0,2:T(8,128)S(1)} %copy_select_fusion.1), channel_id=1, source_target_pairs={{0,2},{6,4},{1,3},{7,5},{8,10},{14,12},{9,11},{15,13},{16,18},{22,... | collective-permute-start | bytes 2359304 | tf_op jit(solution)/shard_map/ppermute | solution.py:32
  590.0 22.8 %collective-permute-start.13 = (f32[2,128,3,256]{3,1,0,2:T(8,128)S(1)}, f32[2,128,3,256]{3,1,0,2:T(8,128)S(1)}, u32[]{:S(2)}, u32[]{:S(2)}) collective-permute-start(f32[2,128,3,256]{3,1,0,2:T(8,128)S(1)} %slice_select_fusion.4), channel_id=1, source_target_pairs={{0,2},{6,4},{1,3},{7,5},{8,10},{14,12},{9,11},{15,13},{16,18},{22,... | collective-permute-start | bytes 2359304 | tf_op jit(solution)/shard_map/ppermute | solution.py:32
  598.5 15.3 %copy-start.11 = (f32[2,128,2,256]{3,1,0,2:T(8,128)S(1)}, f32[2,128,2,256]{3,1,0,2:T(8,128)}, u32[]{:S(2)}) copy-start(f32[2,128,2,256]{3,1,0,2:T(8,128)} %copy-done.10) | copy-start | bytes 1572868
  598.7 16.3 %collective-permute-start.10 = (f32[2,128,2,256]{3,1,0,2:T(8,128)S(1)}, f32[2,128,2,256]{3,1,0,2:T(8,128)S(1)}, u32[]{:S(2)}, u32[]{:S(2)}) collective-permute-start(f32[2,128,2,256]{3,1,0,2:T(8,128)S(1)} %fusion.7), channel_id=1, source_target_pairs={{2,4},{4,2},{3,5},{5,3},{10,12},{12,10},{11,13},{13,11},{18,20},{2... | collective-permute-start | bytes 1572872 | tf_op jit(solution)/shard_map/ppermute | solution.py:32
  613.1 3.4 collective-permute-start.14
  615.2 9.6 %collective-permute-start.11 = (f32[2,128,1,256]{3,1,2,0:T(8,128)S(1)}, f32[2,128,1,256]{3,1,2,0:T(8,128)S(1)}, u32[]{:S(2)}, u32[]{:S(2)}) collective-permute-start(f32[2,128,1,256]{3,1,2,0:T(8,128)S(1)} %fusion.15), channel_id=1, source_target_pairs={{4,6},{2,0},{5,7},{3,1},{12,14},{10,8},{13,15},{11,9},{20,22},{18,... | collective-permute-start | bytes 786440 | tf_op jit(solution)/shard_map/ppermute | solution.py:32
  616.7 17.0 %collective-permute-start.15 = (f32[2,128,1,256]{3,1,0,2:T(8,128)S(1)}, f32[2,128,1,256]{3,1,0,2:T(8,128)S(1)}, u32[]{:S(2)}, u32[]{:S(2)}) collective-permute-start(f32[2,128,1,256]{3,1,0,2:T(8,128)S(1)} %fusion.10), channel_id=1, source_target_pairs={{4,6},{2,0},{5,7},{3,1},{12,14},{10,8},{13,15},{11,9},{20,22},{18,... | collective-permute-start | bytes 786440 | tf_op jit(solution)/shard_map/ppermute | solution.py:32
  (14 other events, 45.3 us)

commit v6 on v5

--- a/solution.py
+++ b/solution.py
@@ -62,7 +62,7 @@
 
     chunks = 4 if slab_rows % 4 == 0 else 1
     rows = slab_rows // chunks
-    partials = []
+    results = []
     for step in range(chunks):
         amps = amplitudes[step * rows:(step + 1) * rows]
         amp_sym = (
@@ -78,7 +78,7 @@
         if step == 1:
             grouped, masked_ints = lax.optimization_barrier((grouped, masked_ints))
         if step >= 2:
-            grouped, partials[step - 2] = lax.optimization_barrier((grouped, partials[step - 2]))
+            grouped, results[step - 2] = lax.optimization_barrier((grouped, results[step - 2]))
         items = lax.all_to_all(grouped, ("row", "col"), split_axis=1, concat_axis=4, tiled=True)
         blocks = jnp.transpose(items.reshape(rows, k_local, a_local, virt_count), (0, 2, 1, 3))
         blocks = blocks.reshape(rows, a_local, k_local * virt_count)
@@ -89,11 +89,11 @@
             precision=lax.Precision.HIGH,
             preferred_element_type=jnp.float32,
         )
-        partials.append(partial_value.reshape(rows, a_local, column_slab * virt_count))
-    if col_count % 4 == 0:
-        results = [scatter_sum(flat, col_count, col_place) for flat in partials]
-    else:
-        results = [lax.psum_scatter(flat, "col", scatter_dimension=2, tiled=True) for flat in partials]
+        flat = partial_value.reshape(rows, a_local, column_slab * virt_count)
+        if col_count % 4 == 0:
+            results.append(scatter_sum(flat, col_count, col_place))
+        else:
+            results.append(lax.psum_scatter(flat, "col", scatter_dimension=2, tiled=True))
     return jnp.concatenate(results, axis=0)
 
 

time: 647 us -> 665 us (1.028)
  waiting for transfers between devices: 221 us -> 271 us
  local copies, waits for them, and re-layouts: 191 us -> 160 us
  matrix products: 103 us -> 127 us
  other arithmetic: 60.6 us -> 49.8 us
  starting transfers between devices: 58.8 us -> 50 us
    ppermute x12, waiting for transfers between devices: 39.8 us -> 91.4 us  [scatter_sum(): got = lax.ppermute(payload, 'col', links)]
    reshape x3 -> x0, local copies, waits for them, and re-layouts: 45.3 us -> none  [the longest x1 39.8 us: per_device(): jnp.where(int_sym == 0, cycle_integrals, 0.0)]
    dot_general x1 -> x2, local copies, waits for them, and re-layouts: 31.2 us -> 62.3 us  [per_device(): jnp.einsum('iap,pq->iaq', blocks, masked_ints, precision=lax.Precision.HI...]
    dot_general x4, matrix products: 103 us -> 127 us  [per_device(): jnp.einsum('iap,pq->iaq', blocks, masked_ints, precision=lax.Precision.HI...]
    ppermute x12, starting transfers between devices: 35.8 us -> 19 us  [scatter_sum(): got = lax.ppermute(payload, 'col', links)]
    all_to_all x4, waiting for transfers between devices: 103 us -> 89.1 us  [per_device(): lax.all_to_all(grouped, ('row', 'col'), split_axis=1, concat_axis=4, tile...]
    ppermute x4, waiting for transfers between devices: 77.4 us -> 90.6 us  [scatter_sum(): line_sum = keep + lax.ppermute(give, 'col', swap)]
    slice x2 -> x0, local copies, waits for them, and re-layouts: 8.04 us -> none  [scatter_sum(): keep = jnp.where(side == 0, parts[:, :, :, 0], parts[:, :, :, 1])]
  transfers between devices with their start and end apart: 20 -> 20, of which waited for: 10 -> 12; matrix products, arithmetic and copies ran while one was open for 51% -> 47% of each run, Pallas kernels for 0% -> 0%
where the time goes in v6:
time: 665 us; the launch traced here: 658 us
  waiting for transfers between devices  271 us (41%)
  local copies, waits for them, and re-layouts  160 us (24%)
  matrix products  127 us (19%)
  starting transfers between devices  50 us (8%)
  other arithmetic  49.8 us (7%)
    dot_general x4, matrix products, per_device(): jnp.einsum('iap,pq->iaq', blocks, masked_ints, precision=lax.Precision.HI...  127 us
    ppermute x12, waiting for transfers between devices, scatter_sum(): got = lax.ppermute(payload, 'col', links)  91.4 us
    ppermute x4, waiting for transfers between devices, scatter_sum(): line_sum = keep + lax.ppermute(give, 'col', swap)  90.6 us
    all_to_all x4, waiting for transfers between devices, per_device(): lax.all_to_all(grouped, ('row', 'col'), split_axis=1, concat_axis=4, tile...  89.1 us
    dot_general x2, local copies, waits for them, and re-layouts, per_device(): jnp.einsum('iap,pq->iaq', blocks, masked_ints, precision=lax.Precision.HI...  62.3 us
    unnamed x15, local copies, waits for them, and re-layouts  31.6 us
    all_to_all x4, starting transfers between devices, per_device(): lax.all_to_all(grouped, ('row', 'col'), split_axis=1, concat_axis=4, tile...  25.3 us
    select_n x1, other arithmetic, per_device(): jnp.where(int_sym == 0, cycle_integrals, 0.0)  23.1 us
  transfers between devices with their start and end apart: 20, of which 12 were waited for; matrix products, arithmetic and copies ran while one was open for 47% of the time, Pallas kernels for 0%

profile of v6, /device:TPU:0, one launch (start us, length us, event | category | flops | bytes accessed | tf_op | source)
XLA Modules:
  0.0 658.1 jit_solution(1569458670281027746)
XLA Ops:
  3.1 11.3 %slice_select_fusion.2 = (f32[2,64,512,16]{2,3,1,0:T(8,128)}, f32[2,64,512,16]{2,3,1,0:T(8,128)}, f32[2,64,512,16]{2,3,1,0:T(8,128)}, f32[2,64,512,16]{2,3,1,0:T(8,128)}) fusion(f32[8,64,512,16]{2,3,1,0:T(8,128)} %param.4, s32[2,64]{1,0:T(2,128)S(1)} %get-tuple-element.44, s32[512,16]{0,1:T(8,128)S(1)} %broadcast_xor_fusion, ...), kind=kLoop, calls=%fused_computation.12 | loop fusion | flops 12582912 | bytes 33589248 | tf_op jit(solution)/shard_map/jit(_where)/select_n | solution.py:73
  24.4 7.4 %all-to-all-start = ((f32[2,32,8,128,16]{3,4,2,0,1:T(8,128)}), f32[2,32,8,128,16]{3,4,2,0,1:T(8,128)}, u32[]{:S(2)}, u32[]{:S(2)}) async-start(f32[2,32,8,128,16]{3,4,2,0,1:T(8,128)} %bitcast.162), calls=%async_computation | async-start | bytes 8388608 | tf_op jit(solution)/shard_map/all_to_all | solution.py:82
  32.1 23.1 %fusion = f32[8,512,4,512]{3,2,1,0:T(4,128)} fusion(f32[8,512,4,512]{3,2,1,0:T(4,128)} %param.5, s32[4,512]{1,0:T(4,128)S(1)} %broadcast_xor_fusion.2, s32[8,512]{1,0:T(8,128)S(1)} %broadcast_xor_fusion.1), kind=kLoop, calls=%fused_computation.1 | loop fusion | flops 25165824 | bytes 67133440 | tf_op jit(solution)/shard_map/jit(_where)/select_n | solution.py:59
  55.2 30.0 %copy.164 = f32[512,8,4,512]{3,1,2,0:T(8,128)} copy(f32[512,8,4,512]{3,2,1,0:T(4,128)} %bitcast.156) | data formatting | bytes 67108864
  95.4 32.4 %all-to-all-done = f32[2,32,8,128,16]{3,4,2,0,1:T(8,128)} async-done(((f32[2,32,8,128,16]{3,4,2,0,1:T(8,128)}), f32[2,32,8,128,16]{3,4,2,0,1:T(8,128)}, u32[]{:S(2)}, u32[]{:S(2)}) %all-to-all-start) | async-done | bytes 4194336 | tf_op jit(solution)/shard_map/all_to_all | solution.py:82
  131.6 31.1 %copy.108 = f32[2048,4096]{1,0:T(8,128)} copy(f32[2048,4096]{0,1:T(8,128)} %bitcast.154) | data formatting | bytes 67108864 | tf_op jit(solution)/shard_map/iap,pq->iaq/dot_general | solution.py:85
  167.3 31.5 %fusion.35 = f32[2,128,4,2,256]{4,1,3,2,0:T(8,128)S(1)} fusion(f32[2,128,4096,1,1]{1,2,4,3,0:T(8,128)} %bitcast.158, f32[4,2,256,4096,1]{3,2,1,0,4:T(8,128)} %bitcast.157), kind=kOutput, calls=%fused_computation.116 | convolution fusion | flops 12884901888 | bytes 39845888 | tf_op jit(solution)/shard_map/iap,pq->iaq/dot_general | solution.py:85
  202.3 33.5 %collective-permute-done = f32[2,128,4,256]{3,1,2,0:T(8,128)S(1)} collective-permute-done((f32[2,128,4,256]{3,1,2,0:T(8,128)}, f32[2,128,4,256]{3,1,2,0:T(8,128)S(1)}, u32[]{:S(2)}, u32[]{:S(2)}) %collective-permute-start) | collective-permute-done | bytes 1048608 | tf_op jit(solution)/shard_map/ppermute | solution.py:17
  241.5 16.9 %collective-permute-done.1 = f32[2,128,3,256]{3,1,0,2:T(8,128)S(1)} collective-permute-done((f32[2,128,3,256]{3,1,0,2:T(8,128)S(1)}, f32[2,128,3,256]{3,1,0,2:T(8,128)S(1)}, u32[]{:S(2)}, u32[]{:S(2)}) %collective-permute-start.1) | collective-permute-done | bytes 786464 | tf_op jit(solution)/shard_map/ppermute | solution.py:32
  271.6 11.5 %collective-permute-done.3 = f32[2,128,1,256]{3,1,2,0:T(8,128)} collective-permute-done((f32[2,128,1,256]{3,1,2,0:T(8,128)S(1)}, f32[2,128,1,256]{3,1,2,0:T(8,128)}, u32[]{:S(2)}, u32[]{:S(2)}) %collective-permute-start.3) | collective-permute-done | bytes 262176 | tf_op jit(solution)/shard_map/ppermute | solution.py:32
  288.9 7.3 %all-to-all-start.2 = ((f32[2,32,8,128,16]{3,4,2,0,1:T(8,128)}), f32[2,32,8,128,16]{3,4,2,0,1:T(8,128)}, u32[]{:S(2)}, u32[]{:S(2)}) async-start(f32[2,32,8,128,16]{3,4,2,0,1:T(8,128)} %copy.135), calls=%async_computation.2 | async-start | bytes 8388608 | tf_op jit(solution)/shard_map/all_to_all | solution.py:82
  296.3 31.1 %copy.132 = f32[2048,4096]{1,0:T(8,128)} copy(f32[2048,4096]{0,1:T(8,128)} %bitcast.155) | data formatting | bytes 67108864 | tf_op jit(solution)/shard_map/iap,pq->iaq/dot_general | solution.py:85
  332.0 31.5 %fusion.5 = f32[2,128,4,2,256]{4,1,0,2,3:T(8,128)S(1)} fusion(f32[2,128,4096,1,1]{1,2,0,3,4:T(8,128)} %bitcast.160, f32[4,2,256,4096,1]{3,2,1,0,4:T(8,128)} %bitcast.151), kind=kOutput, calls=%fused_computation.6 | convolution fusion | flops 12884901888 | bytes 39845888 | tf_op jit(solution)/shard_map/iap,pq->iaq/dot_general | solution.py:85
  365.6 34.0 %collective-permute-done.4 = f32[2,128,4,256]{3,1,0,2:T(8,128)S(1)} collective-permute-done((f32[2,128,4,256]{3,1,0,2:T(8,128)S(1)}, f32[2,128,4,256]{3,1,0,2:T(8,128)S(1)}, u32[]{:S(2)}, u32[]{:S(2)}) %collective-permute-start.4) | collective-permute-done | bytes 1048608 | tf_op jit(solution)/shard_map/ppermute | solution.py:17
  404.3 16.6 %collective-permute-done.5 = f32[2,128,3,256]{3,1,0,2:T(8,128)S(1)} collective-permute-done((f32[2,128,3,256]{3,1,0,2:T(8,128)S(1)}, f32[2,128,3,256]{3,1,0,2:T(8,128)S(1)}, u32[]{:S(2)}, u32[]{:S(2)}) %collective-permute-start.5) | collective-permute-done | bytes 786464 | tf_op jit(solution)/shard_map/ppermute | solution.py:32
  433.1 12.9 %collective-permute-done.7 = f32[2,128,1,256]{3,1,0,2:T(8,128)} collective-permute-done((f32[2,128,1,256]{3,1,0,2:T(8,128)}, f32[2,128,1,256]{3,1,0,2:T(8,128)}, u32[]{:S(2)}, u32[]{:S(2)}) %collective-permute-start.7) | collective-permute-done | bytes 262176 | tf_op jit(solution)/shard_map/ppermute | solution.py:32
  450.0 6.8 %all-to-all-start.3 = ((f32[2,32,8,128,16]{3,4,2,0,1:T(8,128)}), f32[2,32,8,128,16]{3,4,2,0,1:T(8,128)}, u32[]{:S(2)}, u32[]{:S(2)}) async-start(f32[2,32,8,128,16]{3,4,2,0,1:T(8,128)} %copy.140), calls=%async_computation.3 | async-start | bytes 8388608 | tf_op jit(solution)/shard_map/all_to_all | solution.py:82
  461.4 31.5 %fusion.3 = f32[2,128,4,2,256]{4,1,0,2,3:T(8,128)S(1)} fusion(f32[2,128,4096,1,1]{1,2,0,3,4:T(8,128)} %bitcast.161, f32[4,2,256,4096,1]{3,2,1,0,4:T(8,128)} %bitcast.152), kind=kOutput, calls=%fused_computation.4 | convolution fusion | flops 12884901888 | bytes 39845888 | tf_op jit(solution)/shard_map/iap,pq->iaq/dot_general | solution.py:85
  496.0 56.7 %all-to-all-done.3 = f32[2,32,8,128,16]{3,4,2,0,1:T(8,128)} async-done(((f32[2,32,8,128,16]{3,4,2,0,1:T(8,128)}), f32[2,32,8,128,16]{3,4,2,0,1:T(8,128)}, u32[]{:S(2)}, u32[]{:S(2)}) %all-to-all-start.3) | async-done | bytes 4194336 | tf_op jit(solution)/shard_map/all_to_all | solution.py:82
  557.3 32.5 %fusion.1 = f32[2,128,4,2,256]{4,1,0,2,3:T(8,128)} fusion(f32[2,128,4096,1,1]{1,2,0,3,4:T(8,128)} %bitcast.159, f32[4,2,256,4096,1]{3,2,1,0,4:T(8,128)} %bitcast.153), kind=kOutput, calls=%fused_computation.2 | convolution fusion | flops 12884901888 | bytes 39845888 | tf_op jit(solution)/shard_map/iap,pq->iaq/dot_general | solution.py:85
  593.3 23.2 %collective-permute-done.12 = f32[2,128,4,256]{3,1,0,2:T(8,128)S(1)} collective-permute-done((f32[2,128,4,256]{3,1,0,2:T(8,128)S(1)}, f32[2,128,4,256]{3,1,0,2:T(8,128)S(1)}, u32[]{:S(2)}, u32[]{:S(2)}) %collective-permute-start.12) | collective-permute-done | bytes 1048608 | tf_op jit(solution)/shard_map/ppermute | solution.py:17
  619.1 15.1 %collective-permute-done.13 = f32[2,128,3,256]{3,1,0,2:T(8,128)S(1)} collective-permute-done((f32[2,128,3,256]{3,1,0,2:T(8,128)S(1)}, f32[2,128,3,256]{3,1,0,2:T(8,128)S(1)}, u32[]{:S(2)}, u32[]{:S(2)}) %collective-permute-start.13) | collective-permute-done | bytes 786464 | tf_op jit(solution)/shard_map/ppermute | solution.py:32
  638.1 8.2 %collective-permute-done.11 = f32[2,128,1,256]{3,1,0,2:T(8,128)S(1)} collective-permute-done((f32[2,128,1,256]{3,1,0,2:T(8,128)S(1)}, f32[2,128,1,256]{3,1,0,2:T(8,128)S(1)}, u32[]{:S(2)}, u32[]{:S(2)}) %collective-permute-start.11) | collective-permute-done | bytes 262176 | tf_op jit(solution)/shard_map/ppermute | solution.py:32
  646.4 10.3 %collective-permute-done.15 = f32[2,128,1,256]{3,1,0,2:T(8,128)S(1)} collective-permute-done((f32[2,128,1,256]{3,1,0,2:T(8,128)S(1)}, f32[2,128,1,256]{3,1,0,2:T(8,128)S(1)}, u32[]{:S(2)}, u32[]{:S(2)}) %collective-permute-start.15) | collective-permute-done | bytes 262176 | tf_op jit(solution)/shard_map/ppermute | solution.py:32
  (96 shorter events, 111.2 us)
Async XLA Ops:
  24.4 7.5 %copy-start.5 = (s32[512]{0:T(512)S(1)}, s32[512]{0:T(512)}, u32[]{:S(2)}) copy-start(s32[512]{0:T(512)} %param.7) | copy-start | bytes 6148
  24.4 103.4 %all-to-all-start = ((f32[2,32,8,128,16]{3,4,2,0,1:T(8,128)}), f32[2,32,8,128,16]{3,4,2,0,1:T(8,128)}, u32[]{:S(2)}, u32[]{:S(2)}) async-start(f32[2,32,8,128,16]{3,4,2,0,1:T(8,128)} %bitcast.162), calls=%async_computation | async-start | bytes 8388608 | tf_op jit(solution)/shard_map/all_to_all | solution.py:82
  127.8 161.1 %all-to-all-start.1 = ((f32[2,32,8,128,16]{3,4,2,0,1:T(8,128)}), f32[2,32,8,128,16]{3,4,2,0,1:T(8,128)}, u32[]{:S(2)}, u32[]{:S(2)}) async-start(f32[2,32,8,128,16]{3,4,2,0,1:T(8,128)} %copy.129), calls=%async_computation.1 | async-start | bytes 8388608 | tf_op jit(solution)/shard_map/all_to_all | solution.py:82
  200.5 35.3 %collective-permute-start = (f32[2,128,4,256]{3,1,2,0:T(8,128)}, f32[2,128,4,256]{3,1,2,0:T(8,128)S(1)}, u32[]{:S(2)}, u32[]{:S(2)}) collective-permute-start(f32[2,128,4,256]{3,1,2,0:T(8,128)} %get-tuple-element.22), channel_id=1, source_target_pairs={{0,1},{1,0},{2,3},{3,2},{4,5},{5,4},{6,7},{7,6},{8,9},{9,8},{10,11... | collective-permute-start | bytes 3145736 | tf_op jit(solution)/shard_map/ppermute | solution.py:17
  237.5 20.9 %collective-permute-start.1 = (f32[2,128,3,256]{3,1,0,2:T(8,128)S(1)}, f32[2,128,3,256]{3,1,0,2:T(8,128)S(1)}, u32[]{:S(2)}, u32[]{:S(2)}) collective-permute-start(f32[2,128,3,256]{3,1,0,2:T(8,128)S(1)} %copy_select_fusion.1), channel_id=1, source_target_pairs={{0,2},{6,4},{1,3},{7,5},{8,10},{14,12},{9,11},{15,13},{16,18},{22,... | collective-permute-start | bytes 2359304 | tf_op jit(solution)/shard_map/ppermute | solution.py:32
  258.7 0.7 collective-permute-start.2
  260.3 22.8 %collective-permute-start.3 = (f32[2,128,1,256]{3,1,2,0:T(8,128)S(1)}, f32[2,128,1,256]{3,1,2,0:T(8,128)}, u32[]{:S(2)}, u32[]{:S(2)}) collective-permute-start(f32[2,128,1,256]{3,1,2,0:T(8,128)S(1)} %fusion.25), channel_id=1, source_target_pairs={{4,6},{2,0},{5,7},{3,1},{12,14},{10,8},{13,15},{11,9},{20,22},{18,... | collective-permute-start | bytes 786440 | tf_op jit(solution)/shard_map/ppermute | solution.py:32
  288.9 161.1 %all-to-all-start.2 = ((f32[2,32,8,128,16]{3,4,2,0,1:T(8,128)}), f32[2,32,8,128,16]{3,4,2,0,1:T(8,128)}, u32[]{:S(2)}, u32[]{:S(2)}) async-start(f32[2,32,8,128,16]{3,4,2,0,1:T(8,128)} %copy.135), calls=%async_computation.2 | async-start | bytes 8388608 | tf_op jit(solution)/shard_map/all_to_all | solution.py:82
  363.7 35.9 %collective-permute-start.4 = (f32[2,128,4,256]{3,1,0,2:T(8,128)S(1)}, f32[2,128,4,256]{3,1,0,2:T(8,128)S(1)}, u32[]{:S(2)}, u32[]{:S(2)}) collective-permute-start(f32[2,128,4,256]{3,1,0,2:T(8,128)S(1)} %select_bitcast_fusion.2), channel_id=1, source_target_pairs={{0,1},{1,0},{2,3},{3,2},{4,5},{5,4},{6,7},{7,6},{8,9},{9,8},{10,11... | collective-permute-start | bytes 3145736 | tf_op jit(solution)/shard_map/ppermute | solution.py:17
  399.9 21.1 %collective-permute-start.5 = (f32[2,128,3,256]{3,1,0,2:T(8,128)S(1)}, f32[2,128,3,256]{3,1,0,2:T(8,128)S(1)}, u32[]{:S(2)}, u32[]{:S(2)}) collective-permute-start(f32[2,128,3,256]{3,1,0,2:T(8,128)S(1)} %slice_select_fusion.6), channel_id=1, source_target_pairs={{0,2},{6,4},{1,3},{7,5},{8,10},{14,12},{9,11},{15,13},{16,18},{22,... | collective-permute-start | bytes 2359304 | tf_op jit(solution)/shard_map/ppermute | solution.py:32
  421.3 0.7 collective-permute-start.6
  423.6 22.3 %collective-permute-start.7 = (f32[2,128,1,256]{3,1,0,2:T(8,128)}, f32[2,128,1,256]{3,1,0,2:T(8,128)}, u32[]{:S(2)}, u32[]{:S(2)}) collective-permute-start(f32[2,128,1,256]{3,1,0,2:T(8,128)} %fusion.20), channel_id=1, source_target_pairs={{4,6},{2,0},{5,7},{3,1},{12,14},{10,8},{13,15},{11,9},{20,22},{18,... | collective-permute-start | bytes 786440 | tf_op jit(solution)/shard_map/ppermute | solution.py:32
  430.2 15.7 %copy-start.3 = (f32[2,128,2,256]{3,1,0,2:T(8,128)S(1)}, f32[2,128,2,256]{3,1,0,2:T(8,128)}, u32[]{:S(2)}) copy-start(f32[2,128,2,256]{3,1,0,2:T(8,128)} %copy-done.2) | copy-start | bytes 1572868
  450.0 102.6 %all-to-all-start.3 = ((f32[2,32,8,128,16]{3,4,2,0,1:T(8,128)}), f32[2,32,8,128,16]{3,4,2,0,1:T(8,128)}, u32[]{:S(2)}, u32[]{:S(2)}) async-start(f32[2,32,8,128,16]{3,4,2,0,1:T(8,128)} %copy.140), calls=%async_computation.3 | async-start | bytes 8388608 | tf_op jit(solution)/shard_map/all_to_all | solution.py:82
  494.1 97.6 %collective-permute-start.8 = (f32[2,128,4,256]{3,1,0,2:T(8,128)}, f32[2,128,4,256]{3,1,0,2:T(8,128)S(1)}, u32[]{:S(2)}, u32[]{:S(2)}) collective-permute-start(f32[2,128,4,256]{3,1,0,2:T(8,128)} %select_bitcast_fusion.1), channel_id=1, source_target_pairs={{0,1},{1,0},{2,3},{3,2},{4,5},{5,4},{6,7},{7,6},{8,9},{9,8},{10,11... | collective-permute-start | bytes 3145736 | tf_op jit(solution)/shard_map/ppermute | solution.py:17
  589.8 26.7 %copy-start = (f32[2,128,4,2,256]{4,1,0,2,3:T(8,128)S(1)}, f32[2,128,4,2,256]{4,1,0,2,3:T(8,128)}, u32[]{:S(2)}) copy-start(f32[2,128,4,2,256]{4,1,0,2,3:T(8,128)} %fusion.1) | copy-start | bytes 6291460
  591.6 24.9 %collective-permute-start.12 = (f32[2,128,4,256]{3,1,0,2:T(8,128)S(1)}, f32[2,128,4,256]{3,1,0,2:T(8,128)S(1)}, u32[]{:S(2)}, u32[]{:S(2)}) collective-permute-start(f32[2,128,4,256]{3,1,0,2:T(8,128)S(1)} %select_bitcast_fusion), channel_id=1, source_target_pairs={{0,1},{1,0},{2,3},{3,2},{4,5},{5,4},{6,7},{7,6},{8,9},{9,8},{10,11... | collective-permute-start | bytes 3145736 | tf_op jit(solution)/shard_map/ppermute | solution.py:17
  592.0 26.1 %collective-permute-start.9 = (f32[2,128,3,256]{3,1,0,2:T(8,128)S(1)}, f32[2,128,3,256]{3,1,0,2:T(8,128)S(1)}, u32[]{:S(2)}, u32[]{:S(2)}) collective-permute-start(f32[2,128,3,256]{3,1,0,2:T(8,128)S(1)} %slice_select_fusion.5), channel_id=1, source_target_pairs={{0,2},{6,4},{1,3},{7,5},{8,10},{14,12},{9,11},{15,13},{16,18},{22,... | collective-permute-start | bytes 2359304 | tf_op jit(solution)/shard_map/ppermute | solution.py:32
  616.8 17.4 %collective-permute-start.13 = (f32[2,128,3,256]{3,1,0,2:T(8,128)S(1)}, f32[2,128,3,256]{3,1,0,2:T(8,128)S(1)}, u32[]{:S(2)}, u32[]{:S(2)}) collective-permute-start(f32[2,128,3,256]{3,1,0,2:T(8,128)S(1)} %slice_select_fusion.4), channel_id=1, source_target_pairs={{0,2},{6,4},{1,3},{7,5},{8,10},{14,12},{9,11},{15,13},{16,18},{22,... | collective-permute-start | bytes 2359304 | tf_op jit(solution)/shard_map/ppermute | solution.py:32
  618.4 16.8 %collective-permute-start.10 = (f32[2,128,2,256]{3,1,0,2:T(8,128)S(1)}, f32[2,128,2,256]{3,1,0,2:T(8,128)S(1)}, u32[]{:S(2)}, u32[]{:S(2)}) collective-permute-start(f32[2,128,2,256]{3,1,0,2:T(8,128)S(1)} %fusion.9), channel_id=1, source_target_pairs={{2,4},{4,2},{3,5},{5,3},{10,12},{12,10},{11,13},{13,11},{18,20},{2... | collective-permute-start | bytes 1572872 | tf_op jit(solution)/shard_map/ppermute | solution.py:32
  634.5 2.2 collective-permute-start.14
  635.3 21.5 %copy-start.4 = (f32[2,128,256]{2,1,0:T(8,128)S(1)}, f32[2,128,256]{2,1,0:T(8,128)}, u32[]{:S(2)}) copy-start(f32[2,128,256]{2,1,0:T(8,128)} %fusion.23) | copy-start | bytes 786436
  635.4 11.0 %collective-permute-start.11 = (f32[2,128,1,256]{3,1,0,2:T(8,128)S(1)}, f32[2,128,1,256]{3,1,0,2:T(8,128)S(1)}, u32[]{:S(2)}, u32[]{:S(2)}) collective-permute-start(f32[2,128,1,256]{3,1,0,2:T(8,128)S(1)} %fusion.16), channel_id=1, source_target_pairs={{4,6},{2,0},{5,7},{3,1},{12,14},{10,8},{13,15},{11,9},{20,22},{18,... | collective-permute-start | bytes 786440 | tf_op jit(solution)/shard_map/ppermute | solution.py:32
  636.8 19.9 %collective-permute-start.15 = (f32[2,128,1,256]{3,1,0,2:T(8,128)S(1)}, f32[2,128,1,256]{3,1,0,2:T(8,128)S(1)}, u32[]{:S(2)}, u32[]{:S(2)}) collective-permute-start(f32[2,128,1,256]{3,1,0,2:T(8,128)S(1)} %fusion.12), channel_id=1, source_target_pairs={{4,6},{2,0},{5,7},{3,1},{12,14},{10,8},{13,15},{11,9},{20,22},{18,... | collective-permute-start | bytes 786440 | tf_op jit(solution)/shard_map/ppermute | solution.py:32
  (3 other events, 9.0 us)

commit v7 on v6

--- a/solution.py
+++ b/solution.py
@@ -60,7 +60,7 @@
         k_local * virt_count, column_slab * virt_count
     )
 
-    chunks = 4 if slab_rows % 4 == 0 else 1
+    chunks = 2 if slab_rows % 2 == 0 else 1
     rows = slab_rows // chunks
     results = []
     for step in range(chunks):
@@ -75,7 +75,7 @@
         grouped = jnp.transpose(grouped, (0, 3, 1, 2, 4, 5)).reshape(
             rows, row_count * col_count, k_local, a_local, c_local
         )
-        if step == 1:
+        if step == 1 and chunks > 2:
             grouped, masked_ints = lax.optimization_barrier((grouped, masked_ints))
         if step >= 2:
             grouped, results[step - 2] = lax.optimization_barrier((grouped, results[step - 2]))
@@ -90,10 +90,7 @@
             preferred_element_type=jnp.float32,
         )
         flat = partial_value.reshape(rows, a_local, column_slab * virt_count)
-        if col_count % 4 == 0:
-            results.append(scatter_sum(flat, col_count, col_place))
-        else:
-            results.append(lax.psum_scatter(flat, "col", scatter_dimension=2, tiled=True))
+        results.append(lax.psum_scatter(flat, "col", scatter_dimension=2, tiled=True))
     return jnp.concatenate(results, axis=0)
 
 

time: 665 us -> 596 us (0.90)
  waiting for transfers between devices: 271 us -> 379 us
  local copies, waits for them, and re-layouts: 160 us -> 86 us
  matrix products: 127 us -> 65.8 us
  starting transfers between devices: 50 us -> 11.7 us
  between operations: 0.69 us -> 13.5 us
  other arithmetic: 49.8 us -> 38 us
    all_to_all x4 -> x2, waiting for transfers between devices: 89.1 us -> 294 us  [per_device(): lax.all_to_all(grouped, ('row', 'col'), split_axis=1, concat_axis=4, tile...]
    ppermute x16 -> x0, waiting for transfers between devices: 182 us -> none  [the longest x12 91.4 us: scatter_sum(): got = lax.ppermute(payload, 'col', links)]
    reduce_scatter x0 -> x2, waiting for transfers between devices: none -> 84.6 us  [per_device(): lax.psum_scatter(flat, 'col', scatter_dimension=2, tiled=True)]
    dot_general x2 -> x0, local copies, waits for them, and re-layouts: 62.3 us -> none  [per_device(): jnp.einsum('iap,pq->iaq', blocks, masked_ints, precision=lax.Precision.HI...]
    dot_general x4 -> x2, matrix products: 127 us -> 65.8 us  [per_device(): jnp.einsum('iap,pq->iaq', blocks, masked_ints, precision=lax.Precision.HI...]
    reshape x0 -> x1, local copies, waits for them, and re-layouts: none -> 39.8 us  [per_device(): jnp.where(int_sym == 0, cycle_integrals, 0.0)]
    unnamed x15 -> x4, local copies, waits for them, and re-layouts: 31.6 us -> 0.01 us
    ppermute x16 -> x0, starting transfers between devices: 24.7 us -> none  [the longest x12 19 us: scatter_sum(): got = lax.ppermute(payload, 'col', links)]
  transfers between devices with their start and end apart: 20 -> 4, of which waited for: 12 -> 3; matrix products, arithmetic and copies ran while one was open for 47% -> 26% of each run, Pallas kernels for 0% -> 0%
where the time goes in v7:
time: 596 us; the launch traced here: 594 us
  waiting for transfers between devices  379 us (64%)
  local copies, waits for them, and re-layouts  86 us (14%)
  matrix products  65.8 us (11%)
  other arithmetic  38 us (6%)
  between operations  13.5 us (2%)
  starting transfers between devices  11.7 us (2%)
    all_to_all x2, waiting for transfers between devices, per_device(): lax.all_to_all(grouped, ('row', 'col'), split_axis=1, concat_axis=4, tile...  294 us
    reduce_scatter x2, waiting for transfers between devices, per_device(): lax.psum_scatter(flat, 'col', scatter_dimension=2, tiled=True)  84.6 us
    dot_general x2, matrix products, per_device(): jnp.einsum('iap,pq->iaq', blocks, masked_ints, precision=lax.Precision.HI...  65.8 us
    reshape x1, local copies, waits for them, and re-layouts, per_device(): jnp.where(int_sym == 0, cycle_integrals, 0.0)  39.8 us
    select_n x1, other arithmetic, per_device(): jnp.where(int_sym == 0, cycle_integrals, 0.0)  23.1 us
    reshape x2, local copies, waits for them, and re-layouts, per_device(): masked_amps.reshape(rows, col_count, k_local, row_count, a_local, c_local)  19.8 us
    reshape x2, local copies, waits for them, and re-layouts, per_device(): jnp.transpose(grouped, (0, 3, 1, 2, 4, 5))  15.6 us
  transfers between devices with their start and end apart: 4, of which 3 were waited for; matrix products, arithmetic and copies ran while one was open for 26% of the time, Pallas kernels for 0%

profile of v7, /device:TPU:0, one launch (start us, length us, event | category | flops | bytes accessed | tf_op | source)
XLA Modules:
  0.0 593.7 jit_solution(1753503171140539836)
XLA Ops:
  6.5 0.8 fusion.1
  7.3 0.8 dynamic_slice.6
  8.1 0.8 broadcast_xor_fusion
  8.8 0.7 broadcast_xor_fusion.4
  9.6 11.0 %slice_select_fusion.1 = (f32[4,64,512,16]{2,3,1,0:T(8,128)}, f32[4,64,512,16]{2,3,1,0:T(8,128)}) fusion(f32[8,64,512,16]{2,3,1,0:T(8,128)} %param.4, s32[512,16]{0,1:T(8,128)S(1)} %broadcast_xor_fusion, s32[4,64]{1,0:T(4,128)S(1)} %get-tuple-element.7, s32[4,64]{1,0:T(4,128)S(1)} %get-tuple-element.8), kind=kLoop, calls=%fused_computation.4 | loop fusion | flops 12582912 | bytes 33589248 | tf_op jit(solution)/shard_map/jit(_where)/select_n | solution.py:73
  20.6 9.9 %reshape.185 = f32[4,8,8,4,128,16]{4,3,5,2,1,0:T(4,128)} reshape(f32[4,64,512,16]{2,3,1,0:T(8,128)} %get-tuple-element.5) | data formatting | bytes 16777216 | tf_op jit(solution)/shard_map/reshape | solution.py:74
  30.5 7.8 %copy.23 = f32[4,4,8,8,128,16]{4,5,3,0,2,1:T(8,128)} copy(f32[4,4,8,8,128,16]{4,1,5,3,2,0:T(4,128)} %bitcast.38) | data formatting | bytes 16777216 | tf_op jit(solution)/shard_map/reshape | solution.py:75
  38.3 7.4 %all-to-all-start = ((f32[4,32,8,128,16]{3,4,2,0,1:T(8,128)}), f32[4,32,8,128,16]{3,4,2,0,1:T(8,128)}, u32[]{:S(2)}, u32[]{:S(2)}) async-start(f32[4,32,8,128,16]{3,4,2,0,1:T(8,128)} %bitcast.37), calls=%async_computation | async-start | bytes 16777216 | tf_op jit(solution)/shard_map/all_to_all | solution.py:82
  45.7 9.9 %reshape.190 = f32[4,8,8,4,128,16]{4,3,5,2,1,0:T(4,128)} reshape(f32[4,64,512,16]{2,3,1,0:T(8,128)} %get-tuple-element.6) | data formatting | bytes 16777216 | tf_op jit(solution)/shard_map/reshape | solution.py:74
  55.7 7.9 %copy.25 = f32[4,4,8,8,128,16]{4,5,3,0,2,1:T(8,128)} copy(f32[4,4,8,8,128,16]{4,1,5,3,2,0:T(4,128)} %bitcast.39) | data formatting | bytes 16777216 | tf_op jit(solution)/shard_map/reshape | solution.py:75
  63.5 171.8 %all-to-all-done = f32[4,32,8,128,16]{3,4,2,0,1:T(8,128)} async-done(((f32[4,32,8,128,16]{3,4,2,0,1:T(8,128)}), f32[4,32,8,128,16]{3,4,2,0,1:T(8,128)}, u32[]{:S(2)}, u32[]{:S(2)}) %all-to-all-start) | async-done | bytes 8388640 | tf_op jit(solution)/shard_map/all_to_all | solution.py:82
  235.3 3.8 all-to-all-start.1
  239.1 0.2 reduce-scatter.3.cloned.1.call-start
  239.3 0.1 dynamic_slice.7
  239.6 23.1 %fusion = f32[8,512,4,512]{3,2,1,0:T(4,128)} fusion(f32[8,512,4,512]{3,2,1,0:T(4,128)} %param.5, s32[4,512]{1,0:T(4,128)S(1)} %broadcast_xor_fusion.2, s32[8,512]{1,0:T(8,128)S(1)} %broadcast_xor_fusion.1), kind=kLoop, calls=%fused_computation.1 | loop fusion | flops 25165824 | bytes 67133440 | tf_op jit(solution)/shard_map/jit(_where)/select_n | solution.py:59
  262.7 39.8 %reshape.194 = f32[4096,2048,1]{1,0,2:T(8,128)} reshape(f32[8,512,4,512]{3,2,1,0:T(4,128)} %fusion) | data formatting | bytes 67108864 | tf_op jit(solution)/shard_map/reshape | solution.py:59
  302.4 4.5 copy.17
  307.0 32.7 %fusion.2 = f32[4,128,2048]{2,1,0:T(8,128)} fusion(f32[4,128,4096]{1,2,0:T(8,128)S(1)} %bitcast.41, f32[4096,2048,1]{1,0,2:T(8,128)} %reshape.194), kind=kOutput, calls=%fused_computation.13 | convolution fusion | flops 25769803776 | bytes 46137344 | tf_op jit(solution)/shard_map/iap,pq->iaq/dot_general | solution.py:85
  339.8 0.3 reduce-scatter.5.cloned.1.call-start
  340.0 122.3 %all-to-all-done.1 = f32[4,32,8,128,16]{3,4,2,0,1:T(8,128)} async-done(((f32[4,32,8,128,16]{3,4,2,0,1:T(8,128)}), f32[4,32,8,128,16]{3,4,2,0,1:T(8,128)}, u32[]{:S(2)}, u32[]{:S(2)}) %all-to-all-start.1) | async-done | bytes 8388640 | tf_op jit(solution)/shard_map/all_to_all | solution.py:82
  462.3 4.5 copy.21
  466.9 33.0 %fusion.3 = f32[4,128,2048]{2,1,0:T(8,128)} fusion(f32[4,128,4096]{1,2,0:T(8,128)S(1)} %bitcast.40, f32[4096,2048,1]{1,0,2:T(8,128)} %reshape.194), kind=kOutput, calls=%fused_computation.14 | convolution fusion | flops 25769803776 | bytes 46137344 | tf_op jit(solution)/shard_map/iap,pq->iaq/dot_general | solution.py:85
  499.9 84.6 %reduce-scatter.5.cloned.1.call-done = f32[4,128,256]{2,1,0:T(8,128)} async-done(((f32[4,128,2048]{2,1,0:T(8,128)}), f32[4,128,256]{2,1,0:T(8,128)}) %reduce-scatter.5.cloned.1.call-update) | async-done | bytes 524304 | tf_op jit(solution)/shard_map/reduce_scatter | solution.py:93
  584.6 2.2 pad_maximum_fusion
  (9 shorter events, 0.2 us)
Async XLA Ops:
  38.3 197.0 %all-to-all-start = ((f32[4,32,8,128,16]{3,4,2,0,1:T(8,128)}), f32[4,32,8,128,16]{3,4,2,0,1:T(8,128)}, u32[]{:S(2)}, u32[]{:S(2)}) async-start(f32[4,32,8,128,16]{3,4,2,0,1:T(8,128)} %bitcast.37), calls=%async_computation | async-start | bytes 16777216 | tf_op jit(solution)/shard_map/all_to_all | solution.py:82
  235.3 4.1 copy-start.1
  235.3 4.1 copy-start
  235.3 227.0 %all-to-all-start.1 = ((f32[4,32,8,128,16]{3,4,2,0,1:T(8,128)}), f32[4,32,8,128,16]{3,4,2,0,1:T(8,128)}, u32[]{:S(2)}, u32[]{:S(2)}) async-start(f32[4,32,8,128,16]{3,4,2,0,1:T(8,128)} %bitcast.36), calls=%async_computation.2 | async-start | bytes 16777216 | tf_op jit(solution)/shard_map/all_to_all | solution.py:82
  239.1 260.8 %reduce-scatter.3.cloned.1.call-start = ((), (), s32[]{:S(2)}) async-start(), calls=%async_computation.4 | async-start | bytes 4718592 | tf_op jit(solution)/shard_map/reduce_scatter | solution.py:93
  339.8 244.8 %reduce-scatter.5.cloned.1.call-start = ((), (), s32[]{:S(2)}) async-start(), calls=%async_computation.5 | async-start | bytes 4718592 | tf_op jit(solution)/shard_map/reduce_scatter | solution.py:93
Sparse Core Ops, SparseCore 0:
  339.9 149.7 reduce-scatter.2
  500.0 84.4 reduce-scatter.4

commit v8 on v7

--- a/solution.py
+++ b/solution.py
@@ -60,13 +60,15 @@
         k_local * virt_count, column_slab * virt_count
     )
 
-    chunks = 2 if slab_rows % 2 == 0 else 1
-    rows = slab_rows // chunks
-    results = []
-    for step in range(chunks):
-        amps = amplitudes[step * rows:(step + 1) * rows]
+    first = min(slab_rows, (slab_rows * 5 + 7) // 8)
+    bounds = [(0, first)] + ([(first, slab_rows)] if first < slab_rows else [])
+    chunks = len(bounds)
+    exchanged = []
+    for step, (lo, hi) in enumerate(bounds):
+        rows = hi - lo
+        amps = amplitudes[lo:hi]
         amp_sym = (
-            slab_irrep[step * rows:(step + 1) * rows, None, None, None]
+            slab_irrep[lo:hi, None, None, None]
             ^ occ_irrep[None, :, None, None]
             ^ (virt_irrep[None, None, :, None] ^ c_irrep[None, None, None, :])
         )
@@ -75,11 +77,16 @@
         grouped = jnp.transpose(grouped, (0, 3, 1, 2, 4, 5)).reshape(
             rows, row_count * col_count, k_local, a_local, c_local
         )
-        if step == 1 and chunks > 2:
-            grouped, masked_ints = lax.optimization_barrier((grouped, masked_ints))
-        if step >= 2:
-            grouped, results[step - 2] = lax.optimization_barrier((grouped, results[step - 2]))
-        items = lax.all_to_all(grouped, ("row", "col"), split_axis=1, concat_axis=4, tiled=True)
+        if step == 1:
+            grouped, exchanged[0], masked_ints = lax.optimization_barrier(
+                (grouped, exchanged[0], masked_ints)
+            )
+        exchanged.append(
+            lax.all_to_all(grouped, ("row", "col"), split_axis=1, concat_axis=4, tiled=True)
+        )
+    results = []
+    for items in exchanged:
+        rows = items.shape[0]
         blocks = jnp.transpose(items.reshape(rows, k_local, a_local, virt_count), (0, 2, 1, 3))
         blocks = blocks.reshape(rows, a_local, k_local * virt_count)
         partial_value = jnp.einsum(

time: 596 us -> 605 us (1.015)
  waiting for transfers between devices: 379 us -> 388 us
    reshape x1 -> x0, local copies, waits for them, and re-layouts: 39.8 us -> none  [per_device(): jnp.where(int_sym == 0, cycle_integrals, 0.0)]
    unnamed x4 -> x7, local copies, waits for them, and re-layouts: 0.01 us -> 29.9 us
    all_to_all x2, waiting for transfers between devices: 294 us -> 307 us  [per_device(): lax.all_to_all(grouped, ('row', 'col'), split_axis=1, concat_axis=4, tile...]
    reshape x2 -> x1, local copies, waits for them, and re-layouts: 15.6 us -> 9.35 us  [per_device(): jnp.transpose(grouped, (0, 3, 1, 2, 4, 5))]
    transpose x0 -> x1, local copies, waits for them, and re-layouts: none -> 6.27 us  [per_device(): jnp.transpose(grouped, (0, 3, 1, 2, 4, 5))]
    select_n x1 -> x2, other arithmetic: 11 us -> 14 us  [per_device(): masked_amps = jnp.where(amp_sym == 0, amps, 0.0)]
  transfers between devices with their start and end apart: 4 -> 4, of which waited for: 3 -> 4; matrix products, arithmetic and copies ran while one was open for 26% -> 24% of each run, Pallas kernels for 0% -> 0%
where the time goes in v8:
time: 605 us; the launch traced here: 604 us
  waiting for transfers between devices  388 us (64%)
  local copies, waits for them, and re-layouts  82.4 us (14%)
  matrix products  67.8 us (11%)
  other arithmetic  41.1 us (7%)
  between operations  13.5 us (2%)
  starting transfers between devices  11.5 us (2%)
    all_to_all x2, waiting for transfers between devices, per_device(): lax.all_to_all(grouped, ('row', 'col'), split_axis=1, concat_axis=4, tile...  307 us
    reduce_scatter x2, waiting for transfers between devices, per_device(): lax.psum_scatter(flat, 'col', scatter_dimension=2, tiled=True)  80.9 us
    dot_general x2, matrix products, per_device(): jnp.einsum('iap,pq->iaq', blocks, masked_ints, precision=lax.Precision.HI...  67.8 us
    unnamed x7, local copies, waits for them, and re-layouts  29.9 us
    select_n x1, other arithmetic, per_device(): jnp.where(int_sym == 0, cycle_integrals, 0.0)  23.1 us
    reshape x2, local copies, waits for them, and re-layouts, per_device(): masked_amps.reshape(rows, col_count, k_local, row_count, a_local, c_local)  19.8 us
    select_n x2, other arithmetic, per_device(): masked_amps = jnp.where(amp_sym == 0, amps, 0.0)  14 us
    all_to_all x2, local copies, waits for them, and re-layouts, per_device(): lax.all_to_all(grouped, ('row', 'col'), split_axis=1, concat_axis=4, tile...  13 us
  transfers between devices with their start and end apart: 4, of which 4 were waited for; matrix products, arithmetic and copies ran while one was open for 24% of the time, Pallas kernels for 0%

profile of v8, /device:TPU:0, one launch (start us, length us, event | category | flops | bytes accessed | tf_op | source)
XLA Modules:
  0.0 603.8 jit_solution(13408712970463548400)
XLA Ops:
  6.5 0.8 broadcast_xor_fusion.3
  7.3 0.8 dynamic_slice.6
  8.1 0.8 broadcast_xor_fusion
  8.8 9.1 %slice_select_fusion = f32[5,64,512,16]{2,3,1,0:T(8,128)} fusion(f32[8,64,512,16]{2,3,1,0:T(8,128)} %param.4, s32[512,16]{0,1:T(8,128)S(1)} %broadcast_xor_fusion, s32[5,64]{1,0:T(8,128)S(1)} %broadcast_xor_fusion.3), kind=kLoop, calls=%fused_computation.6 | loop fusion | flops 7864320 | bytes 21005568 | tf_op jit(solution)/shard_map/jit(_where)/select_n | solution.py:75
  17.9 12.2 %reshape.189 = f32[5,8,8,4,128,16]{4,3,5,2,1,0:T(4,128)} reshape(f32[5,64,512,16]{2,3,1,0:T(8,128)} %slice_select_fusion) | data formatting | bytes 20971520 | tf_op jit(solution)/shard_map/reshape | solution.py:76
  30.1 9.3 %copy.24 = f32[5,4,8,8,128,16]{4,5,3,0,2,1:T(8,128)} copy(f32[5,4,8,8,128,16]{4,1,5,3,2,0:T(4,128)} %bitcast.46) | data formatting | bytes 20971520 | tf_op jit(solution)/shard_map/reshape | solution.py:77
  39.5 7.4 %all-to-all-start = ((f32[5,32,8,128,16]{3,4,2,0,1:T(8,128)}), f32[5,32,8,128,16]{3,4,2,0,1:T(8,128)}, u32[]{:S(2)}, u32[]{:S(2)}) async-start(f32[5,32,8,128,16]{3,4,2,0,1:T(8,128)} %bitcast.45), calls=%async_computation | async-start | bytes 20971520 | tf_op jit(solution)/shard_map/all_to_all | solution.py:85
  47.1 4.9 slice_select_fusion.1
  52.1 7.6 %reshape.187 = f32[3,8,8,4,128,16]{4,3,5,2,1,0:T(4,128)} reshape(f32[3,64,512,16]{2,3,1,0:T(8,128)} %slice_select_fusion.1) | data formatting | bytes 12582912 | tf_op jit(solution)/shard_map/reshape | solution.py:76
  59.7 6.3 %copy.15 = f32[3,4,8,8,128,16]{4,5,3,2,1,0:T(8,128)} copy(f32[3,4,8,8,128,16]{4,1,5,3,2,0:T(4,128)} %bitcast.50) | data formatting | bytes 12582912 | tf_op jit(solution)/shard_map/transpose | solution.py:77
  66.1 23.1 %fusion.4 = f32[8,512,4,512]{3,2,1,0:T(4,128)} fusion(f32[8,512,4,512]{3,2,1,0:T(4,128)} %param.5, s32[4,512]{1,0:T(4,128)S(1)} %broadcast_xor_fusion.2, s32[8,512]{1,0:T(8,128)S(1)} %broadcast_xor_fusion.1), kind=kLoop, calls=%fused_computation.5 | loop fusion | flops 25165824 | bytes 67133440 | tf_op jit(solution)/shard_map/jit(_where)/select_n | solution.py:59
  89.2 29.9 %copy.26 = f32[512,8,4,512]{3,1,2,0:T(8,128)} copy(f32[512,8,4,512]{3,2,1,0:T(4,128)} %bitcast.44) | data formatting | bytes 67108864
  119.1 164.0 %all-to-all-done = f32[5,32,8,128,16]{3,4,2,0,1:T(8,128)} async-done(((f32[5,32,8,128,16]{3,4,2,0,1:T(8,128)}), f32[5,32,8,128,16]{3,4,2,0,1:T(8,128)}, u32[]{:S(2)}, u32[]{:S(2)}) %all-to-all-start) | async-done | bytes 10485792 | tf_op jit(solution)/shard_map/all_to_all | solution.py:85
  283.1 9.6 %copy.18 = f32[5,32,8,128,16]{3,4,1,2,0:T(8,128)} copy(f32[5,32,8,128,16]{3,4,2,0,1:T(8,128)} %all-to-all-done) | data formatting | bytes 20971520 | tf_op jit(solution)/shard_map/all_to_all | solution.py:85
  292.7 3.1 copy.20
  295.7 3.6 all-to-all-start.1
  299.6 41.2 %fusion.2 = f32[5,128,2048]{2,1,0:T(8,128)} fusion(f32[5,128,4096]{1,2,0:T(8,128)} %bitcast.51, f32[4096,2048]{1,0:T(8,128)} %bitcast.47), kind=kOutput, calls=%fused_computation.2 | convolution fusion | flops 32212254720 | bytes 49283072 | tf_op jit(solution)/shard_map/iap,pq->iaq/dot_general | solution.py:92
  340.8 0.3 reduce-scatter.5.cloned.1.call-start
  341.1 142.6 %all-to-all-done.1 = f32[3,32,8,128,16]{3,4,2,0,1:T(8,128)} async-done(((f32[3,32,8,128,16]{3,4,2,0,1:T(8,128)}), f32[3,32,8,128,16]{3,4,2,0,1:T(8,128)}, u32[]{:S(2)}, u32[]{:S(2)}) %all-to-all-start.1) | async-done | bytes 6291488 | tf_op jit(solution)/shard_map/all_to_all | solution.py:85
  483.7 3.4 copy.21
  487.1 26.6 %fusion = f32[3,128,2048]{2,1,0:T(8,128)} fusion(f32[3,128,4096]{1,2,0:T(8,128)S(1)} %bitcast.52, f32[4096,2048]{1,0:T(8,128)} %bitcast.48), kind=kOutput, calls=%fused_computation | convolution fusion | flops 19327352832 | bytes 42991616 | tf_op jit(solution)/shard_map/iap,pq->iaq/dot_general | solution.py:92
  513.8 2.5 reduce-scatter.3.cloned.1.call-done
  516.3 78.4 %reduce-scatter.5.cloned.1.call-done = f32[3,128,256]{2,1,0:T(8,128)} async-done(((f32[3,128,2048]{2,1,0:T(8,128)}), f32[3,128,256]{2,1,0:T(8,128)}) %reduce-scatter.5.cloned.1.call-update) | async-done | bytes 393232 | tf_op jit(solution)/shard_map/reduce_scatter | solution.py:100
  594.7 2.3 pad_maximum_fusion
  (14 shorter events, 0.6 us)
Async XLA Ops:
  39.5 7.4 %copy-start.2 = (s32[64]{0:T(128)S(1)}, s32[64]{0:T(128)}, u32[]{:S(2)}) copy-start(s32[64]{0:T(128)} %param.6) | copy-start | bytes 772
  39.5 243.6 %all-to-all-start = ((f32[5,32,8,128,16]{3,4,2,0,1:T(8,128)}), f32[5,32,8,128,16]{3,4,2,0,1:T(8,128)}, u32[]{:S(2)}, u32[]{:S(2)}) async-start(f32[5,32,8,128,16]{3,4,2,0,1:T(8,128)} %bitcast.45), calls=%async_computation | async-start | bytes 20971520 | tf_op jit(solution)/shard_map/all_to_all | solution.py:85
  52.1 13.9 %copy-start.1 = (s32[512]{0:T(512)S(1)}, s32[512]{0:T(512)}, u32[]{:S(2)}) copy-start(s32[512]{0:T(512)} %param.7) | copy-start | bytes 6148
  283.1 9.6 %copy-start = (f32[3,4,8,8,128,16]{4,5,3,2,1,0:T(8,128)S(1)}, f32[3,4,8,8,128,16]{4,5,3,2,1,0:T(8,128)}, u32[]{:S(2)}) copy-start(f32[3,4,8,8,128,16]{4,5,3,2,1,0:T(8,128)} %copy.15) | copy-start | bytes 18874372
  295.7 188.0 %all-to-all-start.1 = ((f32[3,32,8,128,16]{3,4,2,0,1:T(8,128)}), f32[3,32,8,128,16]{3,4,2,0,1:T(8,128)}, u32[]{:S(2)}, u32[]{:S(2)}) async-start(f32[3,32,8,128,16]{3,4,2,0,1:T(8,128)} %copy.20), calls=%async_computation.2 | async-start | bytes 12582912 | tf_op jit(solution)/shard_map/all_to_all | solution.py:85
  299.3 216.9 %reduce-scatter.3.cloned.1.call-start = ((), (), s32[]{:S(2)}) async-start(), calls=%async_computation.4 | async-start | bytes 5898240 | tf_op jit(solution)/shard_map/reduce_scatter | solution.py:100
  340.8 253.9 %reduce-scatter.5.cloned.1.call-start = ((), (), s32[]{:S(2)}) async-start(), calls=%async_computation.5 | async-start | bytes 3538944 | tf_op jit(solution)/shard_map/reduce_scatter | solution.py:100
Sparse Core Ops, SparseCore 0:
  340.9 175.3 reduce-scatter.2
  519.9 74.7 reduce-scatter.4

commit v9 on v7

--- a/solution.py
+++ b/solution.py
@@ -90,7 +90,19 @@
             preferred_element_type=jnp.float32,
         )
         flat = partial_value.reshape(rows, a_local, column_slab * virt_count)
-        results.append(lax.psum_scatter(flat, "col", scatter_dimension=2, tiled=True))
+        if step == chunks - 1 and rows % 2 == 0 and col_count % 4 == 0:
+            half = rows // 2
+            results.append(
+                jnp.concatenate(
+                    [
+                        lax.psum_scatter(flat[:half], "col", scatter_dimension=2, tiled=True),
+                        scatter_sum(flat[half:], col_count, col_place),
+                    ],
+                    axis=0,
+                )
+            )
+        else:
+            results.append(lax.psum_scatter(flat, "col", scatter_dimension=2, tiled=True))
     return jnp.concatenate(results, axis=0)
 
 

time: 596 us -> 603 us (1.012)
  local copies, waits for them, and re-layouts: 86 us -> 94 us
    ppermute x0 -> x4, waiting for transfers between devices: none -> 88 us  [the longest x3 53.7 us: scatter_sum(): got = lax.ppermute(payload, 'col', links)]
    reduce_scatter x2 -> x1, waiting for transfers between devices: 84.6 us -> 0.02 us  [per_device(): lax.psum_scatter(flat, 'col', scatter_dimension=2, tiled=True)]
    all_to_all x2, waiting for transfers between devices: 294 us -> 285 us  [per_device(): lax.all_to_all(grouped, ('row', 'col'), split_axis=1, concat_axis=4, tile...]
  transfers between devices with their start and end apart: 4 -> 8, of which waited for: 3 -> 5; matrix products, arithmetic and copies ran while one was open for 26% -> 27% of each run, Pallas kernels for 0% -> 0%
where the time goes in v9:
time: 603 us; the launch traced here: 601 us
  waiting for transfers between devices  373 us (62%)
  local copies, waits for them, and re-layouts  94 us (16%)
  matrix products  64.3 us (11%)
  other arithmetic  41.2 us (7%)
  starting transfers between devices  15.1 us (3%)
  between operations  13.7 us (2%)
    all_to_all x2, waiting for transfers between devices, per_device(): lax.all_to_all(grouped, ('row', 'col'), split_axis=1, concat_axis=4, tile...  285 us
    dot_general x2, matrix products, per_device(): jnp.einsum('iap,pq->iaq', blocks, masked_ints, precision=lax.Precision.HI...  64.3 us
    ppermute x3, waiting for transfers between devices, scatter_sum(): got = lax.ppermute(payload, 'col', links)  53.7 us
    reshape x1, local copies, waits for them, and re-layouts, per_device(): jnp.where(int_sym == 0, cycle_integrals, 0.0)  39.8 us
    ppermute x1, waiting for transfers between devices, scatter_sum(): line_sum = keep + lax.ppermute(give, 'col', swap)  34.4 us
    select_n x1, other arithmetic, per_device(): jnp.where(int_sym == 0, cycle_integrals, 0.0)  23.1 us
    reshape x2, local copies, waits for them, and re-layouts, per_device(): masked_amps.reshape(rows, col_count, k_local, row_count, a_local, c_local)  19.9 us
    reshape x2, local copies, waits for them, and re-layouts, per_device(): jnp.transpose(grouped, (0, 3, 1, 2, 4, 5))  15.6 us
  transfers between devices with their start and end apart: 8, of which 5 were waited for; matrix products, arithmetic and copies ran while one was open for 27% of the time, Pallas kernels for 0%

profile of v9, /device:TPU:0, one launch (start us, length us, event | category | flops | bytes accessed | tf_op | source)
XLA Modules:
  0.0 600.9 jit_solution(17840355223827182168)
XLA Ops:
  9.6 11.1 %slice_select_fusion.1 = (f32[4,64,512,16]{2,3,1,0:T(8,128)}, f32[4,64,512,16]{2,3,1,0:T(8,128)}) fusion(f32[8,64,512,16]{2,3,1,0:T(8,128)} %param.4, s32[512,16]{0,1:T(8,128)S(1)} %broadcast_xor_fusion, s32[4,64]{1,0:T(4,128)S(1)} %get-tuple-element.15, s32[4,64]{1,0:T(4,128)S(1)} %get-tuple-element.16), kind=kLoop, calls=%fused_computation.4 | loop fusion | flops 12582912 | bytes 33589248 | tf_op jit(solution)/shard_map/jit(_where)/select_n | solution.py:73
  20.7 9.9 %reshape.201 = f32[4,8,8,4,128,16]{4,3,5,2,1,0:T(4,128)} reshape(f32[4,64,512,16]{2,3,1,0:T(8,128)} %get-tuple-element.6) | data formatting | bytes 16777216 | tf_op jit(solution)/shard_map/reshape | solution.py:74
  30.6 7.8 %copy.34 = f32[4,4,8,8,128,16]{4,5,3,0,2,1:T(8,128)} copy(f32[4,4,8,8,128,16]{4,1,5,3,2,0:T(4,128)} %bitcast.45) | data formatting | bytes 16777216 | tf_op jit(solution)/shard_map/reshape | solution.py:75
  38.4 7.4 %all-to-all-start.1 = ((f32[4,32,8,128,16]{3,4,2,0,1:T(8,128)}), f32[4,32,8,128,16]{3,4,2,0,1:T(8,128)}, u32[]{:S(2)}, u32[]{:S(2)}) async-start(f32[4,32,8,128,16]{3,4,2,0,1:T(8,128)} %bitcast.44), calls=%async_computation.2 | async-start | bytes 16777216 | tf_op jit(solution)/shard_map/all_to_all | solution.py:82
  45.8 9.9 %reshape.196 = f32[4,8,8,4,128,16]{4,3,5,2,1,0:T(4,128)} reshape(f32[4,64,512,16]{2,3,1,0:T(8,128)} %get-tuple-element.5) | data formatting | bytes 16777216 | tf_op jit(solution)/shard_map/reshape | solution.py:74
  55.8 7.8 %copy.32 = f32[4,4,8,8,128,16]{4,5,3,0,2,1:T(8,128)} copy(f32[4,4,8,8,128,16]{4,1,5,3,2,0:T(4,128)} %bitcast.46) | data formatting | bytes 16777216 | tf_op jit(solution)/shard_map/reshape | solution.py:75
  63.6 171.8 %all-to-all-done.1 = f32[4,32,8,128,16]{3,4,2,0,1:T(8,128)} async-done(((f32[4,32,8,128,16]{3,4,2,0,1:T(8,128)}), f32[4,32,8,128,16]{3,4,2,0,1:T(8,128)}, u32[]{:S(2)}, u32[]{:S(2)}) %all-to-all-start.1) | async-done | bytes 8388640 | tf_op jit(solution)/shard_map/all_to_all | solution.py:82
  235.4 3.8 all-to-all-start
  239.7 23.1 %fusion = f32[8,512,4,512]{3,2,1,0:T(4,128)} fusion(f32[8,512,4,512]{3,2,1,0:T(4,128)} %param.5, s32[4,512]{1,0:T(4,128)S(1)} %broadcast_xor_fusion.2, s32[8,512]{1,0:T(8,128)S(1)} %broadcast_xor_fusion.1), kind=kLoop, calls=%fused_computation.1 | loop fusion | flops 25165824 | bytes 67133440 | tf_op jit(solution)/shard_map/jit(_where)/select_n | solution.py:59
  262.8 39.8 %reshape.208 = f32[4096,2048,1]{1,0,2:T(8,128)} reshape(f32[8,512,4,512]{3,2,1,0:T(4,128)} %fusion) | data formatting | bytes 67108864 | tf_op jit(solution)/shard_map/reshape | solution.py:59
  302.6 4.5 copy.27
  307.1 31.6 %fusion.10 = f32[4,128,2048]{2,1,0:T(8,128)S(1)} fusion(f32[4,128,4096]{1,2,0:T(8,128)S(1)} %bitcast.48, f32[4096,2048,1]{1,0,2:T(8,128)} %reshape.208), kind=kOutput, calls=%fused_computation.36 | convolution fusion | flops 25769803776 | bytes 46137344 | tf_op jit(solution)/shard_map/iap,pq->iaq/dot_general | solution.py:85
  338.8 2.3 fusion.6
  341.3 112.7 %all-to-all-done = f32[4,32,8,128,16]{3,4,2,0,1:T(8,128)} async-done(((f32[4,32,8,128,16]{3,4,2,0,1:T(8,128)}), f32[4,32,8,128,16]{3,4,2,0,1:T(8,128)}, u32[]{:S(2)}, u32[]{:S(2)}) %all-to-all-start) | async-done | bytes 8388640 | tf_op jit(solution)/shard_map/all_to_all | solution.py:82
  454.0 4.5 copy.23
  458.6 32.6 %fusion.9 = f32[4,128,2048]{2,1,0:T(8,128)} fusion(f32[4,128,4096]{1,2,0:T(8,128)S(1)} %bitcast.47, f32[4096,2048,1]{1,0,2:T(8,128)} %reshape.208), kind=kOutput, calls=%fused_computation.35 | convolution fusion | flops 25769803776 | bytes 46137344 | tf_op jit(solution)/shard_map/iap,pq->iaq/dot_general | solution.py:85
  491.2 1.9 copy.29
  494.6 1.6 copy.36
  496.5 34.4 %collective-permute-done = f32[2,128,4,256]{3,1,0,2:T(8,128)} collective-permute-done((f32[2,128,4,256]{3,1,0,2:T(8,128)S(1)}, f32[2,128,4,256]{3,1,0,2:T(8,128)}, u32[]{:S(2)}, u32[]{:S(2)}) %collective-permute-start) | collective-permute-done | bytes 1048608 | tf_op jit(solution)/shard_map/ppermute | solution.py:17
  530.9 1.4 bitcast_add_fusion
  532.4 1.3 collective-permute-start.1
  533.8 18.5 %collective-permute-done.1 = f32[2,128,3,256]{3,1,0,2:T(8,128)S(1)} collective-permute-done((f32[2,128,3,256]{3,1,0,2:T(8,128)S(1)}, f32[2,128,3,256]{3,1,0,2:T(8,128)S(1)}, u32[]{:S(2)}, u32[]{:S(2)}) %collective-permute-start.1) | collective-permute-done | bytes 786464 | tf_op jit(solution)/shard_map/ppermute | solution.py:32
  555.5 35.2 %collective-permute-done.3 = f32[2,128,1,256]{3,1,0,2:T(8,128)} collective-permute-done((f32[2,128,1,256]{3,1,0,2:T(8,128)S(1)}, f32[2,128,1,256]{3,1,0,2:T(8,128)}, u32[]{:S(2)}, u32[]{:S(2)}) %collective-permute-start.3) | collective-permute-done | bytes 262176 | tf_op jit(solution)/shard_map/ppermute | solution.py:32
  591.9 2.2 pad_maximum_fusion
  (32 shorter events, 9.9 us)
Async XLA Ops:
  38.4 197.0 %all-to-all-start.1 = ((f32[4,32,8,128,16]{3,4,2,0,1:T(8,128)}), f32[4,32,8,128,16]{3,4,2,0,1:T(8,128)}, u32[]{:S(2)}, u32[]{:S(2)}) async-start(f32[4,32,8,128,16]{3,4,2,0,1:T(8,128)} %bitcast.44), calls=%async_computation.2 | async-start | bytes 16777216 | tf_op jit(solution)/shard_map/all_to_all | solution.py:82
  235.4 4.1 copy-start.2
  235.4 4.2 copy-start.1
  235.4 218.6 %all-to-all-start = ((f32[4,32,8,128,16]{3,4,2,0,1:T(8,128)}), f32[4,32,8,128,16]{3,4,2,0,1:T(8,128)}, u32[]{:S(2)}, u32[]{:S(2)}) async-start(f32[4,32,8,128,16]{3,4,2,0,1:T(8,128)} %bitcast.43), calls=%async_computation | async-start | bytes 16777216 | tf_op jit(solution)/shard_map/all_to_all | solution.py:82
  239.2 352.6 %reduce-scatter.5.cloned.1.call-start = ((), (), s32[]{:S(2)}) async-start(), calls=%async_computation.5 | async-start | bytes 2359296 | tf_op jit(solution)/shard_map/reduce_scatter | solution.py:98
  341.0 250.8 %reduce-scatter.3.cloned.1.call-start = ((), (), s32[]{:S(2)}) async-start(), calls=%async_computation.4 | async-start | bytes 4718592 | tf_op jit(solution)/shard_map/reduce_scatter | solution.py:105
  496.4 34.5 %collective-permute-start = (f32[2,128,4,256]{3,1,0,2:T(8,128)S(1)}, f32[2,128,4,256]{3,1,0,2:T(8,128)}, u32[]{:S(2)}, u32[]{:S(2)}) collective-permute-start(f32[2,128,4,256]{3,1,0,2:T(8,128)S(1)} %select_bitcast_fusion), channel_id=1, source_target_pairs={{0,1},{1,0},{2,3},{3,2},{4,5},{5,4},{6,7},{7,6},{8,9},{9,8},{10,11... | collective-permute-start | bytes 3145736 | tf_op jit(solution)/shard_map/ppermute | solution.py:17
  532.4 19.8 %collective-permute-start.1 = (f32[2,128,3,256]{3,1,0,2:T(8,128)S(1)}, f32[2,128,3,256]{3,1,0,2:T(8,128)S(1)}, u32[]{:S(2)}, u32[]{:S(2)}) collective-permute-start(f32[2,128,3,256]{3,1,0,2:T(8,128)S(1)} %slice_select_fusion.2), channel_id=1, source_target_pairs={{0,2},{6,4},{1,3},{7,5},{8,10},{14,12},{9,11},{15,13},{16,18},{22,... | collective-permute-start | bytes 2359304 | tf_op jit(solution)/shard_map/ppermute | solution.py:32
  552.5 0.7 collective-permute-start.2
  553.3 0.8 copy-start
  554.2 36.5 %collective-permute-start.3 = (f32[2,128,1,256]{3,1,0,2:T(8,128)S(1)}, f32[2,128,1,256]{3,1,0,2:T(8,128)}, u32[]{:S(2)}, u32[]{:S(2)}) collective-permute-start(f32[2,128,1,256]{3,1,0,2:T(8,128)S(1)} %fusion.2), channel_id=1, source_target_pairs={{4,6},{2,0},{5,7},{3,1},{12,14},{10,8},{13,15},{11,9},{20,22},{18,... | collective-permute-start | bytes 786440 | tf_op jit(solution)/shard_map/ppermute | solution.py:32
Sparse Core Ops, SparseCore 0:
  341.2 108.7 reduce-scatter.4
  491.3 96.6 reduce-scatter.2

commit v10 on v8

--- a/solution.py
+++ b/solution.py
@@ -60,7 +60,7 @@
         k_local * virt_count, column_slab * virt_count
     )
 
-    first = min(slab_rows, (slab_rows * 5 + 7) // 8)
+    first = min(slab_rows, (slab_rows + 1) // 2)
     bounds = [(0, first)] + ([(first, slab_rows)] if first < slab_rows else [])
     chunks = len(bounds)
     exchanged = []
@@ -85,8 +85,10 @@
             lax.all_to_all(grouped, ("row", "col"), split_axis=1, concat_axis=4, tiled=True)
         )
     results = []
-    for items in exchanged:
+    for step, items in enumerate(exchanged):
         rows = items.shape[0]
+        if step >= 1:
+            items, results[step - 1] = lax.optimization_barrier((items, results[step - 1]))
         blocks = jnp.transpose(items.reshape(rows, k_local, a_local, virt_count), (0, 2, 1, 3))
         blocks = blocks.reshape(rows, a_local, k_local * virt_count)
         partial_value = jnp.einsum(
@@ -97,7 +99,10 @@
             preferred_element_type=jnp.float32,
         )
         flat = partial_value.reshape(rows, a_local, column_slab * virt_count)
-        results.append(lax.psum_scatter(flat, "col", scatter_dimension=2, tiled=True))
+        if step < chunks - 1 and col_count % 4 == 0:
+            results.append(scatter_sum(flat, col_count, col_place))
+        else:
+            results.append(lax.psum_scatter(flat, "col", scatter_dimension=2, tiled=True))
     return jnp.concatenate(results, axis=0)
 
 

time: 605 us -> 659 us (1.089)
  waiting for transfers between devices: 388 us -> 325 us
  starting transfers between devices: 11.5 us -> 60.4 us
  local copies, waits for them, and re-layouts: 82.4 us -> 119 us
  matrix products: 67.8 us -> 90.8 us
  other arithmetic: 41.1 us -> 48.6 us
    all_to_all x2, waiting for transfers between devices: 307 us -> 119 us  [per_device(): lax.all_to_all(grouped, ('row', 'col'), split_axis=1, concat_axis=4, tile...]
    ppermute x0 -> x4, waiting for transfers between devices: none -> 118 us  [the longest x3 69.2 us: scatter_sum(): got = lax.ppermute(payload, 'col', links)]
    ppermute x0 -> x4, starting transfers between devices: none -> 49.2 us  [the longest x3 47.5 us: scatter_sum(): got = lax.ppermute(payload, 'col', links)]
    dot_general x0 -> x1, local copies, waits for them, and re-layouts: none -> 31.1 us  [per_device(): jnp.einsum('iap,pq->iaq', blocks, masked_ints, precision=lax.Precision.HI...]
    dot_general x2, matrix products: 67.8 us -> 90.8 us  [per_device(): jnp.einsum('iap,pq->iaq', blocks, masked_ints, precision=lax.Precision.HI...]
    reduce_scatter x2 -> x1, waiting for transfers between devices: 80.9 us -> 88.8 us  [per_device(): lax.psum_scatter(flat, 'col', scatter_dimension=2, tiled=True)]
    unnamed x7 -> x17, local copies, waits for them, and re-layouts: 29.9 us -> 34.2 us
    select_n x2 -> x1, other arithmetic: 14 us -> 11.1 us  [per_device(): masked_amps = jnp.where(amp_sym == 0, amps, 0.0)]
  transfers between devices with their start and end apart: 4 -> 7, of which waited for: 4 -> 5; matrix products, arithmetic and copies ran while one was open for 24% -> 26% of each run, Pallas kernels for 0% -> 0%
where the time goes in v10:
time: 659 us; the launch traced here: 658 us
  waiting for transfers between devices  325 us (49%)
  local copies, waits for them, and re-layouts  119 us (18%)
  matrix products  90.8 us (14%)
  starting transfers between devices  60.4 us (9%)
  other arithmetic  48.6 us (7%)
  between operations  13.6 us (2%)
    all_to_all x2, waiting for transfers between devices, per_device(): lax.all_to_all(grouped, ('row', 'col'), split_axis=1, concat_axis=4, tile...  119 us
    dot_general x2, matrix products, per_device(): jnp.einsum('iap,pq->iaq', blocks, masked_ints, precision=lax.Precision.HI...  90.8 us
    reduce_scatter x1, waiting for transfers between devices, per_device(): lax.psum_scatter(flat, 'col', scatter_dimension=2, tiled=True)  88.8 us
    ppermute x3, waiting for transfers between devices, scatter_sum(): got = lax.ppermute(payload, 'col', links)  69.2 us
    ppermute x1, waiting for transfers between devices, scatter_sum(): line_sum = keep + lax.ppermute(give, 'col', swap)  48.7 us
    ppermute x3, starting transfers between devices, scatter_sum(): got = lax.ppermute(payload, 'col', links)  47.5 us
    unnamed x17, local copies, waits for them, and re-layouts  34.2 us
    dot_general x1, local copies, waits for them, and re-layouts, per_device(): jnp.einsum('iap,pq->iaq', blocks, masked_ints, precision=lax.Precision.HI...  31.1 us
  transfers between devices with their start and end apart: 7, of which 5 were waited for; matrix products, arithmetic and copies ran while one was open for 26% of the time, Pallas kernels for 0%

profile of v10, /device:TPU:0, one launch (start us, length us, event | category | flops | bytes accessed | tf_op | source)
XLA Modules:
  0.0 657.6 jit_solution(15978463351905871320)
XLA Ops:
  9.6 11.1 %slice_select_fusion = (f32[4,64,512,16]{2,3,1,0:T(8,128)}, f32[4,64,512,16]{2,3,1,0:T(8,128)}) fusion(f32[8,64,512,16]{2,3,1,0:T(8,128)} %param.4, s32[4,64]{1,0:T(4,128)S(1)} %get-tuple-element.21, s32[512,16]{0,1:T(8,128)S(1)} %broadcast_xor_fusion, s32[4,64]{1,0:T(4,128)S(1)} %get-tuple-element.22), kind=kLoop, calls=%fused_computation.4 | loop fusion | flops 12582912 | bytes 33589248 | tf_op jit(solution)/shard_map/jit(_where)/select_n | solution.py:75
  20.6 10.0 %reshape.195 = f32[4,8,8,4,128,16]{4,3,5,2,1,0:T(4,128)} reshape(f32[4,64,512,16]{2,3,1,0:T(8,128)} %get-tuple-element.15) | data formatting | bytes 16777216 | tf_op jit(solution)/shard_map/reshape | solution.py:76
  30.6 7.9 %copy.45 = f32[4,4,8,8,128,16]{4,5,3,0,2,1:T(8,128)} copy(f32[4,4,8,8,128,16]{4,1,5,3,2,0:T(4,128)} %bitcast.76) | data formatting | bytes 16777216 | tf_op jit(solution)/shard_map/reshape | solution.py:77
  38.4 7.4 %all-to-all-start = ((f32[4,32,8,128,16]{3,4,2,0,1:T(8,128)}), f32[4,32,8,128,16]{3,4,2,0,1:T(8,128)}, u32[]{:S(2)}, u32[]{:S(2)}) async-start(f32[4,32,8,128,16]{3,4,2,0,1:T(8,128)} %bitcast.74), calls=%async_computation | async-start | bytes 16777216 | tf_op jit(solution)/shard_map/all_to_all | solution.py:85
  45.9 9.9 %reshape.193 = f32[4,8,8,4,128,16]{4,3,5,2,1,0:T(4,128)} reshape(f32[4,64,512,16]{2,3,1,0:T(8,128)} %get-tuple-element.16) | data formatting | bytes 16777216 | tf_op jit(solution)/shard_map/reshape | solution.py:76
  55.8 7.8 %copy.30 = f32[4,4,8,8,128,16]{4,5,3,2,1,0:T(8,128)} copy(f32[4,4,8,8,128,16]{4,1,5,3,2,0:T(4,128)} %bitcast.77) | data formatting | bytes 16777216 | tf_op jit(solution)/shard_map/transpose | solution.py:77
  63.8 23.1 %fusion.2 = f32[8,512,4,512]{3,2,1,0:T(4,128)} fusion(f32[8,512,4,512]{3,2,1,0:T(4,128)} %param.5, s32[4,512]{1,0:T(4,128)S(1)} %broadcast_xor_fusion.2, s32[8,512]{1,0:T(8,128)S(1)} %broadcast_xor_fusion.1), kind=kLoop, calls=%fused_computation.3 | loop fusion | flops 25165824 | bytes 67133440 | tf_op jit(solution)/shard_map/jit(_where)/select_n | solution.py:59
  86.9 29.9 %copy.50 = f32[512,8,4,512]{3,1,2,0:T(8,128)} copy(f32[512,8,4,512]{3,2,1,0:T(4,128)} %bitcast.70) | data formatting | bytes 67108864
  116.8 118.6 %all-to-all-done = f32[4,32,8,128,16]{3,4,2,0,1:T(8,128)} async-done(((f32[4,32,8,128,16]{3,4,2,0,1:T(8,128)}), f32[4,32,8,128,16]{3,4,2,0,1:T(8,128)}, u32[]{:S(2)}, u32[]{:S(2)}) %all-to-all-start) | async-done | bytes 8388640 | tf_op jit(solution)/shard_map/all_to_all | solution.py:85
  235.4 8.0 %copy.33 = f32[4,32,8,128,16]{3,4,1,2,0:T(8,128)} copy(f32[4,32,8,128,16]{3,4,2,0,1:T(8,128)} %all-to-all-done) | data formatting | bytes 16777216 | tf_op jit(solution)/shard_map/all_to_all | solution.py:85
  243.4 3.9 copy.34
  247.4 3.7 all-to-all-start.1
  251.1 31.1 %copy.48 = f32[2048,4096]{1,0:T(8,128)} copy(f32[2048,4096]{0,1:T(8,128)} %bitcast.71) | data formatting | bytes 67108864 | tf_op jit(solution)/shard_map/iap,pq->iaq/dot_general | solution.py:94
  282.2 58.0 %fusion.11 = f32[4,128,4,2,256]{4,1,3,2,0:T(8,128)S(1)} fusion(f32[4,128,4096,1,1]{1,2,4,3,0:T(8,128)} %bitcast.78, f32[4,2,256,4096,1]{3,2,1,0,4:T(8,128)} %bitcast.73), kind=kOutput, calls=%fused_computation.37 | convolution fusion | flops 25769803776 | bytes 46137344 | tf_op jit(solution)/shard_map/iap,pq->iaq/dot_general | solution.py:94
  344.2 48.7 %collective-permute-done = f32[4,128,4,256]{3,1,2,0:T(8,128)} collective-permute-done((f32[4,128,4,256]{3,1,2,0:T(8,128)S(1)}, f32[4,128,4,256]{3,1,2,0:T(8,128)}, u32[]{:S(2)}, u32[]{:S(2)}) %collective-permute-start) | collective-permute-done | bytes 2097184 | tf_op jit(solution)/shard_map/ppermute | solution.py:17
  392.9 3.3 fusion.4
  397.6 45.5 %collective-permute-start.1 = (f32[4,128,3,256]{3,1,2,0:T(8,128)}, f32[4,128,3,256]{3,1,2,0:T(8,128)}, u32[]{:S(2)}, u32[]{:S(2)}) collective-permute-start(f32[4,128,3,256]{3,1,2,0:T(8,128)} %slice_select_fusion.2), channel_id=1, source_target_pairs={{0,2},{6,4},{1,3},{7,5},{8,10},{14,12},{9,11},{15,13},{16,18},{22,... | collective-permute-start | bytes 4718600 | tf_op jit(solution)/shard_map/ppermute | solution.py:32
  443.1 32.3 %collective-permute-done.1 = f32[4,128,3,256]{3,1,2,0:T(8,128)} collective-permute-done((f32[4,128,3,256]{3,1,2,0:T(8,128)}, f32[4,128,3,256]{3,1,2,0:T(8,128)}, u32[]{:S(2)}, u32[]{:S(2)}) %collective-permute-start.1) | collective-permute-done | bytes 1572896 | tf_op jit(solution)/shard_map/ppermute | solution.py:32
  483.0 36.9 %collective-permute-done.3 = f32[4,128,1,256]{3,1,2,0:T(8,128)} collective-permute-done((f32[4,128,1,256]{3,1,2,0:T(8,128)}, f32[4,128,1,256]{3,1,2,0:T(8,128)}, u32[]{:S(2)}, u32[]{:S(2)}) %collective-permute-start.3) | collective-permute-done | bytes 524320 | tf_op jit(solution)/shard_map/ppermute | solution.py:32
  519.9 2.5 fusion.9
  522.5 4.5 copy.35
  527.0 32.8 %fusion = f32[4,128,2048]{2,1,0:T(8,128)} fusion(f32[4,128,4096]{1,2,0:T(8,128)S(1)} %bitcast.79, f32[4096,2048]{1,0:T(8,128)} %bitcast.72), kind=kOutput, calls=%fused_computation | convolution fusion | flops 25769803776 | bytes 46137344 | tf_op jit(solution)/shard_map/iap,pq->iaq/dot_general | solution.py:94
  559.8 88.8 %reduce-scatter.2.cloned.1.call-done = f32[4,128,256]{2,1,0:T(8,128)} async-done(((f32[4,128,2048]{2,1,0:T(8,128)}), f32[4,128,256]{2,1,0:T(8,128)}) %reduce-scatter.2.cloned.1.call-update) | async-done | bytes 524304 | tf_op jit(solution)/shard_map/reduce_scatter | solution.py:105
  648.6 2.1 pad_maximum_fusion
  (36 shorter events, 16.2 us)
Async XLA Ops:
  38.4 197.0 %all-to-all-start = ((f32[4,32,8,128,16]{3,4,2,0,1:T(8,128)}), f32[4,32,8,128,16]{3,4,2,0,1:T(8,128)}, u32[]{:S(2)}, u32[]{:S(2)}) async-start(f32[4,32,8,128,16]{3,4,2,0,1:T(8,128)} %bitcast.74), calls=%async_computation | async-start | bytes 16777216 | tf_op jit(solution)/shard_map/all_to_all | solution.py:85
  55.8 7.8 %copy-start.7 = (s32[64]{0:T(128)S(1)}, s32[64]{0:T(128)}, u32[]{:S(2)}) copy-start(s32[64]{0:T(128)} %param.6) | copy-start | bytes 772
  55.8 7.9 %copy-start.6 = (s32[512]{0:T(512)S(1)}, s32[512]{0:T(512)}, u32[]{:S(2)}) copy-start(s32[512]{0:T(512)} %param.7) | copy-start | bytes 6148
  235.4 8.0 %copy-start = (f32[4,4,8,8,128,16]{4,5,3,2,1,0:T(8,128)S(1)}, f32[4,4,8,8,128,16]{4,5,3,2,1,0:T(8,128)}, u32[]{:S(2)}) copy-start(f32[4,4,8,8,128,16]{4,5,3,2,1,0:T(8,128)} %copy.30) | copy-start | bytes 25165828
  247.4 275.1 %all-to-all-start.1 = ((f32[4,32,8,128,16]{3,4,2,0,1:T(8,128)}), f32[4,32,8,128,16]{3,4,2,0,1:T(8,128)}, u32[]{:S(2)}, u32[]{:S(2)}) async-start(f32[4,32,8,128,16]{3,4,2,0,1:T(8,128)} %copy.34), calls=%async_computation.1 | async-start | bytes 16777216 | tf_op jit(solution)/shard_map/all_to_all | solution.py:85
  251.1 397.6 %reduce-scatter.2.cloned.1.call-start = ((), (), s32[]{:S(2)}) async-start(), calls=%async_computation.3 | async-start | bytes 4718592 | tf_op jit(solution)/shard_map/reduce_scatter | solution.py:105
  340.2 2.1 copy-start.1
  342.6 50.4 %collective-permute-start = (f32[4,128,4,256]{3,1,2,0:T(8,128)S(1)}, f32[4,128,4,256]{3,1,2,0:T(8,128)}, u32[]{:S(2)}, u32[]{:S(2)}) collective-permute-start(f32[4,128,4,256]{3,1,2,0:T(8,128)S(1)} %select_bitcast_fusion), channel_id=1, source_target_pairs={{0,1},{1,0},{2,3},{3,2},{4,5},{5,4},{6,7},{7,6},{8,9},{9,8},{10,11... | collective-permute-start | bytes 6291464 | tf_op jit(solution)/shard_map/ppermute | solution.py:17
  397.6 77.8 %collective-permute-start.1 = (f32[4,128,3,256]{3,1,2,0:T(8,128)}, f32[4,128,3,256]{3,1,2,0:T(8,128)}, u32[]{:S(2)}, u32[]{:S(2)}) collective-permute-start(f32[4,128,3,256]{3,1,2,0:T(8,128)} %slice_select_fusion.2), channel_id=1, source_target_pairs={{0,2},{6,4},{1,3},{7,5},{8,10},{14,12},{9,11},{15,13},{16,18},{22,... | collective-permute-start | bytes 4718600 | tf_op jit(solution)/shard_map/ppermute | solution.py:32
  477.2 1.1 copy-start.2
  477.2 1.6 copy-start.3
  478.8 0.7 collective-permute-start.2
  479.8 1.0 copy-start.4
  481.7 38.2 %collective-permute-start.3 = (f32[4,128,1,256]{3,1,2,0:T(8,128)}, f32[4,128,1,256]{3,1,2,0:T(8,128)}, u32[]{:S(2)}, u32[]{:S(2)}) collective-permute-start(f32[4,128,1,256]{3,1,2,0:T(8,128)} %fusion.6), channel_id=1, source_target_pairs={{4,6},{2,0},{5,7},{3,1},{12,14},{10,8},{13,15},{11,9},{20,22},{18,... | collective-permute-start | bytes 1572872 | tf_op jit(solution)/shard_map/ppermute | solution.py:32
  527.0 121.6 %copy-start.5 = (f32[4,128,256]{2,1,0:T(8,128)S(1)}, f32[4,128,256]{2,1,0:T(8,128)}, u32[]{:S(2)}) copy-start(f32[4,128,256]{2,1,0:T(8,128)} %fusion.9) | copy-start | bytes 1572868
Sparse Core Ops, SparseCore 0:
  559.9 88.6 reduce-scatter.1

commit v11 on v7

--- a/solution.py
+++ b/solution.py
@@ -60,13 +60,16 @@
         k_local * virt_count, column_slab * virt_count
     )
 
-    chunks = 2 if slab_rows % 2 == 0 else 1
-    rows = slab_rows // chunks
+    first = (slab_rows * 3 + 7) // 8
+    second = min(slab_rows, 2 * first)
+    bounds = [(lo, hi) for lo, hi in ((0, first), (first, second), (second, slab_rows)) if hi > lo]
+    chunks = len(bounds)
     results = []
-    for step in range(chunks):
-        amps = amplitudes[step * rows:(step + 1) * rows]
+    for step, (lo, hi) in enumerate(bounds):
+        rows = hi - lo
+        amps = amplitudes[lo:hi]
         amp_sym = (
-            slab_irrep[step * rows:(step + 1) * rows, None, None, None]
+            slab_irrep[lo:hi, None, None, None]
             ^ occ_irrep[None, :, None, None]
             ^ (virt_irrep[None, None, :, None] ^ c_irrep[None, None, None, :])
         )

time: 596 us -> 615 us (1.032)
  local copies, waits for them, and re-layouts: 86 us -> 129 us
  waiting for transfers between devices: 379 us -> 342 us
  matrix products: 65.8 us -> 73.1 us
    all_to_all x2 -> x3, waiting for transfers between devices: 294 us -> 163 us  [per_device(): lax.all_to_all(grouped, ('row', 'col'), split_axis=1, concat_axis=4, tile...]
    reduce_scatter x2 -> x3, waiting for transfers between devices: 84.6 us -> 179 us  [per_device(): lax.psum_scatter(flat, 'col', scatter_dimension=2, tiled=True)]
    unnamed x4 -> x9, local copies, waits for them, and re-layouts: 0.01 us -> 30.2 us
    transpose x0 -> x2, local copies, waits for them, and re-layouts: none -> 11 us  [per_device(): jnp.transpose(grouped, (0, 3, 1, 2, 4, 5))]
    reshape x2 -> x1, local copies, waits for them, and re-layouts: 15.6 us -> 6.33 us  [per_device(): jnp.transpose(grouped, (0, 3, 1, 2, 4, 5))]
    optimization_barrier x0 -> x2, local copies, waits for them, and re-layouts: none -> 8.08 us  [the longest x1 4.75 us: per_device(): lax.optimization_barrier((grouped, results[step - 2]))]
    dot_general x2 -> x3, matrix products: 65.8 us -> 73.1 us  [per_device(): jnp.einsum('iap,pq->iaq', blocks, masked_ints, precision=lax.Precision.HI...]
    all_to_all x2 -> x3, starting transfers between devices: 11.2 us -> 14.9 us  [per_device(): lax.all_to_all(grouped, ('row', 'col'), split_axis=1, concat_axis=4, tile...]
  transfers between devices with their start and end apart: 4 -> 6, of which waited for: 3 -> 5; matrix products, arithmetic and copies ran while one was open for 26% -> 35% of each run, Pallas kernels for 0% -> 0%
where the time goes in v11:
time: 615 us; the launch traced here: 613 us
  waiting for transfers between devices  342 us (56%)
  local copies, waits for them, and re-layouts  129 us (21%)
  matrix products  73.1 us (12%)
  other arithmetic  39.7 us (6%)
  starting transfers between devices  15.4 us (3%)
  between operations  13.2 us (2%)
    reduce_scatter x3, waiting for transfers between devices, per_device(): lax.psum_scatter(flat, 'col', scatter_dimension=2, tiled=True)  179 us
    all_to_all x3, waiting for transfers between devices, per_device(): lax.all_to_all(grouped, ('row', 'col'), split_axis=1, concat_axis=4, tile...  163 us
    dot_general x3, matrix products, per_device(): jnp.einsum('iap,pq->iaq', blocks, masked_ints, precision=lax.Precision.HI...  73.1 us
    reshape x1, local copies, waits for them, and re-layouts, per_device(): jnp.where(int_sym == 0, cycle_integrals, 0.0)  39.8 us
    unnamed x9, local copies, waits for them, and re-layouts  30.2 us
    select_n x1, other arithmetic, per_device(): jnp.where(int_sym == 0, cycle_integrals, 0.0)  23.1 us
    reshape x3, local copies, waits for them, and re-layouts, per_device(): masked_amps.reshape(rows, col_count, k_local, row_count, a_local, c_local)  20.6 us
    all_to_all x3, starting transfers between devices, per_device(): lax.all_to_all(grouped, ('row', 'col'), split_axis=1, concat_axis=4, tile...  14.9 us
  transfers between devices with their start and end apart: 6, of which 5 were waited for; matrix products, arithmetic and copies ran while one was open for 35% of the time, Pallas kernels for 0%

profile of v11, /device:TPU:0, one launch (start us, length us, event | category | flops | bytes accessed | tf_op | source)
XLA Modules:
  0.0 612.5 jit_solution(4722578371152349013)
XLA Ops:
  9.6 8.2 %slice_select_fusion = (f32[3,64,512,16]{2,3,1,0:T(8,128)}, f32[3,64,512,16]{2,3,1,0:T(8,128)}) fusion(f32[8,64,512,16]{2,3,1,0:T(8,128)} %param.4, s32[3,64]{1,0:T(4,128)S(1)} %get-tuple-element.15, s32[512,16]{0,1:T(8,128)S(1)} %broadcast_xor_fusion, s32[3,64]{1,0:T(4,128)S(1)} %get-tuple-element.16), kind=kLoop, calls=%fused_computation.6 | loop fusion | flops 9437184 | bytes 25200128 | tf_op jit(solution)/shard_map/jit(_where)/select_n | solution.py:76
  17.8 7.6 %reshape.232 = f32[3,8,8,4,128,16]{4,3,5,2,1,0:T(4,128)} reshape(f32[3,64,512,16]{2,3,1,0:T(8,128)} %get-tuple-element.14) | data formatting | bytes 12582912 | tf_op jit(solution)/shard_map/reshape | solution.py:77
  25.4 6.3 %copy.32 = f32[3,4,8,8,128,16]{4,5,3,0,2,1:T(8,128)} copy(f32[3,4,8,8,128,16]{4,1,5,3,2,0:T(4,128)} %bitcast.64) | data formatting | bytes 12582912 | tf_op jit(solution)/shard_map/reshape | solution.py:78
  31.7 7.4 %all-to-all-start = ((f32[3,32,8,128,16]{3,4,2,0,1:T(8,128)}), f32[3,32,8,128,16]{3,4,2,0,1:T(8,128)}, u32[]{:S(2)}, u32[]{:S(2)}) async-start(f32[3,32,8,128,16]{3,4,2,0,1:T(8,128)} %bitcast.62), calls=%async_computation | async-start | bytes 12582912 | tf_op jit(solution)/shard_map/all_to_all | solution.py:85
  39.2 7.6 %reshape.237 = f32[3,8,8,4,128,16]{4,3,5,2,1,0:T(4,128)} reshape(f32[3,64,512,16]{2,3,1,0:T(8,128)} %get-tuple-element.13) | data formatting | bytes 12582912 | tf_op jit(solution)/shard_map/reshape | solution.py:77
  46.8 6.3 %copy.25 = f32[3,4,8,8,128,16]{4,5,3,2,1,0:T(8,128)} copy(f32[3,4,8,8,128,16]{4,1,5,3,2,0:T(4,128)} %bitcast.65) | data formatting | bytes 12582912 | tf_op jit(solution)/shard_map/transpose | solution.py:78
  53.3 23.1 %fusion.4 = f32[8,512,4,512]{3,2,1,0:T(4,128)} fusion(f32[8,512,4,512]{3,2,1,0:T(4,128)} %param.5, s32[4,512]{1,0:T(4,128)S(1)} %broadcast_xor_fusion.2, s32[8,512]{1,0:T(8,128)S(1)} %broadcast_xor_fusion.1), kind=kLoop, calls=%fused_computation.5 | loop fusion | flops 25165824 | bytes 67133440 | tf_op jit(solution)/shard_map/jit(_where)/select_n | solution.py:59
  76.3 30.1 %copy.36 = f32[512,8,4,512]{3,1,2,0:T(8,128)} copy(f32[512,8,4,512]{3,2,1,0:T(4,128)} %bitcast.59) | data formatting | bytes 67108864
  109.8 72.2 %all-to-all-done = f32[3,32,8,128,16]{3,4,2,0,1:T(8,128)} async-done(((f32[3,32,8,128,16]{3,4,2,0,1:T(8,128)}), f32[3,32,8,128,16]{3,4,2,0,1:T(8,128)}, u32[]{:S(2)}, u32[]{:S(2)}) %all-to-all-start) | async-done | bytes 6291488 | tf_op jit(solution)/shard_map/all_to_all | solution.py:85
  182.0 3.6 all-to-all-start.1
  185.9 39.8 %reshape.243 = f32[4096,2048,1]{1,0,2:T(8,128)} reshape(f32[8,512,4,512]{3,2,1,0:T(4,128)} %fusion.4) | data formatting | bytes 67108864 | tf_op jit(solution)/shard_map/reshape | solution.py:59
  229.1 26.6 %fusion.6 = f32[3,128,2048]{2,1,0:T(8,128)} fusion(f32[3,128,4096]{1,2,0:T(8,128)S(1)} %bitcast.69, f32[4096,2048,1]{1,0,2:T(8,128)} %reshape.243), kind=kOutput, calls=%fused_computation.20 | convolution fusion | flops 19327352832 | bytes 42991616 | tf_op jit(solution)/shard_map/iap,pq->iaq/dot_general | solution.py:88
  255.9 4.6 slice_select_fusion.2
  260.5 5.4 reshape.230
  266.0 4.7 copy.20
  270.7 106.9 %reduce-scatter.4.cloned.1.call-done = f32[3,128,256]{2,1,0:T(8,128)} async-done(((f32[3,128,2048]{2,1,0:T(8,128)}), f32[3,128,256]{2,1,0:T(8,128)}) %reduce-scatter.4.cloned.1.call-update) | async-done | bytes 393232 | tf_op jit(solution)/shard_map/reduce_scatter | solution.py:96
  377.5 4.8 copy.29
  382.3 3.8 all-to-all-start.2
  386.4 3.4 copy.27
  389.9 26.6 %fusion.2 = f32[3,128,2048]{2,1,0:T(8,128)} fusion(f32[3,128,4096]{1,2,0:T(8,128)S(1)} %bitcast.70, f32[4096,2048]{1,0:T(8,128)} %bitcast.60), kind=kOutput, calls=%fused_computation.2 | convolution fusion | flops 19327352832 | bytes 42991616 | tf_op jit(solution)/shard_map/iap,pq->iaq/dot_general | solution.py:88
  416.6 90.8 %all-to-all-done.2 = f32[2,32,8,128,16]{3,4,2,0,1:T(8,128)} async-done(((f32[2,32,8,128,16]{3,4,2,0,1:T(8,128)}), f32[2,32,8,128,16]{3,4,2,0,1:T(8,128)}, u32[]{:S(2)}, u32[]{:S(2)}) %all-to-all-start.2) | async-done | bytes 4194336 | tf_op jit(solution)/shard_map/all_to_all | solution.py:85
  507.4 4.7 copy.30
  512.1 19.8 %fusion = f32[2,128,2048]{2,1,0:T(8,128)} fusion(f32[2,128,4096]{1,2,0:T(8,128)} %bitcast.66, f32[4096,2048]{1,0:T(8,128)} %bitcast.61), kind=kOutput, calls=%fused_computation | convolution fusion | flops 12884901888 | bytes 39845888 | tf_op jit(solution)/shard_map/iap,pq->iaq/dot_general | solution.py:88
  533.0 70.9 %reduce-scatter.8.cloned.1.call-done = f32[2,128,256]{2,1,0:T(8,128)} async-done(((f32[2,128,2048]{2,1,0:T(8,128)}), f32[2,128,256]{2,1,0:T(8,128)}) %reduce-scatter.8.cloned.1.call-update) | async-done | bytes 262160 | tf_op jit(solution)/shard_map/reduce_scatter | solution.py:96
  (28 shorter events, 13.9 us)
Async XLA Ops:
  31.7 7.4 %copy-start.3 = (s32[64]{0:T(128)S(1)}, s32[64]{0:T(128)}, u32[]{:S(2)}) copy-start(s32[64]{0:T(128)} %param.6) | copy-start | bytes 772
  31.7 150.3 %all-to-all-start = ((f32[3,32,8,128,16]{3,4,2,0,1:T(8,128)}), f32[3,32,8,128,16]{3,4,2,0,1:T(8,128)}, u32[]{:S(2)}, u32[]{:S(2)}) async-start(f32[3,32,8,128,16]{3,4,2,0,1:T(8,128)} %bitcast.62), calls=%async_computation | async-start | bytes 12582912 | tf_op jit(solution)/shard_map/all_to_all | solution.py:85
  46.8 6.3 %copy-start.2 = (s32[512]{0:T(512)S(1)}, s32[512]{0:T(512)}, u32[]{:S(2)}) copy-start(s32[512]{0:T(512)} %param.7) | copy-start | bytes 6148
  76.3 30.1 %copy-start = (f32[3,4,8,8,128,16]{4,5,3,2,1,0:T(8,128)S(1)}, f32[3,4,8,8,128,16]{4,5,3,2,1,0:T(8,128)}, u32[]{:S(2)}) copy-start(f32[3,4,8,8,128,16]{4,5,3,2,1,0:T(8,128)} %copy.25) | copy-start | bytes 18874372
  182.0 200.3 %all-to-all-start.1 = ((f32[3,32,8,128,16]{3,4,2,0,1:T(8,128)}), f32[3,32,8,128,16]{3,4,2,0,1:T(8,128)}, u32[]{:S(2)}, u32[]{:S(2)}) async-start(f32[3,32,8,128,16]{3,4,2,0,1:T(8,128)} %copy.26), calls=%async_computation.2 | async-start | bytes 12582912 | tf_op jit(solution)/shard_map/all_to_all | solution.py:85
  185.6 191.9 %reduce-scatter.4.cloned.1.call-start = ((), (), s32[]{:S(2)}) async-start(), calls=%async_computation.6 | async-start | bytes 3538944 | tf_op jit(solution)/shard_map/reduce_scatter | solution.py:96
  382.3 125.1 %all-to-all-start.2 = ((f32[2,32,8,128,16]{3,4,2,0,1:T(8,128)}), f32[2,32,8,128,16]{3,4,2,0,1:T(8,128)}, u32[]{:S(2)}, u32[]{:S(2)}) async-start(f32[2,32,8,128,16]{3,4,2,0,1:T(8,128)} %copy.29), calls=%async_computation.4 | async-start | bytes 8388608 | tf_op jit(solution)/shard_map/all_to_all | solution.py:85
  386.1 146.8 %reduce-scatter.6.cloned.1.call-start = ((), (), s32[]{:S(2)}) async-start(), calls=%async_computation.7 | async-start | bytes 3538944 | tf_op jit(solution)/shard_map/reduce_scatter | solution.py:96
  416.5 187.4 %reduce-scatter.8.cloned.1.call-start = ((), (), s32[]{:S(2)}) async-start(), calls=%async_computation.8 | async-start | bytes 2359296 | tf_op jit(solution)/shard_map/reduce_scatter | solution.py:96
  512.1 91.8 %copy-start.1 = (f32[3,128,256]{2,1,0:T(8,128)S(1)}, f32[3,128,256]{2,1,0:T(8,128)}, u32[]{:S(2)}) copy-start(f32[3,128,256]{2,1,0:T(8,128)} %reduce-scatter.4.cloned.1.call-done) | copy-start | bytes 1179652
Sparse Core Ops, SparseCore 0:
  255.9 121.6 reduce-scatter.3
  416.6 116.2 reduce-scatter.5
  536.5 67.3 reduce-scatter.7

commit v12 on v7

--- a/solution.py
+++ b/solution.py
@@ -46,9 +46,7 @@
     col_place = lax.axis_index("col")
     row_place = lax.axis_index("row")
     k_irrep = lax.dynamic_slice_in_dim(occ_irrep, col_place * k_local, k_local)
-    c_irrep = lax.dynamic_slice_in_dim(
-        virt_irrep, (row_place * col_count + col_place) * c_local, c_local
-    )
+    a_irrep = lax.dynamic_slice_in_dim(virt_irrep, row_place * a_local, a_local)
     slab_irrep = occ_irrep[:slab_rows]
     column_irrep = occ_irrep[:column_slab]
     int_sym = (
@@ -63,15 +61,10 @@
     chunks = 2 if slab_rows % 2 == 0 else 1
     rows = slab_rows // chunks
     results = []
+    flats = []
     for step in range(chunks):
         amps = amplitudes[step * rows:(step + 1) * rows]
-        amp_sym = (
-            slab_irrep[step * rows:(step + 1) * rows, None, None, None]
-            ^ occ_irrep[None, :, None, None]
-            ^ (virt_irrep[None, None, :, None] ^ c_irrep[None, None, None, :])
-        )
-        masked_amps = jnp.where(amp_sym == 0, amps, 0.0)
-        grouped = masked_amps.reshape(rows, col_count, k_local, row_count, a_local, c_local)
+        grouped = amps.reshape(rows, col_count, k_local, row_count, a_local, c_local)
         grouped = jnp.transpose(grouped, (0, 3, 1, 2, 4, 5)).reshape(
             rows, row_count * col_count, k_local, a_local, c_local
         )
@@ -80,7 +73,15 @@
         if step >= 2:
             grouped, results[step - 2] = lax.optimization_barrier((grouped, results[step - 2]))
         items = lax.all_to_all(grouped, ("row", "col"), split_axis=1, concat_axis=4, tiled=True)
-        blocks = jnp.transpose(items.reshape(rows, k_local, a_local, virt_count), (0, 2, 1, 3))
+        if step >= 1:
+            items, results[step - 1] = lax.optimization_barrier((items, results[step - 1]))
+        amp_sym = (
+            slab_irrep[step * rows:(step + 1) * rows, None, None, None]
+            ^ k_irrep[None, :, None, None]
+            ^ (a_irrep[None, None, :, None] ^ virt_irrep[None, None, None, :])
+        )
+        blocks = jnp.where(amp_sym == 0, items.reshape(rows, k_local, a_local, virt_count), 0.0)
+        blocks = jnp.transpose(blocks, (0, 2, 1, 3))
         blocks = blocks.reshape(rows, a_local, k_local * virt_count)
         partial_value = jnp.einsum(
             "iap,pq->iaq",
@@ -90,6 +91,7 @@
             preferred_element_type=jnp.float32,
         )
         flat = partial_value.reshape(rows, a_local, column_slab * virt_count)
+        flats.append(flat)
         results.append(lax.psum_scatter(flat, "col", scatter_dimension=2, tiled=True))
     return jnp.concatenate(results, axis=0)
 

time: 596 us -> 623 us (1.045)
  waiting for transfers between devices: 379 us -> 399 us
  local copies, waits for them, and re-layouts: 86 us -> 98.7 us
  other arithmetic: 38 us -> 31.4 us
    reduce_scatter x2, waiting for transfers between devices: 84.6 us -> 108 us  [per_device(): lax.psum_scatter(flat, 'col', scatter_dimension=2, tiled=True)]
    slice x0 -> x1, local copies, waits for them, and re-layouts: none -> 11.1 us  [per_device(): amps = amplitudes[step * rows:(step + 1) * rows]]
  transfers between devices with their start and end apart: 4 -> 4, of which waited for: 3 -> 4; matrix products, arithmetic and copies ran while one was open for 26% -> 21% of each run, Pallas kernels for 0% -> 0%
where the time goes in v12:
time: 623 us; the launch traced here: 621 us
  waiting for transfers between devices  399 us (64%)
  local copies, waits for them, and re-layouts  98.7 us (16%)
  matrix products  66.1 us (11%)
  other arithmetic  31.4 us (5%)
  between operations  13.5 us (2%)
  starting transfers between devices  11.7 us (2%)
    all_to_all x2, waiting for transfers between devices, per_device(): lax.all_to_all(grouped, ('row', 'col'), split_axis=1, concat_axis=4, tile...  292 us
    reduce_scatter x2, waiting for transfers between devices, per_device(): lax.psum_scatter(flat, 'col', scatter_dimension=2, tiled=True)  108 us
    dot_general x2, matrix products, per_device(): jnp.einsum('iap,pq->iaq', blocks, masked_ints, precision=lax.Precision.HI...  66.1 us
    reshape x1, local copies, waits for them, and re-layouts, per_device(): jnp.where(int_sym == 0, cycle_integrals, 0.0)  39.8 us
    select_n x1, other arithmetic, per_device(): jnp.where(int_sym == 0, cycle_integrals, 0.0)  23.1 us
    reshape x2, local copies, waits for them, and re-layouts, per_device(): amps.reshape(rows, col_count, k_local, row_count, a_local, c_local)  19.8 us
    reshape x2, local copies, waits for them, and re-layouts, per_device(): jnp.transpose(grouped, (0, 3, 1, 2, 4, 5))  15.7 us
  transfers between devices with their start and end apart: 4, of which 4 were waited for; matrix products, arithmetic and copies ran while one was open for 21% of the time, Pallas kernels for 0%

profile of v12, /device:TPU:0, one launch (start us, length us, event | category | flops | bytes accessed | tf_op | source)
XLA Modules:
  0.0 620.9 jit_solution(4741622214369009746)
XLA Ops:
  6.5 11.1 %fusion.1 = (f32[4,64,512,16]{2,3,1,0:T(8,128)}, f32[4,64,512,16]{2,3,1,0:T(8,128)}) fusion(f32[8,64,512,16]{2,3,1,0:T(8,128)} %param.4), kind=kLoop, calls=%fused_computation.12 | loop fusion | bytes 33554432 | tf_op jit(solution)/shard_map/slice | solution.py:66
  17.7 9.9 %reshape.185 = f32[4,8,8,4,128,16]{4,3,5,2,1,0:T(4,128)} reshape(f32[4,64,512,16]{2,3,1,0:T(8,128)} %get-tuple-element.9) | data formatting | bytes 16777216 | tf_op jit(solution)/shard_map/reshape | solution.py:67
  27.6 7.8 %copy.26 = f32[4,4,8,8,128,16]{4,5,3,0,2,1:T(8,128)} copy(f32[4,4,8,8,128,16]{4,1,5,3,2,0:T(4,128)} %bitcast.40) | data formatting | bytes 16777216 | tf_op jit(solution)/shard_map/reshape | solution.py:68
  35.4 7.4 %all-to-all-start.1 = ((f32[4,32,8,128,16]{3,4,2,0,1:T(8,128)}), f32[4,32,8,128,16]{3,4,2,0,1:T(8,128)}, u32[]{:S(2)}, u32[]{:S(2)}) async-start(f32[4,32,8,128,16]{3,4,2,0,1:T(8,128)} %bitcast.38), calls=%async_computation.1 | async-start | bytes 16777216 | tf_op jit(solution)/shard_map/all_to_all | solution.py:75
  42.8 9.9 %reshape.183 = f32[4,8,8,4,128,16]{4,3,5,2,1,0:T(4,128)} reshape(f32[4,64,512,16]{2,3,1,0:T(8,128)} %get-tuple-element.10) | data formatting | bytes 16777216 | tf_op jit(solution)/shard_map/reshape | solution.py:67
  52.7 7.9 %copy.25 = f32[4,4,8,8,128,16]{4,5,3,0,2,1:T(8,128)} copy(f32[4,4,8,8,128,16]{4,1,5,3,2,0:T(4,128)} %bitcast.41) | data formatting | bytes 16777216 | tf_op jit(solution)/shard_map/reshape | solution.py:68
  60.6 171.7 %all-to-all-done.1 = f32[4,32,8,128,16]{3,4,2,0,1:T(8,128)} async-done(((f32[4,32,8,128,16]{3,4,2,0,1:T(8,128)}), f32[4,32,8,128,16]{3,4,2,0,1:T(8,128)}, u32[]{:S(2)}, u32[]{:S(2)}) %all-to-all-start.1) | async-done | bytes 8388640 | tf_op jit(solution)/shard_map/all_to_all | solution.py:75
  232.4 3.8 all-to-all-start
  236.2 0.2 reduce-scatter.3.cloned.1.call-start
  236.4 0.1 dynamic_slice.6
  236.8 23.1 %fusion = f32[8,512,4,512]{3,2,1,0:T(4,128)} fusion(f32[8,512,4,512]{3,2,1,0:T(4,128)} %param.5, s32[4,512]{1,0:T(4,128)S(1)} %broadcast_xor_fusion.2, s32[8,512]{1,0:T(8,128)S(1)} %broadcast_xor_fusion.1), kind=kLoop, calls=%fused_computation.1 | loop fusion | flops 25165824 | bytes 67133440 | tf_op jit(solution)/shard_map/jit(_where)/select_n | solution.py:57
  259.9 39.8 %reshape.192 = f32[4096,2048,1]{1,0,2:T(8,128)} reshape(f32[8,512,4,512]{3,2,1,0:T(4,128)} %fusion) | data formatting | bytes 67108864 | tf_op jit(solution)/shard_map/reshape | solution.py:57
  299.7 0.1 broadcast_xor_fusion
  299.9 4.3 copy.20
  304.2 1.5 bitcast_select_fusion
  305.7 33.4 %fusion.3 = f32[4,128,2048]{2,1,0:T(8,128)} fusion(f32[4,128,4096]{1,2,0:T(8,128)S(1)} %bitcast.43, f32[4096,2048,1]{1,0,2:T(8,128)} %reshape.192), kind=kOutput, calls=%fused_computation.14 | convolution fusion | flops 25769803776 | bytes 46137344 | tf_op jit(solution)/shard_map/iap,pq->iaq/dot_general | solution.py:86
  339.2 0.3 reduce-scatter.5.cloned.1.call-start
  339.5 119.9 %all-to-all-done = f32[4,32,8,128,16]{3,4,2,0,1:T(8,128)} async-done(((f32[4,32,8,128,16]{3,4,2,0,1:T(8,128)}), f32[4,32,8,128,16]{3,4,2,0,1:T(8,128)}, u32[]{:S(2)}, u32[]{:S(2)}) %all-to-all-start) | async-done | bytes 8388640 | tf_op jit(solution)/shard_map/all_to_all | solution.py:75
  459.3 7.8 %copy.17 = f32[4,32,8,128,16]{3,4,1,2,0:T(8,128)} copy(f32[4,32,8,128,16]{3,4,2,0,1:T(8,128)} %all-to-all-done) | data formatting | bytes 16777216 | tf_op jit(solution)/shard_map/all_to_all | solution.py:75
  467.1 19.6 %reduce-scatter.3.cloned.1.call-done = f32[4,128,256]{2,1,0:T(8,128)} async-done(((f32[4,128,2048]{2,1,0:T(8,128)}), f32[4,128,256]{2,1,0:T(8,128)}) %reduce-scatter.3.cloned.1.call-update) | async-done | bytes 524304 | tf_op jit(solution)/shard_map/reduce_scatter | solution.py:95
  486.7 4.4 bitcast_select_fusion.1
  491.1 32.7 %fusion.4 = f32[4,128,2048]{2,1,0:T(8,128)} fusion(f32[4,128,4096]{1,2,0:T(8,128)S(1)} %bitcast.42, f32[4096,2048,1]{1,0,2:T(8,128)} %reshape.192), kind=kOutput, calls=%fused_computation.15 | convolution fusion | flops 25769803776 | bytes 46137344 | tf_op jit(solution)/shard_map/iap,pq->iaq/dot_general | solution.py:86
  523.8 88.2 %reduce-scatter.5.cloned.1.call-done = f32[4,128,256]{2,1,0:T(8,128)} async-done(((f32[4,128,2048]{2,1,0:T(8,128)}), f32[4,128,256]{2,1,0:T(8,128)}) %reduce-scatter.5.cloned.1.call-update) | async-done | bytes 524304 | tf_op jit(solution)/shard_map/reduce_scatter | solution.py:95
  612.0 2.1 pad_maximum_fusion
  (13 shorter events, 0.4 us)
Async XLA Ops:
  35.4 197.0 %all-to-all-start.1 = ((f32[4,32,8,128,16]{3,4,2,0,1:T(8,128)}), f32[4,32,8,128,16]{3,4,2,0,1:T(8,128)}, u32[]{:S(2)}, u32[]{:S(2)}) async-start(f32[4,32,8,128,16]{3,4,2,0,1:T(8,128)} %bitcast.38), calls=%async_computation.1 | async-start | bytes 16777216 | tf_op jit(solution)/shard_map/all_to_all | solution.py:75
  232.4 4.1 copy-start.2
  232.4 4.1 copy-start.1
  232.4 227.0 %all-to-all-start = ((f32[4,32,8,128,16]{3,4,2,0,1:T(8,128)}), f32[4,32,8,128,16]{3,4,2,0,1:T(8,128)}, u32[]{:S(2)}, u32[]{:S(2)}) async-start(f32[4,32,8,128,16]{3,4,2,0,1:T(8,128)} %bitcast.37), calls=%async_computation | async-start | bytes 16777216 | tf_op jit(solution)/shard_map/all_to_all | solution.py:75
  236.2 250.5 %reduce-scatter.3.cloned.1.call-start = ((), (), s32[]{:S(2)}) async-start(), calls=%async_computation.4 | async-start | bytes 4718592 | tf_op jit(solution)/shard_map/reduce_scatter | solution.py:95
  339.2 272.8 %reduce-scatter.5.cloned.1.call-start = ((), (), s32[]{:S(2)}) async-start(), calls=%async_computation.5 | async-start | bytes 4718592 | tf_op jit(solution)/shard_map/reduce_scatter | solution.py:95
  491.1 120.9 %copy-start = (f32[4,128,256]{2,1,0:T(8,128)S(1)}, f32[4,128,256]{2,1,0:T(8,128)}, u32[]{:S(2)}) copy-start(f32[4,128,256]{2,1,0:T(8,128)} %reduce-scatter.3.cloned.1.call-done) | copy-start | bytes 1572868
Sparse Core Ops, SparseCore 0:
  339.3 147.3 reduce-scatter.2
  523.9 88.0 reduce-scatter.4

commit v13 on v11

--- a/solution.py
+++ b/solution.py
@@ -60,8 +60,8 @@
         k_local * virt_count, column_slab * virt_count
     )
 
-    first = (slab_rows * 3 + 7) // 8
-    second = min(slab_rows, 2 * first)
+    first = (slab_rows * 2 + 7) // 8
+    second = min(slab_rows, first + (slab_rows - first + 1) // 2)
     bounds = [(lo, hi) for lo, hi in ((0, first), (first, second), (second, slab_rows)) if hi > lo]
     chunks = len(bounds)
     results = []

time: 615 us -> 600 us (0.976)
  waiting for transfers between devices: 342 us -> 327 us
    reduce_scatter x3, waiting for transfers between devices: 179 us -> 160 us  [per_device(): lax.psum_scatter(flat, 'col', scatter_dimension=2, tiled=True)]
  transfers between devices with their start and end apart: 6 -> 6, of which waited for: 5 -> 4; matrix products, arithmetic and copies ran while one was open for 35% -> 37% of each run, Pallas kernels for 0% -> 0%
where the time goes in v13:
time: 600 us; the launch traced here: 598 us
  waiting for transfers between devices  327 us (54%)
  local copies, waits for them, and re-layouts  130 us (22%)
  matrix products  72.7 us (12%)
  other arithmetic  39.8 us (7%)
  starting transfers between devices  15.2 us (3%)
  between operations  13.2 us (2%)
    all_to_all x3, waiting for transfers between devices, per_device(): lax.all_to_all(grouped, ('row', 'col'), split_axis=1, concat_axis=4, tile...  167 us
    reduce_scatter x3, waiting for transfers between devices, per_device(): lax.psum_scatter(flat, 'col', scatter_dimension=2, tiled=True)  160 us
    dot_general x3, matrix products, per_device(): jnp.einsum('iap,pq->iaq', blocks, masked_ints, precision=lax.Precision.HI...  72.7 us
    reshape x1, local copies, waits for them, and re-layouts, per_device(): jnp.where(int_sym == 0, cycle_integrals, 0.0)  39.8 us
    unnamed x9, local copies, waits for them, and re-layouts  30.2 us
    select_n x1, other arithmetic, per_device(): jnp.where(int_sym == 0, cycle_integrals, 0.0)  23.1 us
    reshape x3, local copies, waits for them, and re-layouts, per_device(): masked_amps.reshape(rows, col_count, k_local, row_count, a_local, c_local)  20.4 us
    all_to_all x3, starting transfers between devices, per_device(): lax.all_to_all(grouped, ('row', 'col'), split_axis=1, concat_axis=4, tile...  14.7 us
  transfers between devices with their start and end apart: 6, of which 4 were waited for; matrix products, arithmetic and copies ran while one was open for 37% of the time, Pallas kernels for 0%

profile of v13, /device:TPU:0, one launch (start us, length us, event | category | flops | bytes accessed | tf_op | source)
XLA Modules:
  0.0 597.7 jit_solution(16363538832454291029)
XLA Ops:
  8.8 4.7 slice_select_fusion.2
  13.5 5.3 reshape.232
  18.7 4.7 copy.32
  23.5 7.4 %all-to-all-start = ((f32[2,32,8,128,16]{3,4,2,0,1:T(8,128)}), f32[2,32,8,128,16]{3,4,2,0,1:T(8,128)}, u32[]{:S(2)}, u32[]{:S(2)}) async-start(f32[2,32,8,128,16]{3,4,2,0,1:T(8,128)} %bitcast.68), calls=%async_computation | async-start | bytes 8388608 | tf_op jit(solution)/shard_map/all_to_all | solution.py:85
  31.2 8.1 %slice_select_fusion = (f32[3,64,512,16]{2,3,1,0:T(8,128)}, f32[3,64,512,16]{2,3,1,0:T(8,128)}) fusion(f32[8,64,512,16]{2,3,1,0:T(8,128)} %param.4, s32[3,64]{1,0:T(4,128)S(1)} %get-tuple-element.15, s32[512,16]{0,1:T(8,128)S(1)} %broadcast_xor_fusion, s32[3,64]{1,0:T(4,128)S(1)} %get-tuple-element.16), kind=kLoop, calls=%fused_computation.6 | loop fusion | flops 9437184 | bytes 25200128 | tf_op jit(solution)/shard_map/jit(_where)/select_n | solution.py:76
  39.3 7.6 %reshape.237 = f32[3,8,8,4,128,16]{4,3,5,2,1,0:T(4,128)} reshape(f32[3,64,512,16]{2,3,1,0:T(8,128)} %get-tuple-element.13) | data formatting | bytes 12582912 | tf_op jit(solution)/shard_map/reshape | solution.py:77
  46.9 6.4 %copy.25 = f32[3,4,8,8,128,16]{4,5,3,2,1,0:T(8,128)} copy(f32[3,4,8,8,128,16]{4,1,5,3,2,0:T(4,128)} %bitcast.65) | data formatting | bytes 12582912 | tf_op jit(solution)/shard_map/transpose | solution.py:78
  53.4 23.1 %fusion.4 = f32[8,512,4,512]{3,2,1,0:T(4,128)} fusion(f32[8,512,4,512]{3,2,1,0:T(4,128)} %param.5, s32[4,512]{1,0:T(4,128)S(1)} %broadcast_xor_fusion.2, s32[8,512]{1,0:T(8,128)S(1)} %broadcast_xor_fusion.1), kind=kLoop, calls=%fused_computation.5 | loop fusion | flops 25165824 | bytes 67133440 | tf_op jit(solution)/shard_map/jit(_where)/select_n | solution.py:59
  76.5 30.1 %copy.36 = f32[512,8,4,512]{3,1,2,0:T(8,128)} copy(f32[512,8,4,512]{3,2,1,0:T(4,128)} %bitcast.60) | data formatting | bytes 67108864
  110.0 16.9 %all-to-all-done = f32[2,32,8,128,16]{3,4,2,0,1:T(8,128)} async-done(((f32[2,32,8,128,16]{3,4,2,0,1:T(8,128)}), f32[2,32,8,128,16]{3,4,2,0,1:T(8,128)}, u32[]{:S(2)}, u32[]{:S(2)}) %all-to-all-start) | async-done | bytes 4194336 | tf_op jit(solution)/shard_map/all_to_all | solution.py:85
  126.9 3.6 all-to-all-start.1
  130.7 39.8 %reshape.243 = f32[4096,2048,1]{1,0,2:T(8,128)} reshape(f32[8,512,4,512]{3,2,1,0:T(4,128)} %fusion.4) | data formatting | bytes 67108864 | tf_op jit(solution)/shard_map/reshape | solution.py:59
  170.6 4.7 copy.23
  175.3 19.4 %fusion.6 = f32[2,128,2048]{2,1,0:T(8,128)} fusion(f32[2,128,4096]{1,2,0:T(8,128)} %bitcast.67, f32[4096,2048,1]{1,0,2:T(8,128)} %reshape.243), kind=kOutput, calls=%fused_computation.20 | convolution fusion | flops 12884901888 | bytes 39845888 | tf_op jit(solution)/shard_map/iap,pq->iaq/dot_general | solution.py:88
  194.7 7.5 %reshape.230 = f32[3,8,8,4,128,16]{4,3,5,2,1,0:T(4,128)} reshape(f32[3,64,512,16]{2,3,1,0:T(8,128)} %get-tuple-element.14) | data formatting | bytes 12582912 | tf_op jit(solution)/shard_map/reshape | solution.py:77
  202.3 6.4 %copy.20 = f32[3,4,8,8,128,16]{4,5,3,2,1,0:T(8,128)} copy(f32[3,4,8,8,128,16]{4,1,5,3,2,0:T(4,128)} %bitcast.66) | data formatting | bytes 12582912 | tf_op jit(solution)/shard_map/transpose | solution.py:78
  208.7 88.3 %reduce-scatter.4.cloned.1.call-done = f32[2,128,256]{2,1,0:T(8,128)} async-done(((f32[2,128,2048]{2,1,0:T(8,128)}), f32[2,128,256]{2,1,0:T(8,128)}) %reduce-scatter.4.cloned.1.call-update) | async-done | bytes 262160 | tf_op jit(solution)/shard_map/reduce_scatter | solution.py:96
  296.9 6.2 %copy.29 = f32[3,32,8,128,16]{3,4,2,0,1:T(8,128)} copy(f32[3,32,8,128,16]{3,4,2,1,0:T(8,128)} %bitcast.64) | data formatting | bytes 12582912 | tf_op jit(solution)/shard_map/optimization_barrier | solution.py:84
  303.1 3.6 all-to-all-start.2
  307.0 3.4 copy.27
  310.5 26.6 %fusion.2 = f32[3,128,2048]{2,1,0:T(8,128)} fusion(f32[3,128,4096]{1,2,0:T(8,128)S(1)} %bitcast.71, f32[4096,2048]{1,0:T(8,128)} %bitcast.61), kind=kOutput, calls=%fused_computation.2 | convolution fusion | flops 19327352832 | bytes 42991616 | tf_op jit(solution)/shard_map/iap,pq->iaq/dot_general | solution.py:88
  337.2 149.9 %all-to-all-done.2 = f32[3,32,8,128,16]{3,4,2,0,1:T(8,128)} async-done(((f32[3,32,8,128,16]{3,4,2,0,1:T(8,128)}), f32[3,32,8,128,16]{3,4,2,0,1:T(8,128)}, u32[]{:S(2)}, u32[]{:S(2)}) %all-to-all-start.2) | async-done | bytes 6291488 | tf_op jit(solution)/shard_map/all_to_all | solution.py:85
  490.6 26.7 %fusion = f32[3,128,2048]{2,1,0:T(8,128)} fusion(f32[3,128,4096]{1,2,0:T(8,128)S(1)} %bitcast.70, f32[4096,2048]{1,0:T(8,128)} %bitcast.62), kind=kOutput, calls=%fused_computation | convolution fusion | flops 19327352832 | bytes 42991616 | tf_op jit(solution)/shard_map/iap,pq->iaq/dot_general | solution.py:88
  517.3 71.7 %reduce-scatter.8.cloned.1.call-done = f32[3,128,256]{2,1,0:T(8,128)} async-done(((f32[3,128,2048]{2,1,0:T(8,128)}), f32[3,128,256]{2,1,0:T(8,128)}) %reduce-scatter.8.cloned.1.call-update) | async-done | bytes 393232 | tf_op jit(solution)/shard_map/reduce_scatter | solution.py:96
  (27 shorter events, 12.2 us)
Async XLA Ops:
  23.5 7.4 %copy-start.3 = (s32[64]{0:T(128)S(1)}, s32[64]{0:T(128)}, u32[]{:S(2)}) copy-start(s32[64]{0:T(128)} %param.6) | copy-start | bytes 772
  23.5 103.4 %all-to-all-start = ((f32[2,32,8,128,16]{3,4,2,0,1:T(8,128)}), f32[2,32,8,128,16]{3,4,2,0,1:T(8,128)}, u32[]{:S(2)}, u32[]{:S(2)}) async-start(f32[2,32,8,128,16]{3,4,2,0,1:T(8,128)} %bitcast.68), calls=%async_computation | async-start | bytes 8388608 | tf_op jit(solution)/shard_map/all_to_all | solution.py:85
  46.9 6.4 %copy-start.2 = (s32[512]{0:T(512)S(1)}, s32[512]{0:T(512)}, u32[]{:S(2)}) copy-start(s32[512]{0:T(512)} %param.7) | copy-start | bytes 6148
  76.5 30.1 %copy-start = (f32[3,4,8,8,128,16]{4,5,3,2,1,0:T(8,128)S(1)}, f32[3,4,8,8,128,16]{4,5,3,2,1,0:T(8,128)}, u32[]{:S(2)}) copy-start(f32[3,4,8,8,128,16]{4,5,3,2,1,0:T(8,128)} %copy.25) | copy-start | bytes 18874372
  126.9 176.2 %all-to-all-start.1 = ((f32[3,32,8,128,16]{3,4,2,0,1:T(8,128)}), f32[3,32,8,128,16]{3,4,2,0,1:T(8,128)}, u32[]{:S(2)}, u32[]{:S(2)}) async-start(f32[3,32,8,128,16]{3,4,2,0,1:T(8,128)} %copy.26), calls=%async_computation.2 | async-start | bytes 12582912 | tf_op jit(solution)/shard_map/all_to_all | solution.py:85
  130.5 166.4 %reduce-scatter.4.cloned.1.call-start = ((), (), s32[]{:S(2)}) async-start(), calls=%async_computation.6 | async-start | bytes 2359296 | tf_op jit(solution)/shard_map/reduce_scatter | solution.py:96
  303.1 184.0 %all-to-all-start.2 = ((f32[3,32,8,128,16]{3,4,2,0,1:T(8,128)}), f32[3,32,8,128,16]{3,4,2,0,1:T(8,128)}, u32[]{:S(2)}, u32[]{:S(2)}) async-start(f32[3,32,8,128,16]{3,4,2,0,1:T(8,128)} %copy.29), calls=%async_computation.4 | async-start | bytes 12582912 | tf_op jit(solution)/shard_map/all_to_all | solution.py:85
  306.8 210.5 %reduce-scatter.6.cloned.1.call-start = ((), (), s32[]{:S(2)}) async-start(), calls=%async_computation.7 | async-start | bytes 3538944 | tf_op jit(solution)/shard_map/reduce_scatter | solution.py:96
  337.1 251.8 %reduce-scatter.8.cloned.1.call-start = ((), (), s32[]{:S(2)}) async-start(), calls=%async_computation.8 | async-start | bytes 3538944 | tf_op jit(solution)/shard_map/reduce_scatter | solution.py:96
  490.5 98.4 %copy-start.1 = (f32[2,128,256]{2,1,0:T(8,128)S(1)}, f32[2,128,256]{2,1,0:T(8,128)}, u32[]{:S(2)}) copy-start(f32[2,128,256]{2,1,0:T(8,128)} %reduce-scatter.4.cloned.1.call-done) | copy-start | bytes 786436
Sparse Core Ops, SparseCore 0:
  194.8 102.0 reduce-scatter.3
  337.3 140.5 reduce-scatter.5
  517.4 71.5 reduce-scatter.7

commit v14 on v13

--- a/solution.py
+++ b/solution.py
@@ -61,7 +61,7 @@
     )
 
     first = (slab_rows * 2 + 7) // 8
-    second = min(slab_rows, first + (slab_rows - first + 1) // 2)
+    second = min(slab_rows, 2 * first)
     bounds = [(lo, hi) for lo, hi in ((0, first), (first, second), (second, slab_rows)) if hi > lo]
     chunks = len(bounds)
     results = []

time: 600 us -> 634 us (1.057)
  waiting for transfers between devices: 327 us -> 360 us
    all_to_all x3, waiting for transfers between devices: 167 us -> 219 us  [per_device(): lax.all_to_all(grouped, ('row', 'col'), split_axis=1, concat_axis=4, tile...]
    reduce_scatter x3, waiting for transfers between devices: 160 us -> 140 us  [per_device(): lax.psum_scatter(flat, 'col', scatter_dimension=2, tiled=True)]
  transfers between devices with their start and end apart: 6 -> 6, of which waited for: 4 -> 4; matrix products, arithmetic and copies ran while one was open for 37% -> 35% of each run, Pallas kernels for 0% -> 0%
where the time goes in v14:
time: 634 us; the launch traced here: 632 us
  waiting for transfers between devices  360 us (57%)
  local copies, waits for them, and re-layouts  133 us (21%)
  matrix products  71.5 us (11%)
  other arithmetic  38.8 us (6%)
  starting transfers between devices  15.2 us (2%)
  between operations  13.2 us (2%)
    all_to_all x3, waiting for transfers between devices, per_device(): lax.all_to_all(grouped, ('row', 'col'), split_axis=1, concat_axis=4, tile...  219 us
    reduce_scatter x3, waiting for transfers between devices, per_device(): lax.psum_scatter(flat, 'col', scatter_dimension=2, tiled=True)  140 us
    dot_general x3, matrix products, per_device(): jnp.einsum('iap,pq->iaq', blocks, masked_ints, precision=lax.Precision.HI...  71.5 us
    reshape x1, local copies, waits for them, and re-layouts, per_device(): jnp.where(int_sym == 0, cycle_integrals, 0.0)  39.8 us
    unnamed x9, local copies, waits for them, and re-layouts  30.1 us
    select_n x1, other arithmetic, per_device(): jnp.where(int_sym == 0, cycle_integrals, 0.0)  23.1 us
    reshape x3, local copies, waits for them, and re-layouts, per_device(): masked_amps.reshape(rows, col_count, k_local, row_count, a_local, c_local)  20.5 us
    all_to_all x3, starting transfers between devices, per_device(): lax.all_to_all(grouped, ('row', 'col'), split_axis=1, concat_axis=4, tile...  14.7 us
  transfers between devices with their start and end apart: 6, of which 4 were waited for; matrix products, arithmetic and copies ran while one was open for 35% of the time, Pallas kernels for 0%

profile of v14, /device:TPU:0, one launch (start us, length us, event | category | flops | bytes accessed | tf_op | source)
XLA Modules:
  0.0 631.8 jit_solution(2939150795567751831)
XLA Ops:
  9.6 6.0 slice_select_fusion.1
  15.6 5.3 reshape.232
  20.8 4.8 copy.32
  25.6 7.4 %all-to-all-start = ((f32[2,32,8,128,16]{3,4,2,0,1:T(8,128)}), f32[2,32,8,128,16]{3,4,2,0,1:T(8,128)}, u32[]{:S(2)}, u32[]{:S(2)}) async-start(f32[2,32,8,128,16]{3,4,2,0,1:T(8,128)} %bitcast.65), calls=%async_computation | async-start | bytes 8388608 | tf_op jit(solution)/shard_map/all_to_all | solution.py:85
  33.1 5.3 reshape.237
  38.4 4.7 copy.25
  43.4 23.1 %fusion.4 = f32[8,512,4,512]{3,2,1,0:T(4,128)} fusion(f32[8,512,4,512]{3,2,1,0:T(4,128)} %param.5, s32[4,512]{1,0:T(4,128)S(1)} %broadcast_xor_fusion.2, s32[8,512]{1,0:T(8,128)S(1)} %broadcast_xor_fusion.1), kind=kLoop, calls=%fused_computation.5 | loop fusion | flops 25165824 | bytes 67133440 | tf_op jit(solution)/shard_map/jit(_where)/select_n | solution.py:59
  66.5 30.1 %copy.36 = f32[512,8,4,512]{3,1,2,0:T(8,128)} copy(f32[512,8,4,512]{3,2,1,0:T(4,128)} %bitcast.58) | data formatting | bytes 67108864
  99.0 30.1 %all-to-all-done = f32[2,32,8,128,16]{3,4,2,0,1:T(8,128)} async-done(((f32[2,32,8,128,16]{3,4,2,0,1:T(8,128)}), f32[2,32,8,128,16]{3,4,2,0,1:T(8,128)}, u32[]{:S(2)}, u32[]{:S(2)}) %all-to-all-start) | async-done | bytes 4194336 | tf_op jit(solution)/shard_map/all_to_all | solution.py:85
  132.8 39.8 %reshape.243 = f32[4096,2048,1]{1,0,2:T(8,128)} reshape(f32[8,512,4,512]{3,2,1,0:T(4,128)} %fusion.4) | data formatting | bytes 67108864 | tf_op jit(solution)/shard_map/reshape | solution.py:59
  172.6 4.7 copy.23
  177.3 19.4 %fusion.7 = f32[2,128,2048]{2,1,0:T(8,128)} fusion(f32[2,128,4096]{1,2,0:T(8,128)} %bitcast.63, f32[4096,2048,1]{1,0,2:T(8,128)} %reshape.243), kind=kOutput, calls=%fused_computation.21 | convolution fusion | flops 12884901888 | bytes 39845888 | tf_op jit(solution)/shard_map/iap,pq->iaq/dot_general | solution.py:88
  196.9 5.9 slice_select_fusion
  202.8 10.0 %reshape.230 = f32[4,8,8,4,128,16]{4,3,5,2,1,0:T(4,128)} reshape(f32[4,64,512,16]{2,3,1,0:T(8,128)} %slice_select_fusion) | data formatting | bytes 16777216 | tf_op jit(solution)/shard_map/reshape | solution.py:77
  212.7 7.8 %copy.20 = f32[4,4,8,8,128,16]{4,5,3,2,1,0:T(8,128)} copy(f32[4,4,8,8,128,16]{4,1,5,3,2,0:T(4,128)} %bitcast.62) | data formatting | bytes 16777216 | tf_op jit(solution)/shard_map/transpose | solution.py:78
  220.5 54.6 %reduce-scatter.4.cloned.1.call-done = f32[2,128,256]{2,1,0:T(8,128)} async-done(((f32[2,128,2048]{2,1,0:T(8,128)}), f32[2,128,256]{2,1,0:T(8,128)}) %reduce-scatter.4.cloned.1.call-update) | async-done | bytes 262160 | tf_op jit(solution)/shard_map/reduce_scatter | solution.py:96
  275.2 7.7 %copy.29 = f32[4,32,8,128,16]{3,4,2,0,1:T(8,128)} copy(f32[4,32,8,128,16]{3,4,2,1,0:T(8,128)} %bitcast.61) | data formatting | bytes 16777216 | tf_op jit(solution)/shard_map/optimization_barrier | solution.py:84
  282.9 3.7 all-to-all-start.2
  286.6 4.7 copy.27
  291.4 19.4 %fusion.2 = f32[2,128,2048]{2,1,0:T(8,128)} fusion(f32[2,128,4096]{1,2,0:T(8,128)} %bitcast.64, f32[4096,2048]{1,0:T(8,128)} %bitcast.59), kind=kOutput, calls=%fused_computation.2 | convolution fusion | flops 12884901888 | bytes 39845888 | tf_op jit(solution)/shard_map/iap,pq->iaq/dot_general | solution.py:88
  311.1 189.4 %all-to-all-done.2 = f32[4,32,8,128,16]{3,4,2,0,1:T(8,128)} async-done(((f32[4,32,8,128,16]{3,4,2,0,1:T(8,128)}), f32[4,32,8,128,16]{3,4,2,0,1:T(8,128)}, u32[]{:S(2)}, u32[]{:S(2)}) %all-to-all-start.2) | async-done | bytes 8388640 | tf_op jit(solution)/shard_map/all_to_all | solution.py:85
  500.5 4.5 copy.30
  505.0 32.6 %fusion = f32[4,128,2048]{2,1,0:T(8,128)} fusion(f32[4,128,4096]{1,2,0:T(8,128)S(1)} %bitcast.69, f32[4096,2048]{1,0:T(8,128)} %bitcast.60), kind=kOutput, calls=%fused_computation | convolution fusion | flops 25769803776 | bytes 46137344 | tf_op jit(solution)/shard_map/iap,pq->iaq/dot_general | solution.py:88
  537.7 85.4 %reduce-scatter.8.cloned.1.call-done = f32[4,128,256]{2,1,0:T(8,128)} async-done(((f32[4,128,2048]{2,1,0:T(8,128)}), f32[4,128,256]{2,1,0:T(8,128)}) %reduce-scatter.8.cloned.1.call-update) | async-done | bytes 524304 | tf_op jit(solution)/shard_map/reduce_scatter | solution.py:96
  (28 shorter events, 12.1 us)
Async XLA Ops:
  20.8 12.2 %copy-start.3 = (s32[64]{0:T(128)S(1)}, s32[64]{0:T(128)}, u32[]{:S(2)}) copy-start(s32[64]{0:T(128)} %param.6) | copy-start | bytes 772
  25.6 103.4 %all-to-all-start = ((f32[2,32,8,128,16]{3,4,2,0,1:T(8,128)}), f32[2,32,8,128,16]{3,4,2,0,1:T(8,128)}, u32[]{:S(2)}, u32[]{:S(2)}) async-start(f32[2,32,8,128,16]{3,4,2,0,1:T(8,128)} %bitcast.65), calls=%async_computation | async-start | bytes 8388608 | tf_op jit(solution)/shard_map/all_to_all | solution.py:85
  33.1 10.1 %copy-start.2 = (s32[512]{0:T(512)S(1)}, s32[512]{0:T(512)}, u32[]{:S(2)}) copy-start(s32[512]{0:T(512)} %param.7) | copy-start | bytes 6148
  66.5 30.1 %copy-start = (f32[2,4,8,8,128,16]{4,5,3,2,1,0:T(8,128)S(1)}, f32[2,4,8,8,128,16]{4,5,3,2,1,0:T(8,128)}, u32[]{:S(2)}) copy-start(f32[2,4,8,8,128,16]{4,5,3,2,1,0:T(8,128)} %copy.25) | copy-start | bytes 12582916
  129.0 153.9 %all-to-all-start.1 = ((f32[2,32,8,128,16]{3,4,2,0,1:T(8,128)}), f32[2,32,8,128,16]{3,4,2,0,1:T(8,128)}, u32[]{:S(2)}, u32[]{:S(2)}) async-start(f32[2,32,8,128,16]{3,4,2,0,1:T(8,128)} %copy.26), calls=%async_computation.2 | async-start | bytes 8388608 | tf_op jit(solution)/shard_map/all_to_all | solution.py:85
  132.6 142.6 %reduce-scatter.4.cloned.1.call-start = ((), (), s32[]{:S(2)}) async-start(), calls=%async_computation.6 | async-start | bytes 2359296 | tf_op jit(solution)/shard_map/reduce_scatter | solution.py:96
  282.9 217.6 %all-to-all-start.2 = ((f32[4,32,8,128,16]{3,4,2,0,1:T(8,128)}), f32[4,32,8,128,16]{3,4,2,0,1:T(8,128)}, u32[]{:S(2)}, u32[]{:S(2)}) async-start(f32[4,32,8,128,16]{3,4,2,0,1:T(8,128)} %copy.29), calls=%async_computation.4 | async-start | bytes 16777216 | tf_op jit(solution)/shard_map/all_to_all | solution.py:85
  286.6 251.1 %reduce-scatter.6.cloned.1.call-start = ((), (), s32[]{:S(2)}) async-start(), calls=%async_computation.7 | async-start | bytes 2359296 | tf_op jit(solution)/shard_map/reduce_scatter | solution.py:96
  310.8 312.3 %reduce-scatter.8.cloned.1.call-start = ((), (), s32[]{:S(2)}) async-start(), calls=%async_computation.8 | async-start | bytes 4718592 | tf_op jit(solution)/shard_map/reduce_scatter | solution.py:96
  505.0 118.1 %copy-start.1 = (f32[2,128,256]{2,1,0:T(8,128)S(1)}, f32[2,128,256]{2,1,0:T(8,128)}, u32[]{:S(2)}) copy-start(f32[2,128,256]{2,1,0:T(8,128)} %reduce-scatter.4.cloned.1.call-done) | copy-start | bytes 786436
Sparse Core Ops, SparseCore 0:
  196.9 78.2 reduce-scatter.3
  310.9 150.8 reduce-scatter.5
  537.8 85.2 reduce-scatter.7
